TPU v7x, 32 devices: a whole 2x2x4 slice. The times are simulated.
32 devices in a mesh: stream: 2 (over y), dev: 16 (over z, x, core).
Axes of the slice: x: 2, y: 2, z: 4, core: 2. Of those that a mesh axis runs over, the one named last changes fastest.
Arguments:
- latents: bfloat16 [32, 2, 3, 16, 1664], P(('stream', 'dev')), parts along dimension 0, may hold values from -6 to 6
- owners: int32 [4], P('stream'), parts along dimension 0, may hold values from 0 to 15
- conv_in: bfloat16 [432, 384], replicated, may hold values from -0.3125 to 0.3125
- conv_mid: bfloat16 [10368, 384], replicated, may hold values from -0.0625 to 0.0625
- to_pixels: bfloat16 [384, 12], replicated, may hold values from -0.3125 to 0.3125
Outputs:
- pixels: bfloat16 [4, 3, 32, 624], P('stream', None, 'dev'), parts along dimension 0
There are 2 independent parts, one for each index of `stream`. A program takes and returns all parts, laid end to end along the dimension named above; an argument that names none is the same for every part. Nothing has to cross between parts.
Inputs may be any that keep to these rules, and one draw needn't show every extreme that they name: `owners`: each entry is the index of a device on dev.
All inputs are finite; a program needn't handle non-finite values.
Results may differ from a plain program's by a relative error of at most 0.0052.
Values may be sent and summed in bfloat16 or wider, within the bound.
No kernel may reach another device: no remote copies, remote signals or barrier semaphores. Data moves between devices by JAX's collectives and lax.ppermute only.
A program may use at most 128 MiB of HBM per device.

v0:
```python
import jax
import jax.numpy as jnp
from jax import lax
from jax.sharding import PartitionSpec as P

ZC = 16
GROUPS = 2
FRAMES = 3


epsilon = 1e-06


def spread(value, axis, source):
    kept = jnp.where(lax.axis_index(axis) == source, value, 0).astype(value.dtype)
    return lax.psum(kept, axis)


def with_halo(block, sides, width):
    for axis, dim in sides:
        count = lax.axis_size(axis)
        forward = [(i, i + 1) for i in range(count - 1)]
        backward = [(target, source) for source, target in forward]
        low = lax.ppermute(
            lax.slice_in_dim(block, block.shape[dim] - width, None, axis=dim), axis, forward
        )
        high = lax.ppermute(lax.slice_in_dim(block, 0, width, axis=dim), axis, backward)
        block = jnp.concatenate([low, block, high], axis=dim)
    return block


def local_conv(source, weights):
    steps_t = source.shape[0] - 2
    rows_out = source.shape[1] - 2
    columns = source.shape[2]
    channels = source.shape[3]
    padded = jnp.pad(source, ((0, 0), (0, 0), (1, 1), (0, 0)))
    result = jnp.zeros((steps_t * rows_out * columns, weights.shape[1]), jnp.float32)
    for step_t in range(3):
        pieces = []
        for step_r in range(3):
            for step_w in range(3):
                pieces.append(
                    padded[
                        step_t : step_t + steps_t,
                        step_r : step_r + rows_out,
                        step_w : step_w + columns,
                    ]
                )
        stacked = jnp.concatenate(pieces, axis=-1)
        block = weights[step_t * 9 * channels : (step_t + 1) * 9 * channels]
        result = result + jnp.dot(
            stacked.reshape(-1, stacked.shape[-1]), block, preferred_element_type=jnp.float32
        )
    return result.reshape(steps_t, rows_out, columns, weights.shape[1])


def rms_scale(values):
    return values * lax.rsqrt(jnp.mean(values * values, axis=-1, keepdims=True) + epsilon)


def local(latents, owners, conv_in, conv_mid, to_pixels):
    n_devices = lax.axis_size("dev")
    position = lax.axis_index("dev")
    height = latents.shape[3]
    rows_dev = height // n_devices
    columns = latents.shape[4] // ZC
    channels = conv_mid.shape[1]
    first_row = position * rows_dev
    extend = 0
    span_rows = rows_dev + 2 * extend
    latent_cache = jnp.zeros((2, height + 4, columns, ZC), jnp.bfloat16)
    middle_cache = jnp.zeros((2, rows_dev + 2, columns, channels), jnp.bfloat16)
    results = []
    for group in range(GROUPS):
        group_latent = spread(latents[0, group], "dev", owners[group])
        frames = group_latent.reshape(FRAMES, height, columns, ZC)
        frames = jnp.pad(frames, ((0, 0), (2, 2), (0, 0), (0, 0)))
        history = jnp.concatenate([latent_cache, frames], axis=0)
        latent_cache = history[-2:]
        window = lax.dynamic_slice_in_dim(history, first_row + 1 - extend, span_rows + 2, 1)
        first_act = local_conv(window, conv_in)
        activated = jax.nn.silu(rms_scale(first_act)).astype(jnp.bfloat16)
        extended = with_halo(activated, (("dev", 1),), 1)
        middle_history = jnp.concatenate([middle_cache, extended], axis=0)
        middle_cache = middle_history[-2:]
        second_act = local_conv(middle_history, conv_mid)
        normed = rms_scale(first_act + second_act).astype(jnp.bfloat16)
        projected = jnp.dot(
            normed.reshape(-1, channels), to_pixels, preferred_element_type=jnp.float32
        )
        projected = projected.reshape(FRAMES, rows_dev, columns, 2, 2, 3).transpose(
            0, 1, 3, 2, 4, 5
        )
        results.append(projected.reshape(FRAMES, 2 * rows_dev, 6 * columns).astype(jnp.bfloat16))
    return jnp.stack(results, axis=0)


def solution(mesh):
    in_specs = (P(("stream", "dev"), None, None, None, None), P("stream"), P(), P(), P())
    out_specs = P("stream", None, "dev", None)
    return jax.shard_map(local, mesh=mesh, in_specs=in_specs, out_specs=out_specs, check_vma=False)
```

profile of v0, /device:TPU:24, one launch (start us, length us, event | category | flops | bytes accessed | tf_op | source)
XLA Modules:
  0.0 171.8 jit_solution(17543781535209339910)
XLA Ops:
  6.5 1.3 fusion.50
  9.2 1.0 slice_select_fusion
  10.2 2.0 %reshape.290 = bf16[3,16,104,16]{3,2,1,0:T(8,128)(2,1)} reshape(bf16[1,1,3,16,1664]{4,3,2,1,0:T(8,128)(2,1)S(1)} %get-tuple-element.59) | data formatting | bytes 319488 | tf_op jit(solution)/shard_map/reshape | solution.py:77
  12.2 2.0 %reshape.298 = bf16[3,16,104,16]{3,2,1,0:T(8,128)(2,1)} reshape(bf16[1,1,3,16,1664]{4,3,2,1,0:T(8,128)(2,1)S(1)} %get-tuple-element.58) | data formatting | bytes 319488 | tf_op jit(solution)/shard_map/reshape | solution.py:77
  14.2 100.2 %all-reduce.11.cloned.1.call-done = (bf16[3,16,104,16]{3,2,1,0:T(8,128)(2,1)}, bf16[3,16,104,16]{3,2,1,0:T(8,128)(2,1)}) async-done(((bf16[3,16,104,16]{3,2,1,0:T(8,128)(2,1)}, bf16[3,16,104,16]{3,2,1,0:T(8,128)(2,1)}), (bf16[3,16,104,16]{3,2,1,0:T(8,128)(2,1)}, bf16[3,16,104,16]{3,2,1,0:T(8,128)(2,1)})) %all-reduce.11.cloned.1.call-update) | async-done | bytes 319504 | tf_op jit(solution)/shard_map/psum | solution.py:16
  114.4 1.6 pad.23
  118.9 1.9 %collective-permute-start = (bf16[3,1,104,384]{3,2,0,1:T(8,128)(2,1)S(1)}, bf16[3,1,104,384]{3,2,0,1:T(8,128)(2,1)}, u32[]{:S(2)}, u32[]{:S(2)}) collective-permute-start(bf16[3,1,104,384]{3,2,0,1:T(8,128)(2,1)S(1)} %multiply_convert_fusion.5), channel_id=1, source_target_pairs={{0,1},{1,2},{2,3},{3,4},{4,5},{5,6},{6,7},{7,8},{8,9},{9,10},{10,1... | collective-permute-start | bytes 718856 | tf_op jit(solution)/shard_map/ppermute | solution.py:24
  120.9 4.5 %collective-permute-start.1 = (bf16[3,1,104,384]{3,2,0,1:T(8,128)(2,1)S(1)}, bf16[3,1,104,384]{3,2,0,1:T(8,128)(2,1)}, u32[]{:S(2)}, u32[]{:S(2)}) collective-permute-start(bf16[3,1,104,384]{3,2,0,1:T(8,128)(2,1)S(1)} %multiply_convert_fusion.5), channel_id=1, source_target_pairs={{1,0},{2,1},{3,2},{4,3},{5,4},{6,5},{7,6},{8,7},{9,8},{10,9},{11,1... | collective-permute-start | bytes 718856 | tf_op jit(solution)/shard_map/ppermute | solution.py:27
  126.0 1.7 copy.21
  130.9 1.9 %collective-permute-start.2 = (bf16[3,1,104,384]{3,2,0,1:T(8,128)(2,1)S(1)}, bf16[3,1,104,384]{3,2,0,1:T(8,128)(2,1)S(1)}, u32[]{:S(2)}, u32[]{:S(2)}) collective-permute-start(bf16[3,1,104,384]{3,2,0,1:T(8,128)(2,1)S(1)} %multiply_convert_fusion.2), channel_id=1, source_target_pairs={{0,1},{1,2},{2,3},{3,4},{4,5},{5,6},{6,7},{7,8},{8,9},{9,10},{10,1... | collective-permute-start | bytes 718856 | tf_op jit(solution)/shard_map/ppermute | solution.py:24
  132.8 4.7 %collective-permute-start.3 = (bf16[3,1,104,384]{3,2,0,1:T(8,128)(2,1)S(1)}, bf16[3,1,104,384]{3,2,0,1:T(8,128)(2,1)S(1)}, u32[]{:S(2)}, u32[]{:S(2)}) collective-permute-start(bf16[3,1,104,384]{3,2,0,1:T(8,128)(2,1)S(1)} %multiply_convert_fusion.2), channel_id=1, source_target_pairs={{1,0},{2,1},{3,2},{4,3},{5,4},{6,5},{7,6},{8,7},{9,8},{10,9},{11,1... | collective-permute-start | bytes 718856 | tf_op jit(solution)/shard_map/ppermute | solution.py:27
  137.6 1.2 pad_maximum_fusion
  140.2 1.0 constant_dynamic-update-slice_fusion.6
  142.0 0.4 pad_slice_fusion.25
  143.2 1.1 copy-done.5
  144.4 1.8 %constant_dynamic-update-slice_fusion.1 = bf16[312,3456]{1,0:T(8,128)(2,1)S(1)} fusion(bf16[312,3456]{1,0:T(8,128)(2,1)S(1)} %constant_dynamic-update-slice_fusion.2, bf16[312,384]{1,0:T(8,128)(2,1)} %bitcast.13), kind=kLoop, calls=%fused_computation.95 | loop fusion | bytes 479232
  146.7 1.3 fusion.6
  148.1 1.4 fusion.12
  149.5 1.5 multiply_reduce_fusion.2
  152.3 1.2 copy-done.4
  153.5 3.2 %fusion.4 = f32[312,384]{1,0:T(8,128)S(1)} fusion(bf16[312,3456]{1,0:T(8,128)(2,1)S(1)} %bitcast.98, bf16[10368,384]{1,0:T(8,128)(2,1)} %param.8), kind=kOutput, calls=%fused_computation.14 | convolution fusion | flops 828112896 | bytes 5289984 | tf_op jit(solution)/shard_map/dot_general | solution.py:52
  157.0 3.1 %fusion.15 = f32[312,384]{1,0:T(8,128)S(1)} fusion(f32[312,384]{1,0:T(8,128)S(1)} %fusion.4, bf16[312,3456]{1,0:T(8,128)(2,1)S(1)} %bitcast.100, bf16[10368,384]{1,0:T(8,128)(2,1)} %param.8), kind=kOutput, calls=%fused_computation.28 | convolution fusion | flops 828232704 | bytes 5769216 | tf_op jit(solution)/shard_map/dot_general | solution.py:52
  160.1 3.2 %multiply_reduce_fusion = (f32[312]{0:T(512)S(1)}, f32[312,384]{1,0:T(8,128)S(1)}) fusion(f32[312,384]{1,0:T(8,128)S(1)} %get-tuple-element.72, f32[312,384]{1,0:T(8,128)S(1)} %fusion.15, bf16[312,3456]{1,0:T(8,128)(2,1)S(1)} %constant_dynamic-update-slice_fusion.35, bf16[10368,384]{1,0:T(8,128)(2,1)} %param.8), kind=kOutput, calls=%fused_computation.45 | convolution fusion | flops 828591808 | bytes 6249696 | tf_op jit(solution)/shard_map/dot_general | solution.py:52
  164.3 0.6 pad_maximum_fusion.1
  (134 shorter events, 12.4 us)
Async XLA Ops:
  6.5 107.9 %all-reduce.11.cloned.1.call-start = ((), (), s32[]{:S(2)}) async-start(), calls=%async_computation | async-start | bytes 5111808 | tf_op jit(solution)/shard_map/psum | solution.py:16
  12.2 2.0 %copy-start.7 = (bf16[384,12]{0,1:T(8,128)(2,1)S(1)}, bf16[384,12]{0,1:T(8,128)(2,1)}, u32[]{:S(2)}) copy-start(bf16[384,12]{0,1:T(8,128)(2,1)} %param.9) | copy-start | bytes 27652
  116.3 1.0 copy-start.2
  117.8 7.7 %copy-start.1 = (bf16[3,16,104,16]{3,2,1,0:T(8,128)(2,1)S(1)}, bf16[3,16,104,16]{3,2,1,0:T(8,128)(2,1)}, u32[]{:S(2)}) copy-start(bf16[3,16,104,16]{3,2,1,0:T(8,128)(2,1)} %get-tuple-element.5) | copy-start | bytes 479236
  118.9 18.6 %collective-permute-start = (bf16[3,1,104,384]{3,2,0,1:T(8,128)(2,1)S(1)}, bf16[3,1,104,384]{3,2,0,1:T(8,128)(2,1)}, u32[]{:S(2)}, u32[]{:S(2)}) collective-permute-start(bf16[3,1,104,384]{3,2,0,1:T(8,128)(2,1)S(1)} %multiply_convert_fusion.5), channel_id=1, source_target_pairs={{0,1},{1,2},{2,3},{3,4},{4,5},{5,6},{6,7},{7,8},{8,9},{9,10},{10,1... | collective-permute-start | bytes 718856 | tf_op jit(solution)/shard_map/ppermute | solution.py:24
  120.9 16.7 %collective-permute-start.1 = (bf16[3,1,104,384]{3,2,0,1:T(8,128)(2,1)S(1)}, bf16[3,1,104,384]{3,2,0,1:T(8,128)(2,1)}, u32[]{:S(2)}, u32[]{:S(2)}) collective-permute-start(bf16[3,1,104,384]{3,2,0,1:T(8,128)(2,1)S(1)} %multiply_convert_fusion.5), channel_id=1, source_target_pairs={{1,0},{2,1},{3,2},{4,3},{5,4},{6,5},{7,6},{8,7},{9,8},{10,9},{11,1... | collective-permute-start | bytes 718856 | tf_op jit(solution)/shard_map/ppermute | solution.py:27
  130.9 10.7 %collective-permute-start.2 = (bf16[3,1,104,384]{3,2,0,1:T(8,128)(2,1)S(1)}, bf16[3,1,104,384]{3,2,0,1:T(8,128)(2,1)S(1)}, u32[]{:S(2)}, u32[]{:S(2)}) collective-permute-start(bf16[3,1,104,384]{3,2,0,1:T(8,128)(2,1)S(1)} %multiply_convert_fusion.2), channel_id=1, source_target_pairs={{0,1},{1,2},{2,3},{3,4},{4,5},{5,6},{6,7},{7,8},{8,9},{9,10},{10,1... | collective-permute-start | bytes 718856 | tf_op jit(solution)/shard_map/ppermute | solution.py:24
  132.8 8.8 %collective-permute-start.3 = (bf16[3,1,104,384]{3,2,0,1:T(8,128)(2,1)S(1)}, bf16[3,1,104,384]{3,2,0,1:T(8,128)(2,1)S(1)}, u32[]{:S(2)}, u32[]{:S(2)}) collective-permute-start(bf16[3,1,104,384]{3,2,0,1:T(8,128)(2,1)S(1)} %multiply_convert_fusion.2), channel_id=1, source_target_pairs={{1,0},{2,1},{3,2},{4,3},{5,4},{6,5},{7,6},{8,7},{9,8},{10,9},{11,1... | collective-permute-start | bytes 718856 | tf_op jit(solution)/shard_map/ppermute | solution.py:27
  138.7 1.4 copy-start
  140.2 1.4 slice-start
  142.5 3.9 %slice-start.1 = ((s8[7962624]{0:T(1024)(128)(4,1)}), s8[4194304]{0:T(1024)(128)(4,1)S(1)}, s32[]{:S(2)}) async-start(s8[7962624]{0:T(1024)(128)(4,1)} %bitcast.102), calls=%async_computation.2 | async-start | bytes 8388608
  142.9 1.4 copy-start.5
  143.1 3.7 %slice-start.2 = ((s8[7962624]{0:T(1024)(128)(4,1)}), s8[3768320]{0:T(1024)(128)(4,1)S(1)}, s32[]{:S(2)}) async-start(s8[7962624]{0:T(1024)(128)(4,1)} %bitcast.102), calls=%async_computation.3 | async-start | bytes 7536640
  146.4 1.7 copy-start.3
  151.9 1.6 copy-start.4
  153.5 3.4 %copy-start.6 = (bf16[3,1,104,3456]{3,2,0,1:T(8,128)(2,1)S(1)}, bf16[3,1,104,3456]{3,2,0,1:T(8,128)(2,1)}, u32[]{:S(2)}) copy-start(bf16[3,1,104,3456]{3,2,0,1:T(8,128)(2,1)} %copy-done.5) | copy-start | bytes 6469636
Sparse Core Ops, SparseCore 0:
  14.3 100.0 all-reduce.10
where the time goes:
time: 175 us; the launch traced here: 172 us
  waiting for transfers between devices  100 us (57%)
  local copies, waits for them, and re-layouts  22.8 us (13%)
  matrix products  15.9 us (9%)
  between operations  15.5 us (9%)
  starting transfers between devices  13.1 us (7%)
  other arithmetic  4.23 us (2%)
    psum x1, waiting for transfers between devices, spread(): return lax.psum(kept, axis)  100 us
    dot_general x12, matrix products, local_conv(): jnp.dot(stacked.reshape(-1, stacked.shape[-1]), block, preferred_element_...  15.5 us
    unnamed x78, local copies, waits for them, and re-layouts  10.4 us
    ppermute x2, starting transfers between devices, with_halo(): lax.ppermute(lax.slice_in_dim(block, 0, width, axis=dim), axis, backward)  9.26 us
    reshape x2, local copies, waits for them, and re-layouts, local(): frames = group_latent.reshape(FRAMES, height, columns, ZC)  3.94 us
    ppermute x2, starting transfers between devices, with_halo(): lax.ppermute(lax.slice_in_dim(block, block.shape[dim] - width, None, axis...  3.84 us
  transfers between devices with their start and end apart: 5, of which 1 were waited for; matrix products, arithmetic and copies ran while one was open for 5% of the time, Pallas kernels for 0%

commit v1 on v0

v1 whole, which is shorter than its diff:
```python
import jax
import jax.numpy as jnp
from jax import lax
from jax.sharding import PartitionSpec as P

ZC = 16
HALO = 2

epsilon = 1e-06

DIMS = ("NDHWC", "DHWIO", "NDHWC")


def rms_scale(values):
    return values * lax.rsqrt(jnp.mean(values * values, axis=-1, keepdims=True) + epsilon)


def gather_rows(x, n, rows_dev, position):
    bits = n.bit_length() - 1
    for k in reversed(range(bits)):
        half = (1 << k) * rows_dev
        size = half + 2 * HALO
        bit = (position >> k) & 1
        own = lax.dynamic_slice_in_dim(x, bit * half, size, 0)
        send = lax.dynamic_slice_in_dim(x, (1 - bit) * half, size, 0)
        pairs = [(i, i ^ (1 << k)) for i in range(n)]
        x = own + lax.ppermute(send, "dev", pairs)
    return x


def causal_conv(source, weights, channels):
    padded = jnp.pad(source, ((2, 0), (0, 0), (1, 1), (0, 0)))
    kernel = weights.reshape(3, 3, 3, channels, weights.shape[1])
    out = lax.conv_general_dilated(
        padded[None],
        kernel,
        window_strides=(1, 1, 1),
        padding="VALID",
        dimension_numbers=DIMS,
        preferred_element_type=jnp.float32,
    )
    return out[0]


def local(latents, owners, conv_in, conv_mid, to_pixels):
    n = lax.axis_size("dev")
    assert n & (n - 1) == 0
    position = lax.axis_index("dev")
    groups, frames, height, width = latents.shape[1:]
    columns = width // ZC
    channels = conv_mid.shape[1]
    rows_dev = height // n

    x = jnp.transpose(latents[0], (2, 0, 1, 3))
    keep = owners == position
    x = jnp.where(keep[None, :, None, None], x, jnp.zeros_like(x))
    x = jnp.pad(x, ((HALO, HALO), (0, 0), (0, 0), (0, 0)))
    x = gather_rows(x, n, rows_dev, position)

    window = jnp.transpose(x, (1, 2, 0, 3)).reshape(groups * frames, rows_dev + 2 * HALO, columns, ZC)
    first_act = causal_conv(window, conv_in, ZC)
    activated = jax.nn.silu(rms_scale(first_act)).astype(jnp.bfloat16)
    row_of = position * rows_dev - 1 + jnp.arange(rows_dev + 2)
    inside = (row_of >= 0) & (row_of < height)
    activated = jnp.where(inside[None, :, None, None], activated, jnp.zeros_like(activated))
    second_act = causal_conv(activated, conv_mid, channels)
    summed = first_act[:, 1 : 1 + rows_dev] + second_act
    normed = rms_scale(summed).astype(jnp.bfloat16)
    projected = jnp.dot(normed.reshape(-1, channels), to_pixels, preferred_element_type=jnp.float32)
    projected = projected.reshape(groups, frames, rows_dev, columns, 2, 2, 3).transpose(0, 1, 2, 4, 3, 5, 6)
    return projected.reshape(groups, frames, 2 * rows_dev, 6 * columns).astype(jnp.bfloat16)


def solution(mesh):
    in_specs = (P(("stream", "dev"), None, None, None, None), P("stream"), P(), P(), P())
    out_specs = P("stream", None, "dev", None)
    return jax.shard_map(local, mesh=mesh, in_specs=in_specs, out_specs=out_specs, check_vma=False)
```

time: 175 us -> 60.7 us (0.35); the launches traced: 172 us -> 59.7 us
  waiting for transfers between devices: 100 us -> 27.7 us
  between operations: 15.5 us -> 0.3 us
  starting transfers between devices: 13.1 us -> 2.1 us
  local copies, waits for them, and re-layouts: 22.8 us -> 15 us
  matrix products: 15.9 us -> 10.7 us
    psum x1 -> x0, waiting for transfers between devices: 100 us -> none  [spread(): return lax.psum(kept, axis)]
    ppermute x4, waiting for transfers between devices: 0.01 us -> 27.7 us  [gather_rows(): x = own + lax.ppermute(send, 'dev', pairs)]
    dot_general x12 -> x0, matrix products: 15.5 us -> none  [local_conv(): jnp.dot(stacked.reshape(-1, stacked.shape[-1]), block, preferred_element_...]
    ppermute x4, starting transfers between devices: 13.1 us -> 2.1 us  [gather_rows(): x = own + lax.ppermute(send, 'dev', pairs)]
    conv_general_dilated x0 -> x2, matrix products: none -> 10.3 us  [causal_conv(): lax.conv_general_dilated(padded[None], kernel, window_strides=(1, 1, 1),...]
    conv_general_dilated x0 -> x9, local copies, waits for them, and re-layouts: none -> 8.41 us  [causal_conv(): lax.conv_general_dilated(padded[None], kernel, window_strides=(1, 1, 1),...]
    unnamed x78 -> x11, local copies, waits for them, and re-layouts: 10.4 us -> 2.26 us
    reshape x5 -> x1, local copies, waits for them, and re-layouts: 4.34 us -> 0.62 us  [local(): jnp.transpose(x, (1, 2, 0, 3))]
  transfers between devices with their start and end apart: 5 -> 4, of which waited for: 1 -> 4; matrix products, arithmetic and copies ran while one was open for 5% -> 0% of each run, Pallas kernels for 0% -> 0%
where the time goes in v1:
time: 60.7 us; the launch traced here: 59.7 us
  waiting for transfers between devices  27.7 us (46%)
  local copies, waits for them, and re-layouts  15 us (25%)
  matrix products  10.7 us (18%)
  other arithmetic  3.99 us (7%)
  starting transfers between devices  2.1 us (3%)
    ppermute x4, waiting for transfers between devices, gather_rows(): x = own + lax.ppermute(send, 'dev', pairs)  27.7 us
    conv_general_dilated x2, matrix products, causal_conv(): lax.conv_general_dilated(padded[None], kernel, window_strides=(1, 1, 1),...  10.3 us
    conv_general_dilated x9, local copies, waits for them, and re-layouts, causal_conv(): lax.conv_general_dilated(padded[None], kernel, window_strides=(1, 1, 1),...  8.41 us
    unnamed x11, local copies, waits for them, and re-layouts  2.26 us
    ppermute x4, starting transfers between devices, gather_rows(): x = own + lax.ppermute(send, 'dev', pairs)  2.1 us
    convert_element_type x2, local copies, waits for them, and re-layouts, local(): projected.reshape(groups, frames, 2 * rows_dev, 6 * columns)  1.84 us
    broadcast_in_dim x4, local copies, waits for them, and re-layouts, causal_conv(): padded[None]  1.29 us
  transfers between devices with their start and end apart: 4, of which 4 were waited for; matrix products, arithmetic and copies ran while one was open for 0% of the time, Pallas kernels for 0%

profile of v1, /device:TPU:24, one launch (start us, length us, event | category | flops | bytes accessed | tf_op | source)
XLA Modules:
  0.0 59.7 jit_solution(9186513816796094850)
XLA Ops:
  0.0 0.7 %broadcast_compare_fusion = pred[2]{0:T(512)(128)(4,1)S(1)} fusion(s32[2]{0:T(128)} %param.6, s32[]{:T(128)S(6)} %axis_index.12), kind=kLoop, calls=%fused_computation.46 | loop fusion | flops 2 | bytes 14 | tf_op jit(solution)/shard_map/eq | solution.py:55
  0.7 1.1 %fusion.23 = bf16[16,2,3,1664]{3,0,2,1:T(8,128)(2,1)S(1)} fusion(bf16[1,2,3,16,1664]{4,3,2,1,0:T(8,128)(2,1)} %param.5, pred[2]{0:T(512)(128)(4,1)S(1)} %broadcast_compare_fusion), kind=kLoop, calls=%fused_computation.35 | loop fusion | flops 159744 | bytes 638978 | tf_op jit(solution)/shard_map/jit(_where)/select_n | solution.py:56
  1.9 0.4 collective-permute-start
  2.3 16.6 %collective-permute-done = bf16[12,2,3,1664]{3,0,2,1:T(8,128)(2,1)S(1)} collective-permute-done((bf16[12,2,3,1664]{3,0,2,1:T(8,128)(2,1)S(1)}, bf16[12,2,3,1664]{3,0,2,1:T(8,128)(2,1)S(1)}, u32[]{:S(2)}, u32[]{:S(2)}) %collective-permute-start) | collective-permute-done | bytes 239648 | tf_op jit(solution)/shard_map/ppermute | solution.py:27
  19.2 6.0 %collective-permute-done.1 = bf16[8,2,3,1664]{3,0,2,1:T(8,128)(2,1)S(1)} collective-permute-done((bf16[8,2,3,1664]{3,0,2,1:T(8,128)(2,1)S(1)}, bf16[8,2,3,1664]{3,0,2,1:T(8,128)(2,1)S(1)}, u32[]{:S(2)}, u32[]{:S(2)}) %collective-permute-start.1) | collective-permute-done | bytes 159776 | tf_op jit(solution)/shard_map/ppermute | solution.py:27
  25.4 1.6 %collective-permute-start.2 = (bf16[6,2,3,1664]{3,0,2,1:T(8,128)(2,1)S(1)}, bf16[6,2,3,1664]{3,0,2,1:T(8,128)(2,1)S(1)}, u32[]{:S(2)}, u32[]{:S(2)}) collective-permute-start(bf16[6,2,3,1664]{3,0,2,1:T(8,128)(2,1)S(1)} %constant_dynamic-slice_fusion.1), channel_id=1, source_target_pairs={{0,2},{1,3},{2,0},{3,1},{4,6},{5,7},{6,4},{7,5},{8,10},{9,11},{10,... | collective-permute-start | bytes 359432 | tf_op jit(solution)/shard_map/ppermute | solution.py:27
  27.0 3.8 %collective-permute-done.2 = bf16[6,2,3,1664]{3,0,2,1:T(8,128)(2,1)S(1)} collective-permute-done((bf16[6,2,3,1664]{3,0,2,1:T(8,128)(2,1)S(1)}, bf16[6,2,3,1664]{3,0,2,1:T(8,128)(2,1)S(1)}, u32[]{:S(2)}, u32[]{:S(2)}) %collective-permute-start.2) | collective-permute-done | bytes 119840 | tf_op jit(solution)/shard_map/ppermute | solution.py:27
  30.9 1.4 %collective-permute-done.3 = bf16[5,2,3,1664]{3,0,2,1:T(8,128)(2,1)S(1)} collective-permute-done((bf16[5,2,3,1664]{3,0,2,1:T(8,128)(2,1)S(1)}, bf16[5,2,3,1664]{3,0,2,1:T(8,128)(2,1)S(1)}, u32[]{:S(2)}, u32[]{:S(2)}) %collective-permute-start.3) | collective-permute-done | bytes 99872 | tf_op jit(solution)/shard_map/ppermute | solution.py:27
  32.4 0.6 %reshape.51 = bf16[6,5,104,16]{3,2,0,1:T(8,128)(2,1)S(1)} reshape(bf16[2,3,5,1664]{3,1,0,2:T(4,128)(2,1)S(1)} %copy.6) | data formatting | bytes 199680 | tf_op jit(solution)/shard_map/reshape | solution.py:60
  34.4 2.9 %convolution_select_fusion = f32[6,3,8,14,384]{4,2,3,1,0:T(8,128)S(1)} fusion(bf16[3,3,3,16,384]{4,3,2,1,0:T(8,128)(2,1)S(1)} %bitcast.62, pred[8,14]{0,1:T(8,128)(4,1)S(1)} %copy-done.2, bf16[8,5,1,7,2,16]{5,3,4,1,0,2:T(8,128)(2,1)S(1)} %slice.8, bf16[8,5,1,8,14,16]{5,3,4,1,0,2:T(8,128)(2,1)S(1)} %copy.9), kind=kOutput, calls=%fused_computation.14 | convolution fusion | flops 670126080 | bytes 3589744 | tf_op jit(solution)/shard_map/conv_general_dilated | solution.py:34
  37.3 2.4 %copy.10 = f32[6,3,8,14,384]{4,3,2,1,0:T(8,128)} copy(f32[6,3,8,14,384]{4,2,3,1,0:T(8,128)S(1)} %convolution_select_fusion) | data formatting | bytes 6193152 | tf_op jit(solution)/shard_map/conv_general_dilated | solution.py:34
  39.7 3.0 %reshape.61 = f32[6,3,1,112,384]{4,3,1,0,2:T(8,128)S(1)} reshape(f32[6,3,8,14,384]{4,3,2,1,0:T(8,128)} %copy.10) | data formatting | bytes 6193152 | tf_op jit(solution)/shard_map/conv_general_dilated | solution.py:34
  42.8 0.4 multiply_reduce_fusion
  43.4 0.9 %fusion.9 = bf16[6,3,104,384]{3,2,1,0:T(8,128)(2,1)S(1)} fusion(f32[6,3,104]{2,1,0:T(4,128)S(1)} %add_rsqrt_fusion, pred[3]{0:T(512)(128)(4,1)S(1)} %compare_and_fusion, f32[6,3,1,112,384]{4,3,1,0,2:T(8,128)S(1)} %reshape.61), kind=kLoop, calls=%fused_computation.15 | loop fusion | flops 5031936 | bytes 4320579 | tf_op jit(solution)/shard_map/jit(_where)/select_n | solution.py:65
  44.3 0.6 pad_bitcast_fusion
  44.9 0.4 copy.22
  45.5 0.5 copy.13
  46.1 0.4 slice-done
  46.5 1.4 %slice-done.1 = s8[3768320]{0:T(1024)(128)(4,1)S(1)} async-done(((s8[7962624]{0:T(1024)(128)(4,1)}), s8[3768320]{0:T(1024)(128)(4,1)S(1)}, s32[]{:S(2)}) %slice-start.1) | async-done | bytes 3768344
  47.9 7.4 %fusion.10 = f32[6,1,8,14,384]{4,2,3,1,0:T(8,128)S(1)} fusion(bf16[3,3,3,384,384]{4,3,2,1,0:T(8,128)(2,1)S(1)} %bitcast.69, bf16[8,3,1,7,2,384]{5,3,4,1,0,2:T(8,128)(2,1)S(1)} %slice.11, bf16[8,3,1,8,14,384]{5,3,4,1,0,2:T(8,128)(2,1)S(1)} %copy.13, pred[8,14]{0,1:T(8,128)(4,1)S(1)} %copy-done.2), kind=kOutput, calls=%fused_computation.16 | convolution fusion | flops 5358219264 | bytes 11317360 | tf_op jit(solution)/shard_map/conv_general_dilated | solution.py:34
  55.3 1.1 %copy.14 = f32[6,1,8,14,384]{4,1,3,2,0:T(1,128)S(1)} copy(f32[6,1,8,14,384]{4,2,3,1,0:T(8,128)S(1)} %fusion.10) | data formatting | bytes 2064384 | tf_op jit(solution)/shard_map/conv_general_dilated | solution.py:34
  56.4 0.7 %slice.12 = f32[6,1,1,104,384]{4,1,3,0,2:T(1,128)S(1)} slice(f32[6,1,1,112,384]{4,1,3,0,2:T(1,128)S(1)} %bitcast.64), slice={[0:6], [0:1], [0:1], [0:104], [0:384]} | slice | bytes 1916928 | tf_op jit(solution)/shard_map/conv_general_dilated | solution.py:34
  57.9 0.5 copy.16
  58.4 1.3 %convert_element_type.29 = bf16[2,3,2,624]{3,2,1,0:T(2,128)(2,1)} reshape(bf16[2,3,1,2,104,2,3]{6,5,4,3,1,0,2:T(2,128)(2,1)S(1)} %copy.16) | data formatting | bytes 29952 | tf_op jit(solution)/shard_map/convert_element_type | solution.py:71
  (35 shorter events, 3.5 us)
Async XLA Ops:
  0.0 34.4 %copy-start = (bf16[432,384]{1,0:T(8,128)(2,1)S(1)}, bf16[432,384]{1,0:T(8,128)(2,1)}, u32[]{:S(2)}) copy-start(bf16[432,384]{1,0:T(8,128)(2,1)} %param.7) | copy-start | bytes 995332
  0.0 26.9 %copy-start.1 = (bf16[384,12]{0,1:T(8,128)(2,1)S(1)}, bf16[384,12]{0,1:T(8,128)(2,1)}, u32[]{:S(2)}) copy-start(bf16[384,12]{0,1:T(8,128)(2,1)} %param.9) | copy-start | bytes 27652
  1.9 17.0 %collective-permute-start = (bf16[12,2,3,1664]{3,0,2,1:T(8,128)(2,1)S(1)}, bf16[12,2,3,1664]{3,0,2,1:T(8,128)(2,1)S(1)}, u32[]{:S(2)}, u32[]{:S(2)}) collective-permute-start(bf16[12,2,3,1664]{3,0,2,1:T(8,128)(2,1)S(1)} %pad_dynamic-slice_fusion), channel_id=1, source_target_pairs={{0,8},{1,9},{2,10},{3,11},{4,12},{5,13},{6,14},{7,15},{8,0},{9,1},... | collective-permute-start | bytes 718856 | tf_op jit(solution)/shard_map/ppermute | solution.py:27
  19.2 6.1 %collective-permute-start.1 = (bf16[8,2,3,1664]{3,0,2,1:T(8,128)(2,1)S(1)}, bf16[8,2,3,1664]{3,0,2,1:T(8,128)(2,1)S(1)}, u32[]{:S(2)}, u32[]{:S(2)}) collective-permute-start(bf16[8,2,3,1664]{3,0,2,1:T(8,128)(2,1)S(1)} %constant_dynamic-slice_fusion.2), channel_id=1, source_target_pairs={{0,4},{1,5},{2,6},{3,7},{4,0},{5,1},{6,2},{7,3},{8,12},{9,13},{10,... | collective-permute-start | bytes 479240 | tf_op jit(solution)/shard_map/ppermute | solution.py:27
  25.4 5.3 %collective-permute-start.2 = (bf16[6,2,3,1664]{3,0,2,1:T(8,128)(2,1)S(1)}, bf16[6,2,3,1664]{3,0,2,1:T(8,128)(2,1)S(1)}, u32[]{:S(2)}, u32[]{:S(2)}) collective-permute-start(bf16[6,2,3,1664]{3,0,2,1:T(8,128)(2,1)S(1)} %constant_dynamic-slice_fusion.1), channel_id=1, source_target_pairs={{0,2},{1,3},{2,0},{3,1},{4,6},{5,7},{6,4},{7,5},{8,10},{9,11},{10,... | collective-permute-start | bytes 359432 | tf_op jit(solution)/shard_map/ppermute | solution.py:27
  30.9 1.5 %collective-permute-start.3 = (bf16[5,2,3,1664]{3,0,2,1:T(8,128)(2,1)S(1)}, bf16[5,2,3,1664]{3,0,2,1:T(8,128)(2,1)S(1)}, u32[]{:S(2)}, u32[]{:S(2)}) collective-permute-start(bf16[5,2,3,1664]{3,0,2,1:T(8,128)(2,1)S(1)} %constant_dynamic-slice_fusion), channel_id=1, source_target_pairs={{0,1},{1,0},{2,3},{3,2},{4,5},{5,4},{6,7},{7,6},{8,9},{9,8},{10,11... | collective-permute-start | bytes 299528 | tf_op jit(solution)/shard_map/ppermute | solution.py:27
  33.6 0.8 %copy-start.2 = (pred[8,14]{0,1:T(8,128)(4,1)S(1)}, pred[8,14]{0,1:T(8,128)(4,1)}, u32[]{:S(2)}) copy-start(pred[8,14]{0,1:T(8,128)(4,1)} %constant.61) | copy-start | bytes 340
  44.3 2.2 %slice-start = ((s8[7962624]{0:T(1024)(128)(4,1)}), s8[4194304]{0:T(1024)(128)(4,1)S(1)}, s32[]{:S(2)}) async-start(s8[7962624]{0:T(1024)(128)(4,1)} %bitcast.67), calls=%async_computation | async-start | bytes 8388608
  45.3 2.6 %slice-start.1 = ((s8[7962624]{0:T(1024)(128)(4,1)}), s8[3768320]{0:T(1024)(128)(4,1)S(1)}, s32[]{:S(2)}) async-start(s8[7962624]{0:T(1024)(128)(4,1)} %bitcast.67), calls=%async_computation.1 | async-start | bytes 7536640

commit v2 on v1

--- a/solution.py
+++ b/solution.py
@@ -15,15 +15,20 @@
     return values * lax.rsqrt(jnp.mean(values * values, axis=-1, keepdims=True) + epsilon)
 
 
-def gather_rows(x, n, rows_dev, position):
+def reverse_bits(value, bits):
+    return sum(((value >> b) & 1) << (bits - 1 - b) for b in range(bits))
+
+
+def gather_rows(x, n, rows_dev, slot):
     bits = n.bit_length() - 1
     for k in reversed(range(bits)):
         half = (1 << k) * rows_dev
         size = half + 2 * HALO
-        bit = (position >> k) & 1
+        bit = (slot >> k) & 1
         own = lax.dynamic_slice_in_dim(x, bit * half, size, 0)
         send = lax.dynamic_slice_in_dim(x, (1 - bit) * half, size, 0)
-        pairs = [(i, i ^ (1 << k)) for i in range(n)]
+        flip = 1 << (bits - 1 - k)
+        pairs = [(i, i ^ flip) for i in range(n)]
         x = own + lax.ppermute(send, "dev", pairs)
     return x
 
@@ -50,17 +55,19 @@
     columns = width // ZC
     channels = conv_mid.shape[1]
     rows_dev = height // n
+    bits = n.bit_length() - 1
+    slot = reverse_bits(position, bits)
 
     x = jnp.transpose(latents[0], (2, 0, 1, 3))
     keep = owners == position
     x = jnp.where(keep[None, :, None, None], x, jnp.zeros_like(x))
     x = jnp.pad(x, ((HALO, HALO), (0, 0), (0, 0), (0, 0)))
-    x = gather_rows(x, n, rows_dev, position)
+    x = gather_rows(x, n, rows_dev, slot)
 
     window = jnp.transpose(x, (1, 2, 0, 3)).reshape(groups * frames, rows_dev + 2 * HALO, columns, ZC)
     first_act = causal_conv(window, conv_in, ZC)
     activated = jax.nn.silu(rms_scale(first_act)).astype(jnp.bfloat16)
-    row_of = position * rows_dev - 1 + jnp.arange(rows_dev + 2)
+    row_of = slot * rows_dev - 1 + jnp.arange(rows_dev + 2)
     inside = (row_of >= 0) & (row_of < height)
     activated = jnp.where(inside[None, :, None, None], activated, jnp.zeros_like(activated))
     second_act = causal_conv(activated, conv_mid, channels)
@@ -68,7 +75,8 @@
     normed = rms_scale(summed).astype(jnp.bfloat16)
     projected = jnp.dot(normed.reshape(-1, channels), to_pixels, preferred_element_type=jnp.float32)
     projected = projected.reshape(groups, frames, rows_dev, columns, 2, 2, 3).transpose(0, 1, 2, 4, 3, 5, 6)
-    return projected.reshape(groups, frames, 2 * rows_dev, 6 * columns).astype(jnp.bfloat16)
+    pixels = projected.reshape(groups, frames, 2 * rows_dev, 6 * columns).astype(jnp.bfloat16)
+    return lax.ppermute(pixels, "dev", [(i, reverse_bits(i, bits)) for i in range(n)])
 
 
 def solution(mesh):

time: 60.7 us -> 59.5 us (0.980); the launches traced: 59.7 us -> 59.3 us
  waiting for transfers between devices: 27.7 us -> 24.9 us
  starting transfers between devices: 2.1 us -> 4.46 us
    ppermute x4, waiting for transfers between devices: 27.7 us -> 19.1 us  [gather_rows(): x = own + lax.ppermute(send, 'dev', pairs)]
    ppermute x0 -> x1, waiting for transfers between devices: none -> 5.82 us  [local(): lax.ppermute(pixels, 'dev', [(i, reverse_bits(i, bits)) for i in range(n)])]
    ppermute x0 -> x1, starting transfers between devices: none -> 1.92 us  [local(): lax.ppermute(pixels, 'dev', [(i, reverse_bits(i, bits)) for i in range(n)])]
    unnamed x11 -> x12, local copies, waits for them, and re-layouts: 2.26 us -> 2.86 us
  transfers between devices with their start and end apart: 4 -> 5, of which waited for: 4 -> 5; matrix products, arithmetic and copies ran while one was open for 0% -> 0% of each run, Pallas kernels for 0% -> 0%
where the time goes in v2:
time: 59.5 us; the launch traced here: 59.3 us
  waiting for transfers between devices  24.9 us (42%)
  local copies, waits for them, and re-layouts  15 us (25%)
  matrix products  10.7 us (18%)
  starting transfers between devices  4.46 us (7%)
  other arithmetic  3.98 us (7%)
    ppermute x4, waiting for transfers between devices, gather_rows(): x = own + lax.ppermute(send, 'dev', pairs)  19.1 us
    conv_general_dilated x2, matrix products, causal_conv(): lax.conv_general_dilated(padded[None], kernel, window_strides=(1, 1, 1),...  10.3 us
    conv_general_dilated x9, local copies, waits for them, and re-layouts, causal_conv(): lax.conv_general_dilated(padded[None], kernel, window_strides=(1, 1, 1),...  8.41 us
    ppermute x1, waiting for transfers between devices, local(): lax.ppermute(pixels, 'dev', [(i, reverse_bits(i, bits)) for i in range(n)])  5.82 us
    unnamed x12, local copies, waits for them, and re-layouts  2.86 us
    ppermute x4, starting transfers between devices, gather_rows(): x = own + lax.ppermute(send, 'dev', pairs)  2.54 us
    ppermute x1, starting transfers between devices, local(): lax.ppermute(pixels, 'dev', [(i, reverse_bits(i, bits)) for i in range(n)])  1.92 us
    broadcast_in_dim x4, local copies, waits for them, and re-layouts, causal_conv(): padded[None]  1.29 us
  transfers between devices with their start and end apart: 5, of which 5 were waited for; matrix products, arithmetic and copies ran while one was open for 0% of the time, Pallas kernels for 0%

profile of v2, /device:TPU:24, one launch (start us, length us, event | category | flops | bytes accessed | tf_op | source)
XLA Modules:
  0.0 59.3 jit_solution(17622118793618414425)
XLA Ops:
  0.0 0.7 %broadcast_compare_fusion = pred[2]{0:T(512)(128)(4,1)S(1)} fusion(s32[2]{0:T(128)} %param.6, s32[]{:T(128)S(6)} %axis_index.12), kind=kLoop, calls=%fused_computation.46 | loop fusion | flops 2 | bytes 14 | tf_op jit(solution)/shard_map/eq | solution.py:62
  0.7 1.1 %fusion.23 = bf16[16,2,3,1664]{3,0,2,1:T(8,128)(2,1)S(1)} fusion(bf16[1,2,3,16,1664]{4,3,2,1,0:T(8,128)(2,1)} %param.5, pred[2]{0:T(512)(128)(4,1)S(1)} %broadcast_compare_fusion), kind=kLoop, calls=%fused_computation.35 | loop fusion | flops 159744 | bytes 638978 | tf_op jit(solution)/shard_map/jit(_where)/select_n | solution.py:63
  2.0 1.6 %collective-permute-done = bf16[12,2,3,1664]{3,0,2,1:T(8,128)(2,1)S(1)} collective-permute-done((bf16[12,2,3,1664]{3,0,2,1:T(8,128)(2,1)S(1)}, bf16[12,2,3,1664]{3,0,2,1:T(8,128)(2,1)S(1)}, u32[]{:S(2)}, u32[]{:S(2)}) %collective-permute-start) | collective-permute-done | bytes 239648 | tf_op jit(solution)/shard_map/ppermute | solution.py:32
  3.9 1.6 %collective-permute-start.1 = (bf16[8,2,3,1664]{3,0,2,1:T(8,128)(2,1)S(1)}, bf16[8,2,3,1664]{3,0,2,1:T(8,128)(2,1)S(1)}, u32[]{:S(2)}, u32[]{:S(2)}) collective-permute-start(bf16[8,2,3,1664]{3,0,2,1:T(8,128)(2,1)S(1)} %constant_dynamic-slice_fusion.2), channel_id=1, source_target_pairs={{0,2},{1,3},{2,0},{3,1},{4,6},{5,7},{6,4},{7,5},{8,10},{9,11},{10,... | collective-permute-start | bytes 479240 | tf_op jit(solution)/shard_map/ppermute | solution.py:32
  5.4 4.7 %collective-permute-done.1 = bf16[8,2,3,1664]{3,0,2,1:T(8,128)(2,1)S(1)} collective-permute-done((bf16[8,2,3,1664]{3,0,2,1:T(8,128)(2,1)S(1)}, bf16[8,2,3,1664]{3,0,2,1:T(8,128)(2,1)S(1)}, u32[]{:S(2)}, u32[]{:S(2)}) %collective-permute-start.1) | collective-permute-done | bytes 159776 | tf_op jit(solution)/shard_map/ppermute | solution.py:32
  10.2 0.5 collective-permute-start.2
  10.8 4.8 %collective-permute-done.2 = bf16[6,2,3,1664]{3,0,2,1:T(8,128)(2,1)S(1)} collective-permute-done((bf16[6,2,3,1664]{3,0,2,1:T(8,128)(2,1)S(1)}, bf16[6,2,3,1664]{3,0,2,1:T(8,128)(2,1)S(1)}, u32[]{:S(2)}, u32[]{:S(2)}) %collective-permute-start.2) | collective-permute-done | bytes 119840 | tf_op jit(solution)/shard_map/ppermute | solution.py:32
  16.1 8.0 %collective-permute-done.3 = bf16[5,2,3,1664]{3,0,2,1:T(8,128)(2,1)S(1)} collective-permute-done((bf16[5,2,3,1664]{3,0,2,1:T(8,128)(2,1)S(1)}, bf16[5,2,3,1664]{3,0,2,1:T(8,128)(2,1)S(1)}, u32[]{:S(2)}, u32[]{:S(2)}) %collective-permute-start.3) | collective-permute-done | bytes 99872 | tf_op jit(solution)/shard_map/ppermute | solution.py:32
  24.3 0.6 %reshape.51 = bf16[6,5,104,16]{3,2,0,1:T(8,128)(2,1)S(1)} reshape(bf16[2,3,5,1664]{3,1,0,2:T(4,128)(2,1)S(1)} %copy.6) | data formatting | bytes 199680 | tf_op jit(solution)/shard_map/reshape | solution.py:67
  26.2 2.9 %convolution_select_fusion = f32[6,3,8,14,384]{4,2,3,1,0:T(8,128)S(1)} fusion(bf16[3,3,3,16,384]{4,3,2,1,0:T(8,128)(2,1)S(1)} %bitcast.62, pred[8,14]{0,1:T(8,128)(4,1)S(1)} %copy-done.2, bf16[8,5,1,7,2,16]{5,3,4,1,0,2:T(8,128)(2,1)S(1)} %slice.8, bf16[8,5,1,8,14,16]{5,3,4,1,0,2:T(8,128)(2,1)S(1)} %copy.9), kind=kOutput, calls=%fused_computation.14 | convolution fusion | flops 670126080 | bytes 3589744 | tf_op jit(solution)/shard_map/conv_general_dilated | solution.py:39
  29.2 2.4 %copy.10 = f32[6,3,8,14,384]{4,3,2,1,0:T(8,128)} copy(f32[6,3,8,14,384]{4,2,3,1,0:T(8,128)S(1)} %convolution_select_fusion) | data formatting | bytes 6193152 | tf_op jit(solution)/shard_map/conv_general_dilated | solution.py:39
  31.5 3.0 %reshape.61 = f32[6,3,1,112,384]{4,3,1,0,2:T(8,128)S(1)} reshape(f32[6,3,8,14,384]{4,3,2,1,0:T(8,128)} %copy.10) | data formatting | bytes 6193152 | tf_op jit(solution)/shard_map/conv_general_dilated | solution.py:39
  35.2 0.9 %fusion.9 = bf16[6,3,104,384]{3,2,1,0:T(8,128)(2,1)S(1)} fusion(f32[6,3,104]{2,1,0:T(4,128)S(1)} %add_rsqrt_fusion, pred[3]{0:T(512)(128)(4,1)S(1)} %compare_and_fusion, f32[6,3,1,112,384]{4,3,1,0,2:T(8,128)S(1)} %reshape.61), kind=kLoop, calls=%fused_computation.15 | loop fusion | flops 5031936 | bytes 4320579 | tf_op jit(solution)/shard_map/jit(_where)/select_n | solution.py:72
  36.1 0.6 pad_bitcast_fusion
  37.4 0.5 copy.13
  38.3 1.4 %slice-done.1 = s8[3768320]{0:T(1024)(128)(4,1)S(1)} async-done(((s8[7962624]{0:T(1024)(128)(4,1)}), s8[3768320]{0:T(1024)(128)(4,1)S(1)}, s32[]{:S(2)}) %slice-start.1) | async-done | bytes 3768344
  39.7 7.4 %fusion.10 = f32[6,1,8,14,384]{4,2,3,1,0:T(8,128)S(1)} fusion(bf16[3,3,3,384,384]{4,3,2,1,0:T(8,128)(2,1)S(1)} %bitcast.69, bf16[8,3,1,7,2,384]{5,3,4,1,0,2:T(8,128)(2,1)S(1)} %slice.11, bf16[8,3,1,8,14,384]{5,3,4,1,0,2:T(8,128)(2,1)S(1)} %copy.13, pred[8,14]{0,1:T(8,128)(4,1)S(1)} %copy-done.2), kind=kOutput, calls=%fused_computation.16 | convolution fusion | flops 5358219264 | bytes 11317360 | tf_op jit(solution)/shard_map/conv_general_dilated | solution.py:39
  47.1 1.1 %copy.14 = f32[6,1,8,14,384]{4,1,3,2,0:T(1,128)S(1)} copy(f32[6,1,8,14,384]{4,2,3,1,0:T(8,128)S(1)} %fusion.10) | data formatting | bytes 2064384 | tf_op jit(solution)/shard_map/conv_general_dilated | solution.py:39
  48.2 0.7 %slice.12 = f32[6,1,1,104,384]{4,1,3,0,2:T(1,128)S(1)} slice(f32[6,1,1,112,384]{4,1,3,0,2:T(1,128)S(1)} %bitcast.64), slice={[0:6], [0:1], [0:1], [0:104], [0:384]} | slice | bytes 1916928 | tf_op jit(solution)/shard_map/conv_general_dilated | solution.py:39
  49.7 0.5 copy.16
  50.2 0.7 %convert_element_type.29 = bf16[2,3,2,624]{3,2,1,0:T(2,128)(2,1)S(1)} reshape(bf16[2,3,1,2,104,2,3]{6,5,4,3,1,0,2:T(2,128)(2,1)S(1)} %copy.16) | data formatting | bytes 29952 | tf_op jit(solution)/shard_map/convert_element_type | solution.py:78
  50.9 1.9 %collective-permute-start.4 = (bf16[2,3,2,624]{3,2,1,0:T(2,128)(2,1)S(1)}, bf16[2,3,2,624]{3,2,1,0:T(2,128)(2,1)S(1)}, u32[]{:S(2)}, u32[]{:S(2)}) collective-permute-start(bf16[2,3,2,624]{3,2,1,0:T(2,128)(2,1)S(1)} %convert_element_type.29), channel_id=1, source_target_pairs={{0,0},{1,8},{2,4},{3,12},{4,2},{5,10},{6,6},{7,14},{8,1},{9,9},{10... | collective-permute-start | bytes 44936 | tf_op jit(solution)/shard_map/ppermute | solution.py:79
  52.9 5.8 %collective-permute-done.4 = bf16[2,3,2,624]{3,2,1,0:T(2,128)(2,1)S(1)} collective-permute-done((bf16[2,3,2,624]{3,2,1,0:T(2,128)(2,1)S(1)}, bf16[2,3,2,624]{3,2,1,0:T(2,128)(2,1)S(1)}, u32[]{:S(2)}, u32[]{:S(2)}) %collective-permute-start.4) | collective-permute-done | bytes 15008 | tf_op jit(solution)/shard_map/ppermute | solution.py:79
  58.7 0.6 %copy.31 = bf16[2,3,2,624]{3,2,1,0:T(2,128)(2,1)} copy(bf16[2,3,2,624]{3,2,1,0:T(2,128)(2,1)S(1)} %collective-permute-done.4) | data formatting | bytes 29952
  (38 shorter events, 5.0 us)
Async XLA Ops:
  0.0 26.2 %copy-start = (bf16[432,384]{1,0:T(8,128)(2,1)S(1)}, bf16[432,384]{1,0:T(8,128)(2,1)}, u32[]{:S(2)}) copy-start(bf16[432,384]{1,0:T(8,128)(2,1)} %param.7) | copy-start | bytes 995332
  0.0 10.7 %copy-start.1 = (bf16[384,12]{0,1:T(8,128)(2,1)S(1)}, bf16[384,12]{0,1:T(8,128)(2,1)}, u32[]{:S(2)}) copy-start(bf16[384,12]{0,1:T(8,128)(2,1)} %param.9) | copy-start | bytes 27652
  1.9 1.7 %collective-permute-start = (bf16[12,2,3,1664]{3,0,2,1:T(8,128)(2,1)S(1)}, bf16[12,2,3,1664]{3,0,2,1:T(8,128)(2,1)S(1)}, u32[]{:S(2)}, u32[]{:S(2)}) collective-permute-start(bf16[12,2,3,1664]{3,0,2,1:T(8,128)(2,1)S(1)} %pad_dynamic-slice_fusion), channel_id=1, source_target_pairs={{0,1},{1,0},{2,3},{3,2},{4,5},{5,4},{6,7},{7,6},{8,9},{9,8},{10,11... | collective-permute-start | bytes 718856 | tf_op jit(solution)/shard_map/ppermute | solution.py:32
  3.9 6.2 %collective-permute-start.1 = (bf16[8,2,3,1664]{3,0,2,1:T(8,128)(2,1)S(1)}, bf16[8,2,3,1664]{3,0,2,1:T(8,128)(2,1)S(1)}, u32[]{:S(2)}, u32[]{:S(2)}) collective-permute-start(bf16[8,2,3,1664]{3,0,2,1:T(8,128)(2,1)S(1)} %constant_dynamic-slice_fusion.2), channel_id=1, source_target_pairs={{0,2},{1,3},{2,0},{3,1},{4,6},{5,7},{6,4},{7,5},{8,10},{9,11},{10,... | collective-permute-start | bytes 479240 | tf_op jit(solution)/shard_map/ppermute | solution.py:32
  10.2 5.4 %collective-permute-start.2 = (bf16[6,2,3,1664]{3,0,2,1:T(8,128)(2,1)S(1)}, bf16[6,2,3,1664]{3,0,2,1:T(8,128)(2,1)S(1)}, u32[]{:S(2)}, u32[]{:S(2)}) collective-permute-start(bf16[6,2,3,1664]{3,0,2,1:T(8,128)(2,1)S(1)} %constant_dynamic-slice_fusion.1), channel_id=1, source_target_pairs={{0,4},{1,5},{2,6},{3,7},{4,0},{5,1},{6,2},{7,3},{8,12},{9,13},{10,... | collective-permute-start | bytes 359432 | tf_op jit(solution)/shard_map/ppermute | solution.py:32
  15.7 8.4 %collective-permute-start.3 = (bf16[5,2,3,1664]{3,0,2,1:T(8,128)(2,1)S(1)}, bf16[5,2,3,1664]{3,0,2,1:T(8,128)(2,1)S(1)}, u32[]{:S(2)}, u32[]{:S(2)}) collective-permute-start(bf16[5,2,3,1664]{3,0,2,1:T(8,128)(2,1)S(1)} %constant_dynamic-slice_fusion), channel_id=1, source_target_pairs={{0,8},{1,9},{2,10},{3,11},{4,12},{5,13},{6,14},{7,15},{8,0},{9,1},... | collective-permute-start | bytes 299528 | tf_op jit(solution)/shard_map/ppermute | solution.py:32
  25.4 0.8 %copy-start.2 = (pred[8,14]{0,1:T(8,128)(4,1)S(1)}, pred[8,14]{0,1:T(8,128)(4,1)}, u32[]{:S(2)}) copy-start(pred[8,14]{0,1:T(8,128)(4,1)} %constant.61) | copy-start | bytes 340
  36.1 2.2 %slice-start = ((s8[7962624]{0:T(1024)(128)(4,1)}), s8[4194304]{0:T(1024)(128)(4,1)S(1)}, s32[]{:S(2)}) async-start(s8[7962624]{0:T(1024)(128)(4,1)} %bitcast.67), calls=%async_computation | async-start | bytes 8388608
  37.1 2.6 %slice-start.1 = ((s8[7962624]{0:T(1024)(128)(4,1)}), s8[3768320]{0:T(1024)(128)(4,1)S(1)}, s32[]{:S(2)}) async-start(s8[7962624]{0:T(1024)(128)(4,1)} %bitcast.67), calls=%async_computation.1 | async-start | bytes 7536640
  50.9 7.7 %collective-permute-start.4 = (bf16[2,3,2,624]{3,2,1,0:T(2,128)(2,1)S(1)}, bf16[2,3,2,624]{3,2,1,0:T(2,128)(2,1)S(1)}, u32[]{:S(2)}, u32[]{:S(2)}) collective-permute-start(bf16[2,3,2,624]{3,2,1,0:T(2,128)(2,1)S(1)} %convert_element_type.29), channel_id=1, source_target_pairs={{0,0},{1,8},{2,4},{3,12},{4,2},{5,10},{6,6},{7,14},{8,1},{9,9},{10... | collective-permute-start | bytes 44936 | tf_op jit(solution)/shard_map/ppermute | solution.py:79

commit v3 on v2

v3 whole, which is shorter than its diff:
```python
import jax
import jax.numpy as jnp
from jax import lax
from jax.sharding import PartitionSpec as P

ZC = 16
HALO = 2

epsilon = 1e-06

DIMS = ("NDHWC", "DHWIO", "NDHWC")


def rms_scale(values):
    return values * lax.rsqrt(jnp.mean(values * values, axis=-1, keepdims=True) + epsilon)


def reverse_bits(value, bits):
    return sum(((value >> b) & 1) << (bits - 1 - b) for b in range(bits))


def gather_rows(x, n, rows_dev, slot, hooks=()):
    bits = n.bit_length() - 1
    for k in reversed(range(bits)):
        half = (1 << k) * rows_dev
        size = half + 2 * HALO
        bit = (slot >> k) & 1
        own = lax.dynamic_slice_in_dim(x, bit * half, size, 0)
        send = lax.dynamic_slice_in_dim(x, (1 - bit) * half, size, 0)
        flip = 1 << (bits - 1 - k)
        pairs = [(i, i ^ flip) for i in range(n)]
        x = own + lax.ppermute(send, "dev", pairs)
        step = bits - 1 - k
        if step < len(hooks):
            x = hooks[step](x)
    return x


def causal_conv(source, history, weights, channels):
    padded = jnp.pad(jnp.concatenate([history, source], axis=0), ((0, 0), (0, 0), (1, 1), (0, 0)))
    kernel = weights.reshape(3, 3, 3, channels, weights.shape[1])
    out = lax.conv_general_dilated(
        padded[None],
        kernel,
        window_strides=(1, 1, 1),
        padding="VALID",
        dimension_numbers=DIMS,
        preferred_element_type=jnp.float32,
    )
    return out[0]


def local(latents, owners, conv_in, conv_mid, to_pixels):
    n = lax.axis_size("dev")
    assert n & (n - 1) == 0
    position = lax.axis_index("dev")
    groups, frames, height, width = latents.shape[1:]
    columns = width // ZC
    channels = conv_mid.shape[1]
    rows_dev = height // n
    bits = n.bit_length() - 1
    slot = reverse_bits(position, bits)
    row_of = slot * rows_dev - 1 + jnp.arange(rows_dev + 2)
    inside = (row_of >= 0) & (row_of < height)

    def prepare(group):
        x = jnp.transpose(latents[0, group], (1, 0, 2))
        x = jnp.where(owners[group] == position, x, jnp.zeros_like(x))
        return jnp.pad(x, ((HALO, HALO), (0, 0), (0, 0)))

    def to_window(x):
        return jnp.transpose(x, (1, 0, 2)).reshape(frames, rows_dev + 2 * HALO, columns, ZC)

    def stages(state):
        def first(st):
            st["first"] = causal_conv(st["window"], st["x_history"], conv_in, ZC)

        def activate(st):
            activated = jax.nn.silu(rms_scale(st["first"])).astype(jnp.bfloat16)
            st["activated"] = jnp.where(inside[None, :, None, None], activated, jnp.zeros_like(activated))

        def second(st):
            st["second"] = causal_conv(st["activated"], st["a_history"], conv_mid, channels)

        def finish(st):
            summed = st["first"][:, 1 : 1 + rows_dev] + st["second"]
            normed = rms_scale(summed).astype(jnp.bfloat16)
            projected = jnp.dot(normed.reshape(-1, channels), to_pixels, preferred_element_type=jnp.float32)
            projected = projected.reshape(frames, rows_dev, columns, 2, 2, 3).transpose(0, 1, 3, 2, 4, 5)
            st["pixels"] = projected.reshape(frames, 2 * rows_dev, 6 * columns).astype(jnp.bfloat16)

        return [first, activate, second, finish]

    x_history = jnp.zeros((2, rows_dev + 2 * HALO, columns, ZC), jnp.bfloat16)
    a_history = jnp.zeros((2, rows_dev + 2, columns, channels), jnp.bfloat16)
    window = to_window(gather_rows(prepare(0), n, rows_dev, slot))
    results = []
    for group in range(groups):
        state = {"window": window, "x_history": x_history, "a_history": a_history}
        steps = stages(state)
        if group + 1 < groups:
            def hook_for(run):
                def hook(x):
                    run(state)
                    keys = sorted(state)
                    x, values = lax.optimization_barrier((x, [state[k] for k in keys]))
                    state.update(zip(keys, values))
                    return x

                return hook

            nxt = prepare(group + 1)
            nxt, window = lax.optimization_barrier((nxt, window))
            state["window"] = window
            hooks = [hook_for(run) for run in steps[: bits - 1]]
            nxt = gather_rows(nxt, n, rows_dev, slot, hooks)
            for run in steps[bits - 1 :]:
                run(state)
            next_window = to_window(nxt)
        else:
            for run in steps:
                run(state)
        results.append(state["pixels"])
        x_history = jnp.concatenate([x_history, state["window"]], axis=0)[-2:]
        a_history = jnp.concatenate([a_history, state["activated"]], axis=0)[-2:]
        if group + 1 < groups:
            window = next_window
    pixels = jnp.stack(results, axis=0)
    return lax.ppermute(pixels, "dev", [(i, reverse_bits(i, bits)) for i in range(n)])


def solution(mesh):
    in_specs = (P(("stream", "dev"), None, None, None, None), P("stream"), P(), P(), P())
    out_specs = P("stream", None, "dev", None)
    return jax.shard_map(local, mesh=mesh, in_specs=in_specs, out_specs=out_specs, check_vma=False)
```

time: 59.5 us -> 83.7 us (1.41); the launches traced: 59.3 us -> 82.4 us
  local copies, waits for them, and re-layouts: 15 us -> 23.3 us
  matrix products: 10.7 us -> 18.4 us
  starting transfers between devices: 4.46 us -> 7.6 us
  waiting for transfers between devices: 24.9 us -> 27 us
  between operations: 0.3 us -> 1.82 us
    conv_general_dilated x2 -> x4, matrix products: 10.3 us -> 17.8 us  [causal_conv(): lax.conv_general_dilated(padded[None], kernel, window_strides=(1, 1, 1),...]
    conv_general_dilated x9 -> x20, local copies, waits for them, and re-layouts: 8.41 us -> 12.5 us  [causal_conv(): lax.conv_general_dilated(padded[None], kernel, window_strides=(1, 1, 1),...]
    ppermute x4 -> x8, waiting for transfers between devices: 19.1 us -> 22.6 us  [gather_rows(): x = own + lax.ppermute(send, 'dev', pairs)]
    squeeze x1 -> x2, local copies, waits for them, and re-layouts: 0.19 us -> 2.69 us  [causal_conv(): return out[0]]
    slice x0 -> x6, local copies, waits for them, and re-layouts: none -> 2.01 us  [the longest x1 1.36 us: prepare(): x = jnp.where(owners[group] == position, x, jnp.zeros_like(x))]
    ppermute x4 -> x8, starting transfers between devices: 2.54 us -> 4.31 us  [gather_rows(): x = own + lax.ppermute(send, 'dev', pairs)]
    ppermute x1, starting transfers between devices: 1.92 us -> 3.29 us  [local(): lax.ppermute(pixels, 'dev', [(i, reverse_bits(i, bits)) for i in range(n)])]
    ppermute x1, waiting for transfers between devices: 5.82 us -> 4.45 us  [local(): lax.ppermute(pixels, 'dev', [(i, reverse_bits(i, bits)) for i in range(n)])]
  transfers between devices with their start and end apart: 5 -> 9, of which waited for: 5 -> 7; matrix products, arithmetic and copies ran while one was open for 0% -> 13% of each run, Pallas kernels for 0% -> 0%
where the time goes in v3:
time: 83.7 us; the launch traced here: 82.4 us
  waiting for transfers between devices  27 us (32%)
  local copies, waits for them, and re-layouts  23.3 us (28%)
  matrix products  18.4 us (22%)
  starting transfers between devices  7.6 us (9%)
  other arithmetic  4.31 us (5%)
  between operations  1.82 us (2%)
    ppermute x8, waiting for transfers between devices, gather_rows(): x = own + lax.ppermute(send, 'dev', pairs)  22.6 us
    conv_general_dilated x4, matrix products, causal_conv(): lax.conv_general_dilated(padded[None], kernel, window_strides=(1, 1, 1),...  17.8 us
    conv_general_dilated x20, local copies, waits for them, and re-layouts, causal_conv(): lax.conv_general_dilated(padded[None], kernel, window_strides=(1, 1, 1),...  12.5 us
    ppermute x1, waiting for transfers between devices, local(): lax.ppermute(pixels, 'dev', [(i, reverse_bits(i, bits)) for i in range(n)])  4.45 us
    ppermute x8, starting transfers between devices, gather_rows(): x = own + lax.ppermute(send, 'dev', pairs)  4.31 us
    ppermute x1, starting transfers between devices, local(): lax.ppermute(pixels, 'dev', [(i, reverse_bits(i, bits)) for i in range(n)])  3.29 us
    squeeze x2, local copies, waits for them, and re-layouts, causal_conv(): return out[0]  2.69 us
    unnamed x14, local copies, waits for them, and re-layouts  1.92 us
  transfers between devices with their start and end apart: 9, of which 7 were waited for; matrix products, arithmetic and copies ran while one was open for 13% of the time, Pallas kernels for 0%

profile of v3, /device:TPU:24, one launch (start us, length us, event | category | flops | bytes accessed | tf_op | source)
XLA Modules:
  0.0 82.4 jit_solution(12809402786541723377)
XLA Ops:
  0.0 1.4 %fusion.74 = (s32[1]{0:T(128)}, s32[1]{0:T(128)}) fusion(s32[2]{0:T(128)} %param.6), kind=kLoop, calls=%fused_computation.114 | loop fusion | bytes 16 | tf_op jit(solution)/shard_map/slice | solution.py:68
  2.6 1.0 %select_bitcast_fusion = (bf16[16,3,1664]{2,0,1:T(8,128)(2,1)S(1)}, bf16[16,3,1664]{2,0,1:T(8,128)(2,1)S(1)}) fusion(bf16[1,2,3,16,1664]{4,3,2,1,0:T(8,128)(2,1)} %param.5, pred[]{:T(512)S(6)} %eq.7, pred[]{:T(512)S(6)} %eq.6), kind=kLoop, calls=%fused_computation.79 | loop fusion | flops 159744 | bytes 638978 | tf_op jit(solution)/shard_map/jit(_where)/select_n | solution.py:68
  3.8 1.4 %collective-permute-done = bf16[12,3,1664]{2,0,1:T(8,128)(2,1)S(1)} collective-permute-done((bf16[12,3,1664]{2,0,1:T(8,128)(2,1)S(1)}, bf16[12,3,1664]{2,0,1:T(8,128)(2,1)S(1)}, u32[]{:S(2)}, u32[]{:S(2)}) %collective-permute-start) | collective-permute-done | bytes 119840 | tf_op jit(solution)/shard_map/ppermute | solution.py:32
  5.4 1.6 %collective-permute-start.1 = (bf16[8,3,1664]{2,0,1:T(8,128)(2,1)S(1)}, bf16[8,3,1664]{2,0,1:T(8,128)(2,1)S(1)}, u32[]{:S(2)}, u32[]{:S(2)}) collective-permute-start(bf16[8,3,1664]{2,0,1:T(8,128)(2,1)S(1)} %constant_dynamic-slice_fusion.6), channel_id=1, source_target_pairs={{0,2},{1,3},{2,0},{3,1},{4,6},{5,7},{6,4},{7,5},{8,10},{9,11},{10,... | collective-permute-start | bytes 239624 | tf_op jit(solution)/shard_map/ppermute | solution.py:32
  6.9 3.0 %collective-permute-done.1 = bf16[8,3,1664]{2,0,1:T(8,128)(2,1)S(1)} collective-permute-done((bf16[8,3,1664]{2,0,1:T(8,128)(2,1)S(1)}, bf16[8,3,1664]{2,0,1:T(8,128)(2,1)S(1)}, u32[]{:S(2)}, u32[]{:S(2)}) %collective-permute-start.1) | collective-permute-done | bytes 79904 | tf_op jit(solution)/shard_map/ppermute | solution.py:32
  10.5 4.0 %collective-permute-done.2 = bf16[6,3,1664]{2,0,1:T(8,128)(2,1)S(1)} collective-permute-done((bf16[6,3,1664]{2,0,1:T(8,128)(2,1)S(1)}, bf16[6,3,1664]{2,0,1:T(8,128)(2,1)S(1)}, u32[]{:S(2)}, u32[]{:S(2)}) %collective-permute-start.2) | collective-permute-done | bytes 59936 | tf_op jit(solution)/shard_map/ppermute | solution.py:32
  15.0 5.6 %collective-permute-done.3 = bf16[5,3,1664]{2,0,1:T(8,128)(2,1)S(1)} collective-permute-done((bf16[5,3,1664]{2,0,1:T(8,128)(2,1)S(1)}, bf16[5,3,1664]{2,0,1:T(8,128)(2,1)S(1)}, u32[]{:S(2)}, u32[]{:S(2)}) %collective-permute-start.3) | collective-permute-done | bytes 49952 | tf_op jit(solution)/shard_map/ppermute | solution.py:32
  22.7 1.8 %convolution_select_fusion.1 = f32[3,3,8,14,384]{4,2,3,1,0:T(8,128)S(1)} fusion(bf16[3,3,3,16,384]{4,3,2,1,0:T(8,128)(2,1)S(1)} %bitcast.113, bf16[5,5,1,7,2,16]{5,3,4,1,0,2:T(8,128)(2,1)S(1)} %slice.40, bf16[5,5,1,8,14,16]{5,3,4,1,0,2:T(8,128)(2,1)S(1)} %copy.29, pred[8,14]{0,1:T(8,128)(4,1)S(1)} %copy-done.5), kind=kOutput, calls=%fused_computation.28 | convolution fusion | flops 335124480 | bytes 1980976 | tf_op jit(solution)/shard_map/conv_general_dilated | solution.py:42
  24.8 1.3 %reshape.125 = f32[3,3,1,112,384]{4,3,1,0,2:T(8,128)} reshape(f32[3,3,8,14,384]{4,3,2,1,0:T(8,128)S(1)} %copy.30) | data formatting | bytes 3096576 | tf_op jit(solution)/shard_map/conv_general_dilated | solution.py:42
  26.3 1.5 %slice_bitcast_fusion.1 = f32[3,3,104,384]{3,2,1,0:T(8,128)S(1)} fusion(f32[3,3,1,112,384]{4,3,1,0,2:T(8,128)} %reshape.125), kind=kLoop, calls=%fused_computation.22 | loop fusion | bytes 2875392 | tf_op jit(solution)/shard_map/squeeze | solution.py:50
  28.1 1.6 %collective-permute-start.5 = (bf16[8,3,1664]{2,0,1:T(8,128)(2,1)S(1)}, bf16[8,3,1664]{2,0,1:T(8,128)(2,1)S(1)}, u32[]{:S(2)}, u32[]{:S(2)}) collective-permute-start(bf16[8,3,1664]{2,0,1:T(8,128)(2,1)S(1)} %constant_dynamic-slice_fusion.2), channel_id=1, source_target_pairs={{0,2},{1,3},{2,0},{3,1},{4,6},{5,7},{6,4},{7,5},{8,10},{9,11},{10,... | collective-permute-start | bytes 239624 | tf_op jit(solution)/shard_map/ppermute | solution.py:32
  30.2 2.8 %collective-permute-done.5 = bf16[8,3,1664]{2,0,1:T(8,128)(2,1)S(1)} collective-permute-done((bf16[8,3,1664]{2,0,1:T(8,128)(2,1)S(1)}, bf16[8,3,1664]{2,0,1:T(8,128)(2,1)S(1)}, u32[]{:S(2)}, u32[]{:S(2)}) %collective-permute-start.5) | collective-permute-done | bytes 79904 | tf_op jit(solution)/shard_map/ppermute | solution.py:32
  33.6 1.2 %pad.30 = bf16[5,3,1,112,384]{4,3,1,0,2:T(8,128)(2,1)} pad(bf16[5,3,1,106,384]{4,3,1,0,2:T(8,128)(2,1)S(1)} %fusion.23, bf16[]{:T(256)} %constant.19.clone.1), padding=0_0x0_0x0_0x0_6x0_0 | pad | bytes 2511362 | tf_op jit(solution)/shard_map/broadcast_in_dim | solution.py:43
  34.8 2.2 %reshape.128 = bf16[5,3,1,8,14,384]{5,4,3,1,0,2:T(8,128)(2,1)S(1)} reshape(bf16[5,3,1,112,384]{4,3,1,0,2:T(8,128)(2,1)} %pad.30) | data formatting | bytes 2580480 | tf_op jit(solution)/shard_map/conv_general_dilated | solution.py:42
  37.5 7.1 %fusion.27 = f32[3,1,8,14,384]{4,2,3,1,0:T(8,128)S(1)} fusion(bf16[3,3,3,384,384]{4,3,2,1,0:T(8,128)(2,1)} %bitcast.120, bf16[5,3,1,7,2,384]{5,3,4,1,0,2:T(8,128)(2,1)S(1)} %slice.42, bf16[5,3,1,8,14,384]{5,3,4,1,0,2:T(8,128)(2,1)S(1)} %copy.32, pred[8,14]{0,1:T(8,128)(4,1)S(1)} %copy-done.5), kind=kOutput, calls=%fused_computation.36 | convolution fusion | flops 2679994368 | bytes 9930352 | tf_op jit(solution)/shard_map/conv_general_dilated | solution.py:42
  46.9 5.8 %collective-permute-done.7 = bf16[5,3,1664]{2,0,1:T(8,128)(2,1)S(1)} collective-permute-done((bf16[5,3,1664]{2,0,1:T(8,128)(2,1)S(1)}, bf16[5,3,1664]{2,0,1:T(8,128)(2,1)S(1)}, u32[]{:S(2)}, u32[]{:S(2)}) %collective-permute-start.7) | collective-permute-done | bytes 49952 | tf_op jit(solution)/shard_map/ppermute | solution.py:32
  54.0 1.4 %copy.40 = bf16[5,5,1,8,14,16]{5,3,4,1,0,2:T(8,128)(2,1)S(1)} copy(bf16[5,5,1,8,14,16]{4,3,5,1,0,2:T(8,128)(2,1)S(1)} %reshape.135) | data formatting | bytes 179200 | tf_op jit(solution)/shard_map/conv_general_dilated | solution.py:42
  55.5 1.8 %convolution_select_fusion = f32[3,3,8,14,384]{4,2,3,1,0:T(8,128)S(1)} fusion(bf16[3,3,3,16,384]{4,3,2,1,0:T(8,128)(2,1)S(1)} %bitcast.114, bf16[5,5,1,7,2,16]{5,3,4,1,0,2:T(8,128)(2,1)S(1)} %slice.44, bf16[5,5,1,8,14,16]{5,3,4,1,0,2:T(8,128)(2,1)S(1)} %copy.40, pred[8,14]{0,1:T(8,128)(4,1)S(1)} %copy-done.5), kind=kOutput, calls=%fused_computation.27 | convolution fusion | flops 335124480 | bytes 1980976 | tf_op jit(solution)/shard_map/conv_general_dilated | solution.py:42
  57.3 1.6 %copy.41 = f32[3,3,8,14,384]{4,3,2,1,0:T(8,128)} copy(f32[3,3,8,14,384]{4,2,3,1,0:T(8,128)S(1)} %convolution_select_fusion) | data formatting | bytes 3096576 | tf_op jit(solution)/shard_map/conv_general_dilated | solution.py:42
  58.9 1.5 %reshape.139 = f32[3,3,1,112,384]{4,3,1,0,2:T(8,128)S(1)} reshape(f32[3,3,8,14,384]{4,3,2,1,0:T(8,128)} %copy.41) | data formatting | bytes 3096576 | tf_op jit(solution)/shard_map/conv_general_dilated | solution.py:42
  60.6 1.2 %slice_bitcast_fusion = f32[3,3,104,384]{3,2,1,0:T(8,128)} fusion(f32[3,3,1,112,384]{4,3,1,0,2:T(8,128)S(1)} %reshape.139), kind=kLoop, calls=%fused_computation.21 | loop fusion | bytes 2875392 | tf_op jit(solution)/shard_map/squeeze | solution.py:50
  64.5 7.1 %fusion.24 = f32[3,1,8,14,384]{4,2,3,1,0:T(8,128)S(1)} fusion(bf16[3,3,3,384,384]{4,3,2,1,0:T(8,128)(2,1)} %bitcast.121, bf16[5,3,1,7,2,384]{5,3,4,1,0,2:T(8,128)(2,1)S(1)} %slice.47, bf16[5,3,1,8,14,384]{5,3,4,1,0,2:T(8,128)(2,1)S(1)} %copy.43, pred[8,14]{0,1:T(8,128)(4,1)S(1)} %copy-done.5), kind=kOutput, calls=%fused_computation.35 | convolution fusion | flops 2679994368 | bytes 9930352 | tf_op jit(solution)/shard_map/conv_general_dilated | solution.py:42
  74.1 3.3 %collective-permute-start.8 = (bf16[2,3,2,624]{3,2,1,0:T(2,128)(2,1)S(1)}, bf16[2,3,2,624]{3,2,1,0:T(2,128)(2,1)S(1)}, u32[]{:S(2)}, u32[]{:S(2)}) collective-permute-start(bf16[2,3,2,624]{3,2,1,0:T(2,128)(2,1)S(1)} %pad_maximum_fusion), channel_id=1, source_target_pairs={{0,0},{1,8},{2,4},{3,12},{4,2},{5,10},{6,6},{7,14},{8,1},{9,9},{10... | collective-permute-start | bytes 44936 | tf_op jit(solution)/shard_map/ppermute | solution.py:129
  77.4 4.4 %collective-permute-done.8 = bf16[2,3,2,624]{3,2,1,0:T(2,128)(2,1)S(1)} collective-permute-done((bf16[2,3,2,624]{3,2,1,0:T(2,128)(2,1)S(1)}, bf16[2,3,2,624]{3,2,1,0:T(2,128)(2,1)S(1)}, u32[]{:S(2)}, u32[]{:S(2)}) %collective-permute-start.8) | collective-permute-done | bytes 15008 | tf_op jit(solution)/shard_map/ppermute | solution.py:129
  (90 shorter events, 15.0 us)
Async XLA Ops:
  0.0 22.4 %copy-start = (bf16[432,384]{1,0:T(8,128)(2,1)S(1)}, bf16[432,384]{1,0:T(8,128)(2,1)}, u32[]{:S(2)}) copy-start(bf16[432,384]{1,0:T(8,128)(2,1)} %param.7) | copy-start | bytes 995332
  0.0 14.9 %copy-start.4 = (bf16[384,12]{0,1:T(8,128)(2,1)S(1)}, bf16[384,12]{0,1:T(8,128)(2,1)}, u32[]{:S(2)}) copy-start(bf16[384,12]{0,1:T(8,128)(2,1)} %param.9) | copy-start | bytes 27652
  3.8 1.5 %collective-permute-start = (bf16[12,3,1664]{2,0,1:T(8,128)(2,1)S(1)}, bf16[12,3,1664]{2,0,1:T(8,128)(2,1)S(1)}, u32[]{:S(2)}, u32[]{:S(2)}) collective-permute-start(bf16[12,3,1664]{2,0,1:T(8,128)(2,1)S(1)} %pad_dynamic-slice_fusion), channel_id=1, source_target_pairs={{0,1},{1,0},{2,3},{3,2},{4,5},{5,4},{6,7},{7,6},{8,9},{9,8},{10,11... | collective-permute-start | bytes 359432 | tf_op jit(solution)/shard_map/ppermute | solution.py:32
  5.4 4.5 %collective-permute-start.1 = (bf16[8,3,1664]{2,0,1:T(8,128)(2,1)S(1)}, bf16[8,3,1664]{2,0,1:T(8,128)(2,1)S(1)}, u32[]{:S(2)}, u32[]{:S(2)}) collective-permute-start(bf16[8,3,1664]{2,0,1:T(8,128)(2,1)S(1)} %constant_dynamic-slice_fusion.6), channel_id=1, source_target_pairs={{0,2},{1,3},{2,0},{3,1},{4,6},{5,7},{6,4},{7,5},{8,10},{9,11},{10,... | collective-permute-start | bytes 239624 | tf_op jit(solution)/shard_map/ppermute | solution.py:32
  10.0 4.5 %collective-permute-start.2 = (bf16[6,3,1664]{2,0,1:T(8,128)(2,1)S(1)}, bf16[6,3,1664]{2,0,1:T(8,128)(2,1)S(1)}, u32[]{:S(2)}, u32[]{:S(2)}) collective-permute-start(bf16[6,3,1664]{2,0,1:T(8,128)(2,1)S(1)} %constant_dynamic-slice_fusion.5), channel_id=1, source_target_pairs={{0,4},{1,5},{2,6},{3,7},{4,0},{5,1},{6,2},{7,3},{8,12},{9,13},{10,... | collective-permute-start | bytes 179720 | tf_op jit(solution)/shard_map/ppermute | solution.py:32
  14.5 6.1 %collective-permute-start.3 = (bf16[5,3,1664]{2,0,1:T(8,128)(2,1)S(1)}, bf16[5,3,1664]{2,0,1:T(8,128)(2,1)S(1)}, u32[]{:S(2)}, u32[]{:S(2)}) collective-permute-start(bf16[5,3,1664]{2,0,1:T(8,128)(2,1)S(1)} %constant_dynamic-slice_fusion.4), channel_id=1, source_target_pairs={{0,8},{1,9},{2,10},{3,11},{4,12},{5,13},{6,14},{7,15},{8,0},{9,1},... | collective-permute-start | bytes 149768 | tf_op jit(solution)/shard_map/ppermute | solution.py:32
  21.0 0.8 copy-start.3
  22.0 0.7 copy-start.5
  26.2 1.5 %collective-permute-start.4 = (bf16[12,3,1664]{2,0,1:T(8,128)(2,1)S(1)}, bf16[12,3,1664]{2,0,1:T(8,128)(2,1)S(1)}, u32[]{:S(2)}, u32[]{:S(2)}) collective-permute-start(bf16[12,3,1664]{2,0,1:T(8,128)(2,1)S(1)} %constant_dynamic-slice_fusion.3), channel_id=1, source_target_pairs={{0,1},{1,0},{2,3},{3,2},{4,5},{5,4},{6,7},{7,6},{8,9},{9,8},{10,11... | collective-permute-start | bytes 359432 | tf_op jit(solution)/shard_map/ppermute | solution.py:32
  28.1 4.9 %collective-permute-start.5 = (bf16[8,3,1664]{2,0,1:T(8,128)(2,1)S(1)}, bf16[8,3,1664]{2,0,1:T(8,128)(2,1)S(1)}, u32[]{:S(2)}, u32[]{:S(2)}) collective-permute-start(bf16[8,3,1664]{2,0,1:T(8,128)(2,1)S(1)} %constant_dynamic-slice_fusion.2), channel_id=1, source_target_pairs={{0,2},{1,3},{2,0},{3,1},{4,6},{5,7},{6,4},{7,5},{8,10},{9,11},{10,... | collective-permute-start | bytes 239624 | tf_op jit(solution)/shard_map/ppermute | solution.py:32
  30.2 3.4 %copy-start.1 = (bf16[3,3,104,384]{3,2,1,0:T(8,128)(2,1)}, bf16[3,3,104,384]{3,2,1,0:T(8,128)(2,1)S(1)}, u32[]{:S(2)}) copy-start(bf16[3,3,104,384]{3,2,1,0:T(8,128)(2,1)S(1)} %fusion.46) | copy-start | bytes 2156548
  37.4 8.1 %collective-permute-start.6 = (bf16[6,3,1664]{2,0,1:T(8,128)(2,1)S(1)}, bf16[6,3,1664]{2,0,1:T(8,128)(2,1)S(1)}, u32[]{:S(2)}, u32[]{:S(2)}) collective-permute-start(bf16[6,3,1664]{2,0,1:T(8,128)(2,1)S(1)} %constant_dynamic-slice_fusion.1), channel_id=1, source_target_pairs={{0,4},{1,5},{2,6},{3,7},{4,0},{5,1},{6,2},{7,3},{8,12},{9,13},{10,... | collective-permute-start | bytes 179720 | tf_op jit(solution)/shard_map/ppermute | solution.py:32
  45.5 1.2 %slice-start.1 = ((bf16[3,5,104,16]{3,2,0,1:T(8,128)(2,1)}), bf16[2,5,104,16]{3,2,0,1:T(8,128)(2,1)S(1)}, s32[]{:S(2)}) async-start(bf16[3,5,104,16]{3,2,0,1:T(8,128)(2,1)} %copy-done.3), calls=%async_computation.1 | async-start | bytes 532480 | tf_op jit(solution)/shard_map/slice | solution.py:124
  45.8 7.0 %collective-permute-start.7 = (bf16[5,3,1664]{2,0,1:T(8,128)(2,1)S(1)}, bf16[5,3,1664]{2,0,1:T(8,128)(2,1)S(1)}, u32[]{:S(2)}, u32[]{:S(2)}) collective-permute-start(bf16[5,3,1664]{2,0,1:T(8,128)(2,1)S(1)} %constant_dynamic-slice_fusion), channel_id=1, source_target_pairs={{0,8},{1,9},{2,10},{3,11},{4,12},{5,13},{6,14},{7,15},{8,0},{9,1},... | collective-permute-start | bytes 149768 | tf_op jit(solution)/shard_map/ppermute | solution.py:32
  61.9 1.0 %slice-start = ((bf16[3,3,104,384]{3,2,1,0:T(8,128)(2,1)}), bf16[2,3,104,384]{3,2,1,0:T(8,128)(2,1)S(1)}, s32[]{:S(2)}) async-start(bf16[3,3,104,384]{3,2,1,0:T(8,128)(2,1)} %copy-done.1), calls=%async_computation | async-start | bytes 958464 | tf_op jit(solution)/shard_map/slice | solution.py:125
  71.6 1.4 %copy-start.2 = (f32[3,3,104,384]{3,2,1,0:T(8,128)S(1)}, f32[3,3,104,384]{3,2,1,0:T(8,128)}, u32[]{:S(2)}) copy-start(f32[3,3,104,384]{3,2,1,0:T(8,128)} %slice_bitcast_fusion) | copy-start | bytes 4313092
  74.1 7.7 %collective-permute-start.8 = (bf16[2,3,2,624]{3,2,1,0:T(2,128)(2,1)S(1)}, bf16[2,3,2,624]{3,2,1,0:T(2,128)(2,1)S(1)}, u32[]{:S(2)}, u32[]{:S(2)}) collective-permute-start(bf16[2,3,2,624]{3,2,1,0:T(2,128)(2,1)S(1)} %pad_maximum_fusion), channel_id=1, source_target_pairs={{0,0},{1,8},{2,4},{3,12},{4,2},{5,10},{6,6},{7,14},{8,1},{9,9},{10... | collective-permute-start | bytes 44936 | tf_op jit(solution)/shard_map/ppermute | solution.py:129

commit v4 on v2

--- a/solution.py
+++ b/solution.py
@@ -65,7 +65,18 @@
     x = gather_rows(x, n, rows_dev, slot)
 
     window = jnp.transpose(x, (1, 2, 0, 3)).reshape(groups * frames, rows_dev + 2 * HALO, columns, ZC)
-    first_act = causal_conv(window, conv_in, ZC)
+    steps = groups * frames
+    rows_in = rows_dev + 2
+    padded = jnp.pad(window, ((2, 0), (0, 0), (1, 1), (0, 0)))
+    pieces = [
+        padded[a : a + steps, b : b + rows_in, e : e + columns]
+        for a in range(3)
+        for b in range(3)
+        for e in range(3)
+    ]
+    xcol = jnp.concatenate(pieces, axis=-1).reshape(-1, 27 * ZC)
+    first_act = jnp.dot(xcol, conv_in, preferred_element_type=jnp.float32)
+    first_act = first_act.reshape(steps, rows_in, columns, channels)
     activated = jax.nn.silu(rms_scale(first_act)).astype(jnp.bfloat16)
     row_of = slot * rows_dev - 1 + jnp.arange(rows_dev + 2)
     inside = (row_of >= 0) & (row_of < height)

time: 59.5 us -> 69.7 us (1.17); the launches traced: 59.3 us -> 68.5 us
  local copies, waits for them, and re-layouts: 15 us -> 26.3 us
  matrix products: 10.7 us -> 9 us
    concatenate x0 -> x1, local copies, waits for them, and re-layouts: none -> 11.7 us  [local(): xcol = jnp.concatenate(pieces, axis=-1).reshape(-1, 27 * ZC)]
    slice x0 -> x2, local copies, waits for them, and re-layouts: none -> 6.4 us  [local(): padded[a:a + steps, b:b + rows_in, e:e + columns]]
    conv_general_dilated x9 -> x4, local copies, waits for them, and re-layouts: 8.41 us -> 2.47 us  [causal_conv(): lax.conv_general_dilated(padded[None], kernel, window_strides=(1, 1, 1),...]
    conv_general_dilated x2 -> x1, matrix products: 10.3 us -> 7.41 us  [causal_conv(): lax.conv_general_dilated(padded[None], kernel, window_strides=(1, 1, 1),...]
    dot_general x0 -> x1, matrix products: none -> 1.27 us  [local(): first_act = jnp.dot(xcol, conv_in, preferred_element_type=jnp.float32)]
where the time goes in v4:
time: 69.7 us; the launch traced here: 68.5 us
  local copies, waits for them, and re-layouts  26.3 us (38%)
  waiting for transfers between devices  24.9 us (36%)
  matrix products  9 us (13%)
  starting transfers between devices  4.46 us (6%)
  other arithmetic  3.6 us (5%)
    ppermute x4, waiting for transfers between devices, gather_rows(): x = own + lax.ppermute(send, 'dev', pairs)  19.1 us
    concatenate x1, local copies, waits for them, and re-layouts, local(): xcol = jnp.concatenate(pieces, axis=-1).reshape(-1, 27 * ZC)  11.7 us
    conv_general_dilated x1, matrix products, causal_conv(): lax.conv_general_dilated(padded[None], kernel, window_strides=(1, 1, 1),...  7.41 us
    slice x2, local copies, waits for them, and re-layouts, local(): padded[a:a + steps, b:b + rows_in, e:e + columns]  6.4 us
    ppermute x1, waiting for transfers between devices, local(): lax.ppermute(pixels, 'dev', [(i, reverse_bits(i, bits)) for i in range(n)])  5.82 us
    unnamed x12, local copies, waits for them, and re-layouts  2.85 us
    ppermute x4, starting transfers between devices, gather_rows(): x = own + lax.ppermute(send, 'dev', pairs)  2.54 us
    conv_general_dilated x4, local copies, waits for them, and re-layouts, causal_conv(): lax.conv_general_dilated(padded[None], kernel, window_strides=(1, 1, 1),...  2.47 us
  transfers between devices with their start and end apart: 5, of which 5 were waited for; matrix products, arithmetic and copies ran while one was open for 0% of the time, Pallas kernels for 0%

profile of v4, /device:TPU:24, one launch (start us, length us, event | category | flops | bytes accessed | tf_op | source)
XLA Modules:
  0.0 68.5 jit_solution(12485813162846382028)
XLA Ops:
  0.0 0.7 %broadcast_compare_fusion = pred[2]{0:T(512)(128)(4,1)S(1)} fusion(s32[2]{0:T(128)} %param.6, s32[]{:T(128)S(6)} %axis_index.12), kind=kLoop, calls=%fused_computation.61 | loop fusion | flops 2 | bytes 14 | tf_op jit(solution)/shard_map/eq | solution.py:62
  0.7 1.1 %fusion.17 = bf16[16,2,3,1664]{3,0,2,1:T(8,128)(2,1)S(1)} fusion(bf16[1,2,3,16,1664]{4,3,2,1,0:T(8,128)(2,1)} %param.5, pred[2]{0:T(512)(128)(4,1)S(1)} %broadcast_compare_fusion), kind=kLoop, calls=%fused_computation.50 | loop fusion | flops 159744 | bytes 638978 | tf_op jit(solution)/shard_map/jit(_where)/select_n | solution.py:63
  2.0 1.6 %collective-permute-done = bf16[12,2,3,1664]{3,0,2,1:T(8,128)(2,1)S(1)} collective-permute-done((bf16[12,2,3,1664]{3,0,2,1:T(8,128)(2,1)S(1)}, bf16[12,2,3,1664]{3,0,2,1:T(8,128)(2,1)S(1)}, u32[]{:S(2)}, u32[]{:S(2)}) %collective-permute-start) | collective-permute-done | bytes 239648 | tf_op jit(solution)/shard_map/ppermute | solution.py:32
  3.9 1.6 %collective-permute-start.1 = (bf16[8,2,3,1664]{3,0,2,1:T(8,128)(2,1)S(1)}, bf16[8,2,3,1664]{3,0,2,1:T(8,128)(2,1)S(1)}, u32[]{:S(2)}, u32[]{:S(2)}) collective-permute-start(bf16[8,2,3,1664]{3,0,2,1:T(8,128)(2,1)S(1)} %constant_dynamic-slice_fusion.2), channel_id=1, source_target_pairs={{0,2},{1,3},{2,0},{3,1},{4,6},{5,7},{6,4},{7,5},{8,10},{9,11},{10,... | collective-permute-start | bytes 479240 | tf_op jit(solution)/shard_map/ppermute | solution.py:32
  5.4 4.7 %collective-permute-done.1 = bf16[8,2,3,1664]{3,0,2,1:T(8,128)(2,1)S(1)} collective-permute-done((bf16[8,2,3,1664]{3,0,2,1:T(8,128)(2,1)S(1)}, bf16[8,2,3,1664]{3,0,2,1:T(8,128)(2,1)S(1)}, u32[]{:S(2)}, u32[]{:S(2)}) %collective-permute-start.1) | collective-permute-done | bytes 159776 | tf_op jit(solution)/shard_map/ppermute | solution.py:32
  10.2 0.5 collective-permute-start.2
  10.8 4.8 %collective-permute-done.2 = bf16[6,2,3,1664]{3,0,2,1:T(8,128)(2,1)S(1)} collective-permute-done((bf16[6,2,3,1664]{3,0,2,1:T(8,128)(2,1)S(1)}, bf16[6,2,3,1664]{3,0,2,1:T(8,128)(2,1)S(1)}, u32[]{:S(2)}, u32[]{:S(2)}) %collective-permute-start.2) | collective-permute-done | bytes 119840 | tf_op jit(solution)/shard_map/ppermute | solution.py:32
  16.1 8.0 %collective-permute-done.3 = bf16[5,2,3,1664]{3,0,2,1:T(8,128)(2,1)S(1)} collective-permute-done((bf16[5,2,3,1664]{3,0,2,1:T(8,128)(2,1)S(1)}, bf16[5,2,3,1664]{3,0,2,1:T(8,128)(2,1)S(1)}, u32[]{:S(2)}, u32[]{:S(2)}) %collective-permute-start.3) | collective-permute-done | bytes 99872 | tf_op jit(solution)/shard_map/ppermute | solution.py:32
  24.2 0.6 reshape.73
  24.8 4.3 %pad_slice_fusion = (bf16[6,3,104,16]{3,2,1,0:T(8,128)(2,1)S(1)}, bf16[6,3,104,16]{3,2,1,0:T(8,128)(2,1)S(1)}, bf16[6,3,104,16]{3,2,1,0:T(8,128)(2,1)}, bf16[6,3...) fusion(bf16[6,5,104,16]{3,2,1,0:T(8,128)(2,1)S(1)} %reshape.73), kind=kLoop, calls=%fused_computation.11 | loop fusion | bytes 1238016 | tf_op jit(solution)/shard_map/slice | solution.py:72
  29.1 2.1 %fusion.22 = (bf16[6,3,104,16]{3,2,1,0:T(8,128)(2,1)}, bf16[6,3,104,16]{3,2,1,0:T(8,128)(2,1)}, bf16[6,3,104,16]{3,2,1,0:T(8,128)(2,1)}, bf16[6,3,104,16]{3,2,1,...) fusion(bf16[6,5,104,16]{3,2,1,0:T(8,128)(2,1)S(1)} %reshape.73), kind=kLoop, calls=%fused_computation.65 | loop fusion | bytes 2715648 | tf_op jit(solution)/shard_map/slice | solution.py:72
  31.2 11.7 %concatenate.3 = bf16[6,3,104,432]{3,2,1,0:T(8,128)(2,1)S(1)} concatenate(bf16[6,3,104,16]{3,2,1,0:T(8,128)(2,1)} %get-tuple-element.31, bf16[6,3,104,16]{3,2,1,0:T(8,128)(2,1)S(1)} %get-tuple-element.6, bf16[6,3,104,16]{3,2,1,0:T(8,128)(2,1)} %get-tuple-element.7, bf16[6,3,104,16]{3,2,1,0:T(8,128)(2,1)} %get-tuple-element.8, bf16[6,3,104,16]{3,2,1,0:T(8,128)(2,1)} %get-tuple-element.9, ...), dimensions={3} | concatenate | bytes 3234816 | tf_op jit(solution)/shard_map/concatenate | solution.py:77
  42.9 1.3 %multiply_reduce_fusion = (f32[6,3,104]{2,1,0:T(4,128)S(1)}, f32[6,3,104,384]{3,2,1,0:T(8,128)S(1)}) fusion(bf16[6,3,104,432]{3,2,1,0:T(8,128)(2,1)S(1)} %concatenate.3, bf16[432,384]{1,0:T(8,128)(2,1)S(1)} %copy-done), kind=kOutput, calls=%fused_computation.3 | convolution fusion | flops 622520512 | bytes 4832064 | tf_op jit(solution)/shard_map/dot_general | solution.py:78
  44.2 0.9 %fusion.8 = bf16[6,3,104,384]{3,2,1,0:T(8,128)(2,1)S(1)} fusion(f32[6,3,104,384]{3,2,1,0:T(8,128)S(1)} %get-tuple-element.33, f32[6,3,104]{2,1,0:T(4,128)S(1)} %add_rsqrt_fusion, pred[3]{0:T(512)(128)(4,1)S(1)} %compare_and_fusion), kind=kLoop, calls=%fused_computation.35 | loop fusion | flops 5031936 | bytes 4320579 | tf_op jit(solution)/shard_map/jit(_where)/select_n | solution.py:83
  45.2 0.6 pad_bitcast_fusion
  47.3 1.4 %slice-done.1 = s8[3768320]{0:T(1024)(128)(4,1)S(1)} async-done(((s8[7962624]{0:T(1024)(128)(4,1)}), s8[3768320]{0:T(1024)(128)(4,1)S(1)}, s32[]{:S(2)}) %slice-start.1) | async-done | bytes 3768344
  48.7 7.4 %fusion.9 = f32[6,1,8,14,384]{4,2,3,1,0:T(8,128)S(1)} fusion(bf16[3,3,3,384,384]{4,3,2,1,0:T(8,128)(2,1)S(1)} %bitcast.57, bf16[8,3,1,7,2,384]{5,3,4,1,0,2:T(8,128)(2,1)S(1)} %slice.121, bf16[8,3,1,8,14,384]{5,3,4,1,0,2:T(8,128)(2,1)S(1)} %copy.16, pred[8,14]{0,1:T(8,128)(4,1)S(1)} %copy-done.2), kind=kOutput, calls=%fused_computation.36 | convolution fusion | flops 5358219264 | bytes 11317360 | tf_op jit(solution)/shard_map/conv_general_dilated | solution.py:39
  56.2 1.3 %copy.17 = f32[6,1,8,14,384]{4,1,3,2,0:T(1,128)S(1)} copy(f32[6,1,8,14,384]{4,2,3,1,0:T(8,128)S(1)} %fusion.9) | data formatting | bytes 2064384 | tf_op jit(solution)/shard_map/conv_general_dilated | solution.py:39
  57.4 0.7 slice.122
  58.9 0.5 copy.19
  59.5 0.7 %convert_element_type.29 = bf16[2,3,2,624]{3,2,1,0:T(2,128)(2,1)S(1)} reshape(bf16[2,3,1,2,104,2,3]{6,5,4,3,1,0,2:T(2,128)(2,1)S(1)} %copy.19) | data formatting | bytes 29952 | tf_op jit(solution)/shard_map/convert_element_type | solution.py:89
  60.2 1.9 %collective-permute-start.4 = (bf16[2,3,2,624]{3,2,1,0:T(2,128)(2,1)S(1)}, bf16[2,3,2,624]{3,2,1,0:T(2,128)(2,1)S(1)}, u32[]{:S(2)}, u32[]{:S(2)}) collective-permute-start(bf16[2,3,2,624]{3,2,1,0:T(2,128)(2,1)S(1)} %convert_element_type.29), channel_id=1, source_target_pairs={{0,0},{1,8},{2,4},{3,12},{4,2},{5,10},{6,6},{7,14},{8,1},{9,9},{10... | collective-permute-start | bytes 44936 | tf_op jit(solution)/shard_map/ppermute | solution.py:90
  62.1 5.8 %collective-permute-done.4 = bf16[2,3,2,624]{3,2,1,0:T(2,128)(2,1)S(1)} collective-permute-done((bf16[2,3,2,624]{3,2,1,0:T(2,128)(2,1)S(1)}, bf16[2,3,2,624]{3,2,1,0:T(2,128)(2,1)S(1)}, u32[]{:S(2)}, u32[]{:S(2)}) %collective-permute-start.4) | collective-permute-done | bytes 15008 | tf_op jit(solution)/shard_map/ppermute | solution.py:90
  67.9 0.6 copy.34
  (31 shorter events, 3.6 us)
Async XLA Ops:
  0.0 42.9 %copy-start = (bf16[432,384]{1,0:T(8,128)(2,1)S(1)}, bf16[432,384]{1,0:T(8,128)(2,1)}, u32[]{:S(2)}) copy-start(bf16[432,384]{1,0:T(8,128)(2,1)} %param.7) | copy-start | bytes 995332
  0.0 10.7 %copy-start.1 = (bf16[384,12]{0,1:T(8,128)(2,1)S(1)}, bf16[384,12]{0,1:T(8,128)(2,1)}, u32[]{:S(2)}) copy-start(bf16[384,12]{0,1:T(8,128)(2,1)} %param.9) | copy-start | bytes 27652
  1.9 1.7 %collective-permute-start = (bf16[12,2,3,1664]{3,0,2,1:T(8,128)(2,1)S(1)}, bf16[12,2,3,1664]{3,0,2,1:T(8,128)(2,1)S(1)}, u32[]{:S(2)}, u32[]{:S(2)}) collective-permute-start(bf16[12,2,3,1664]{3,0,2,1:T(8,128)(2,1)S(1)} %pad_dynamic-slice_fusion), channel_id=1, source_target_pairs={{0,1},{1,0},{2,3},{3,2},{4,5},{5,4},{6,7},{7,6},{8,9},{9,8},{10,11... | collective-permute-start | bytes 718856 | tf_op jit(solution)/shard_map/ppermute | solution.py:32
  3.9 6.2 %collective-permute-start.1 = (bf16[8,2,3,1664]{3,0,2,1:T(8,128)(2,1)S(1)}, bf16[8,2,3,1664]{3,0,2,1:T(8,128)(2,1)S(1)}, u32[]{:S(2)}, u32[]{:S(2)}) collective-permute-start(bf16[8,2,3,1664]{3,0,2,1:T(8,128)(2,1)S(1)} %constant_dynamic-slice_fusion.2), channel_id=1, source_target_pairs={{0,2},{1,3},{2,0},{3,1},{4,6},{5,7},{6,4},{7,5},{8,10},{9,11},{10,... | collective-permute-start | bytes 479240 | tf_op jit(solution)/shard_map/ppermute | solution.py:32
  10.2 5.4 %collective-permute-start.2 = (bf16[6,2,3,1664]{3,0,2,1:T(8,128)(2,1)S(1)}, bf16[6,2,3,1664]{3,0,2,1:T(8,128)(2,1)S(1)}, u32[]{:S(2)}, u32[]{:S(2)}) collective-permute-start(bf16[6,2,3,1664]{3,0,2,1:T(8,128)(2,1)S(1)} %constant_dynamic-slice_fusion.1), channel_id=1, source_target_pairs={{0,4},{1,5},{2,6},{3,7},{4,0},{5,1},{6,2},{7,3},{8,12},{9,13},{10,... | collective-permute-start | bytes 359432 | tf_op jit(solution)/shard_map/ppermute | solution.py:32
  15.7 8.4 %collective-permute-start.3 = (bf16[5,2,3,1664]{3,0,2,1:T(8,128)(2,1)S(1)}, bf16[5,2,3,1664]{3,0,2,1:T(8,128)(2,1)S(1)}, u32[]{:S(2)}, u32[]{:S(2)}) collective-permute-start(bf16[5,2,3,1664]{3,0,2,1:T(8,128)(2,1)S(1)} %constant_dynamic-slice_fusion), channel_id=1, source_target_pairs={{0,8},{1,9},{2,10},{3,11},{4,12},{5,13},{6,14},{7,15},{8,0},{9,1},... | collective-permute-start | bytes 299528 | tf_op jit(solution)/shard_map/ppermute | solution.py:32
  45.2 2.2 %slice-start = ((s8[7962624]{0:T(1024)(128)(4,1)}), s8[4194304]{0:T(1024)(128)(4,1)S(1)}, s32[]{:S(2)}) async-start(s8[7962624]{0:T(1024)(128)(4,1)} %bitcast.55), calls=%async_computation | async-start | bytes 8388608
  46.2 2.6 %slice-start.1 = ((s8[7962624]{0:T(1024)(128)(4,1)}), s8[3768320]{0:T(1024)(128)(4,1)S(1)}, s32[]{:S(2)}) async-start(s8[7962624]{0:T(1024)(128)(4,1)} %bitcast.55), calls=%async_computation.1 | async-start | bytes 7536640
  46.4 2.4 %copy-start.2 = (pred[8,14]{0,1:T(8,128)(4,1)S(1)}, pred[8,14]{0,1:T(8,128)(4,1)}, u32[]{:S(2)}) copy-start(pred[8,14]{0,1:T(8,128)(4,1)} %constant.57) | copy-start | bytes 340
  60.2 7.7 %collective-permute-start.4 = (bf16[2,3,2,624]{3,2,1,0:T(2,128)(2,1)S(1)}, bf16[2,3,2,624]{3,2,1,0:T(2,128)(2,1)S(1)}, u32[]{:S(2)}, u32[]{:S(2)}) collective-permute-start(bf16[2,3,2,624]{3,2,1,0:T(2,128)(2,1)S(1)} %convert_element_type.29), channel_id=1, source_target_pairs={{0,0},{1,8},{2,4},{3,12},{4,2},{5,10},{6,6},{7,14},{8,1},{9,9},{10... | collective-permute-start | bytes 44936 | tf_op jit(solution)/shard_map/ppermute | solution.py:90

commit v5 on v4

v5 whole, which is shorter than its diff:
```python
import jax
import jax.numpy as jnp
from jax import lax
from jax.experimental import pallas as pl
from jax.experimental.pallas import tpu as pltpu
from jax.sharding import PartitionSpec as P

ZC = 16
HALO = 2

epsilon = 1e-06

def rms_scale(values):
    return values * lax.rsqrt(jnp.mean(values * values, axis=-1, keepdims=True) + epsilon)


def reverse_bits(value, bits):
    return sum(((value >> b) & 1) << (bits - 1 - b) for b in range(bits))


def gather_rows(x, n, rows_dev, slot):
    bits = n.bit_length() - 1
    for k in reversed(range(bits)):
        half = (1 << k) * rows_dev
        size = half + 2 * HALO
        bit = (slot >> k) & 1
        own = lax.dynamic_slice_in_dim(x, bit * half, size, 0)
        send = lax.dynamic_slice_in_dim(x, (1 - bit) * half, size, 0)
        flip = 1 << (bits - 1 - k)
        pairs = [(i, i ^ flip) for i in range(n)]
        x = own + lax.ppermute(send, "dev", pairs)
    return x


def decode_kernel(row_ok_ref, xcol_ref, w_in_ref, w_vmem, w_pix_ref, out_ref, act_ref, center_ref):
    rows_in, span, _ = xcol_ref.shape
    rows_out = rows_in - 2
    lead = act_ref.shape[2] - span
    cp = lead // 2
    channels = act_ref.shape[3]
    taps = w_vmem.shape[0] // 3
    zeros = jnp.zeros((lead, channels), act_ref.dtype)
    for e in range(3):
        for j in range(rows_in):
            act_ref[e, j, 0:lead, :] = zeros
    w_in = w_in_ref[...]
    for j in range(rows_in):
        first = jnp.dot(xcol_ref[j], w_in, preferred_element_type=jnp.float32)
        if 1 <= j <= rows_out:
            center_ref[j - 1] = first
        scaled = first * lax.rsqrt(jnp.mean(first * first, axis=-1, keepdims=True) + epsilon)
        act = scaled / (1.0 + jnp.exp(-scaled)) * row_ok_ref[j]
        act_ref[1, j, lead:, :] = act.astype(act_ref.dtype)
        act_ref[0, j, lead:, :] = pltpu.roll(act, 1, 0).astype(act_ref.dtype)
        act_ref[2, j, lead:, :] = pltpu.roll(act, span - 1, 0).astype(act_ref.dtype)
    for jo in range(rows_out):

        def tap(t, acc):
            a = t // 9
            b = (t // 3) % 3
            e = t % 3
            start = pl.multiple_of(a * cp, 16)
            piece = act_ref[e, jo + b, pl.ds(start, span), :]
            return acc + jnp.dot(piece, w_vmem[t], preferred_element_type=jnp.float32)

        acc = lax.fori_loop(0, 27, tap, center_ref[jo])
        scale = lax.rsqrt(jnp.mean(acc * acc, axis=-1, keepdims=True) + epsilon)
        normed = (acc * scale).astype(jnp.bfloat16)
        out_ref[jo] = jnp.dot(normed, w_pix_ref[...], preferred_element_type=jnp.float32)


def decode(row_ok, xcol, conv_in, conv_mid, to_pixels, cp):
    rows_in, span, _ = xcol.shape
    channels = conv_mid.shape[1]
    w_mid = conv_mid.reshape(27, channels, channels)
    lanes = 128
    k_in = -(-xcol.shape[2] // lanes) * lanes
    xcol = jnp.pad(xcol, ((0, 0), (0, 0), (0, k_in - xcol.shape[2])))
    conv_in = jnp.pad(conv_in, ((0, k_in - conv_in.shape[0]), (0, 0)))
    n_pix = to_pixels.shape[1]
    to_pixels = jnp.pad(to_pixels, ((0, 0), (0, lanes - n_pix)))
    vmem = pltpu.MemorySpace.VMEM
    return pl.pallas_call(
        decode_kernel,
        out_shape=jax.ShapeDtypeStruct((rows_in - 2, span, lanes), jnp.float32),
        in_specs=[
            pl.BlockSpec(memory_space=pltpu.MemorySpace.SMEM),
            pl.BlockSpec(memory_space=vmem),
            pl.BlockSpec(memory_space=vmem),
            pl.BlockSpec(memory_space=vmem),
            pl.BlockSpec(memory_space=vmem),
        ],
        out_specs=pl.BlockSpec(memory_space=vmem),
        scratch_shapes=[
            pltpu.VMEM((3, rows_in, span + 2 * cp, channels), jnp.bfloat16),
            pltpu.VMEM((rows_in - 2, span, channels), jnp.float32),
        ],
        compiler_params=pltpu.CompilerParams(vmem_limit_bytes=48 * 1024 * 1024),
    )(row_ok, xcol, conv_in, w_mid, to_pixels)[:, :, :n_pix]


def local(latents, owners, conv_in, conv_mid, to_pixels):
    n = lax.axis_size("dev")
    assert n & (n - 1) == 0
    position = lax.axis_index("dev")
    groups, frames, height, width = latents.shape[1:]
    columns = width // ZC
    rows_dev = height // n
    bits = n.bit_length() - 1
    slot = reverse_bits(position, bits)
    cp = -(-columns // 16) * 16
    steps = groups * frames

    x = jnp.transpose(latents[0], (2, 0, 1, 3))
    keep = owners == position
    x = jnp.where(keep[None, :, None, None], x, jnp.zeros_like(x))
    x = jnp.pad(x, ((HALO, HALO), (0, 0), (0, 0), (0, 0)))
    x = gather_rows(x, n, rows_dev, slot)

    rows_in = rows_dev + 2
    window = jnp.transpose(x, (1, 2, 0, 3)).reshape(steps, rows_dev + 2 * HALO, columns, ZC)
    padded = jnp.pad(window, ((2, 0), (0, 0), (1, 1 + cp - columns), (0, 0)))
    pieces = [
        padded[a : a + steps, b : b + rows_in, e : e + cp]
        for a in range(3)
        for b in range(3)
        for e in range(3)
    ]
    xcol = jnp.concatenate(pieces, axis=-1)
    col_ok = jnp.arange(cp) < columns
    xcol = jnp.where(col_ok[None, None, :, None], xcol, jnp.zeros_like(xcol))
    xcol = jnp.transpose(xcol, (1, 0, 2, 3)).reshape(rows_in, steps * cp, 27 * ZC)
    row_of = slot * rows_dev - 1 + jnp.arange(rows_in)
    row_ok = ((row_of >= 0) & (row_of < height)).astype(jnp.float32)

    projected = decode(row_ok, xcol, conv_in, conv_mid, to_pixels, cp)
    projected = projected.reshape(rows_dev, groups, frames, cp, 2, 2, 3)[:, :, :, :columns]
    projected = projected.transpose(1, 2, 0, 4, 3, 5, 6)
    pixels = projected.reshape(groups, frames, 2 * rows_dev, 6 * columns).astype(jnp.bfloat16)
    return lax.ppermute(pixels, "dev", [(i, reverse_bits(i, bits)) for i in range(n)])


def solution(mesh):
    in_specs = (P(("stream", "dev"), None, None, None, None), P("stream"), P(), P(), P())
    out_specs = P("stream", None, "dev", None)
    return jax.shard_map(local, mesh=mesh, in_specs=in_specs, out_specs=out_specs, check_vma=False)
```

time: 69.7 us -> 78.2 us (1.12)
  Pallas kernels: 0 us -> 21.8 us
  matrix products: 9 us -> 0 us
  local copies, waits for them, and re-layouts: 26.3 us -> 23.5 us
  other arithmetic: 3.6 us -> 2.32 us
    pallas_call x0 -> x1, Pallas kernels: none -> 21.8 us  [decode(): pl.pallas_call(decode_kernel, out_shape=jax.ShapeDtypeStruct((rows_in - 2...]
    conv_general_dilated x1 -> x0, matrix products: 7.41 us -> none  [causal_conv(): lax.conv_general_dilated(padded[None], kernel, window_strides=(1, 1, 1),...]
    conv_general_dilated x4 -> x0, local copies, waits for them, and re-layouts: 2.47 us -> none  [causal_conv(): lax.conv_general_dilated(padded[None], kernel, window_strides=(1, 1, 1),...]
    unnamed x12 -> x6, local copies, waits for them, and re-layouts: 2.85 us -> 0.76 us
    dot_general x2 -> x0, matrix products: 1.59 us -> none  [the longest x1 1.27 us: local(): first_act = jnp.dot(xcol, conv_in, preferred_element_type=jnp.float32)]
    slice x2 -> x4, local copies, waits for them, and re-layouts: 6.4 us -> 7.9 us  [the longest x2 7.77 us: local(): padded[a:a + steps, b:b + rows_in, e:e + cp]]
where the time goes in v5:
time: 78.2 us; the launch traced here: 77 us
  waiting for transfers between devices  24.7 us (32%)
  local copies, waits for them, and re-layouts  23.5 us (30%)
  Pallas kernels  21.8 us (28%)
  starting transfers between devices  4.46 us (6%)
  other arithmetic  2.32 us (3%)
    pallas_call x1, Pallas kernels, decode(): pl.pallas_call(decode_kernel, out_shape=jax.ShapeDtypeStruct((rows_in - 2...  21.8 us
    ppermute x4, waiting for transfers between devices, gather_rows(): x = own + lax.ppermute(send, 'dev', pairs)  18.9 us
    concatenate x1, local copies, waits for them, and re-layouts, local(): xcol = jnp.concatenate(pieces, axis=-1)  12.2 us
    slice x2, local copies, waits for them, and re-layouts, local(): padded[a:a + steps, b:b + rows_in, e:e + cp]  7.77 us
    ppermute x1, waiting for transfers between devices, local(): lax.ppermute(pixels, 'dev', [(i, reverse_bits(i, bits)) for i in range(n)])  5.82 us
    ppermute x4, starting transfers between devices, gather_rows(): x = own + lax.ppermute(send, 'dev', pairs)  2.54 us
    ppermute x1, starting transfers between devices, local(): lax.ppermute(pixels, 'dev', [(i, reverse_bits(i, bits)) for i in range(n)])  1.92 us
  transfers between devices with their start and end apart: 5, of which 5 were waited for; matrix products, arithmetic and copies ran while one was open for 0% of the time, Pallas kernels for 0%

profile of v5, /device:TPU:24, one launch (start us, length us, event | category | flops | bytes accessed | tf_op | source)
XLA Modules:
  0.0 77.0 jit_solution(17103814829123742265)
XLA Ops:
  0.0 0.7 broadcast_compare_fusion
  0.7 1.1 %fusion.1 = bf16[16,2,3,1664]{3,0,2,1:T(8,128)(2,1)S(1)} fusion(bf16[1,2,3,16,1664]{4,3,2,1,0:T(8,128)(2,1)} %param.5, pred[2]{0:T(512)(128)(4,1)S(1)} %broadcast_compare_fusion), kind=kLoop, calls=%fused_computation.33 | loop fusion | flops 159744 | bytes 638978 | tf_op jit(solution)/shard_map/jit(_where)/select_n | solution.py:116
  1.7 0.1 pad_dynamic-slice_fusion
  2.0 1.6 %collective-permute-done = bf16[12,2,3,1664]{3,0,2,1:T(8,128)(2,1)S(1)} collective-permute-done((bf16[12,2,3,1664]{3,0,2,1:T(8,128)(2,1)S(1)}, bf16[12,2,3,1664]{3,0,2,1:T(8,128)(2,1)S(1)}, u32[]{:S(2)}, u32[]{:S(2)}) %collective-permute-start) | collective-permute-done | bytes 239648 | tf_op jit(solution)/shard_map/ppermute | solution.py:31
  3.6 0.2 fusion
  3.8 1.6 %collective-permute-start.1 = (bf16[8,2,3,1664]{3,0,2,1:T(8,128)(2,1)S(1)}, bf16[8,2,3,1664]{3,0,2,1:T(8,128)(2,1)S(1)}, u32[]{:S(2)}, u32[]{:S(2)}) collective-permute-start(bf16[8,2,3,1664]{3,0,2,1:T(8,128)(2,1)S(1)} %constant_dynamic-slice_fusion.2), channel_id=1, source_target_pairs={{0,2},{1,3},{2,0},{3,1},{4,6},{5,7},{6,4},{7,5},{8,10},{9,11},{10,... | collective-permute-start | bytes 479240 | tf_op jit(solution)/shard_map/ppermute | solution.py:31
  5.4 4.7 %collective-permute-done.1 = bf16[8,2,3,1664]{3,0,2,1:T(8,128)(2,1)S(1)} collective-permute-done((bf16[8,2,3,1664]{3,0,2,1:T(8,128)(2,1)S(1)}, bf16[8,2,3,1664]{3,0,2,1:T(8,128)(2,1)S(1)}, u32[]{:S(2)}, u32[]{:S(2)}) %collective-permute-start.1) | collective-permute-done | bytes 159776 | tf_op jit(solution)/shard_map/ppermute | solution.py:31
  10.2 0.5 collective-permute-start.2
  10.7 0.1 copy.10
  10.9 4.6 %collective-permute-done.2 = bf16[6,2,3,1664]{3,0,2,1:T(8,128)(2,1)S(1)} collective-permute-done((bf16[6,2,3,1664]{3,0,2,1:T(8,128)(2,1)S(1)}, bf16[6,2,3,1664]{3,0,2,1:T(8,128)(2,1)S(1)}, u32[]{:S(2)}, u32[]{:S(2)}) %collective-permute-start.2) | collective-permute-done | bytes 119840 | tf_op jit(solution)/shard_map/ppermute | solution.py:31
  15.7 0.4 collective-permute-start.3
  16.1 8.0 %collective-permute-done.3 = bf16[5,2,3,1664]{3,0,2,1:T(8,128)(2,1)S(1)} collective-permute-done((bf16[5,2,3,1664]{3,0,2,1:T(8,128)(2,1)S(1)}, bf16[5,2,3,1664]{3,0,2,1:T(8,128)(2,1)S(1)}, u32[]{:S(2)}, u32[]{:S(2)}) %collective-permute-start.3) | collective-permute-done | bytes 99872 | tf_op jit(solution)/shard_map/ppermute | solution.py:31
  24.2 0.6 reshape.20
  24.8 5.4 %pad_slice_fusion = (bf16[6,3,112,16]{3,2,0,1:T(8,128)(2,1)S(1)}, bf16[6,3,112,16]{3,2,0,1:T(8,128)(2,1)}, bf16[6,3,112,16]{3,2,0,1:T(8,128)(2,1)}, bf16[6,3,112...) fusion(bf16[6,5,104,16]{3,2,0,1:T(8,128)(2,1)S(1)} %reshape.20), kind=kLoop, calls=%fused_computation | loop fusion | bytes 1325568 | tf_op jit(solution)/shard_map/slice | solution.py:124
  30.3 2.3 %pad_slice_fusion.1 = (bf16[6,3,112,16]{3,2,0,1:T(8,128)(2,1)}, bf16[6,3,112,16]{3,2,0,1:T(8,128)(2,1)}, bf16[6,3,112,16]{3,2,0,1:T(8,128)(2,1)}, bf16[6,3,112,1...) fusion(bf16[6,5,104,16]{3,2,0,1:T(8,128)(2,1)S(1)} %reshape.20), kind=kLoop, calls=%fused_computation.1 | loop fusion | bytes 615936 | tf_op jit(solution)/shard_map/slice | solution.py:124
  32.6 12.2 %concatenate.3 = bf16[6,3,112,432]{3,2,0,1:T(8,128)(2,1)S(1)} concatenate(bf16[6,3,112,16]{3,2,0,1:T(8,128)(2,1)} %get-tuple-element.31, bf16[6,3,112,16]{3,2,0,1:T(8,128)(2,1)} %get-tuple-element.6, bf16[6,3,112,16]{3,2,0,1:T(8,128)(2,1)} %get-tuple-element.7, bf16[6,3,112,16]{3,2,0,1:T(8,128)(2,1)} %get-tuple-element.8, bf16[6,3,112,16]{3,2,0,1:T(8,128)(2,1)} %get-tuple-element.9, ...), dimensions={3} | concatenate | bytes 3483648 | tf_op jit(solution)/shard_map/concatenate | solution.py:129
  44.8 0.2 broadcast_select_fusion
  45.0 0.3 pad.22.xcol_ref
  45.3 21.8 %shard_map.55 = f32[1,672,128]{2,1,0:T(8,128)S(1)} custom-call(f32[3]{0:T(128)S(1)} %and_convert_fusion.row_ok_ref, bf16[3,672,512]{2,1,0:T(8,128)(2,1)S(1)} %pad.22.xcol_ref, bf16[512,384]{1,0:T(8,128)(2,1)S(1)} %pad.23.w_in_ref, bf16[27,384,384]{2,1,0:T(8,128)(2,1)} %bitcast.21, bf16[384,128]{1,0:T(8,128)(2,1)S(1)} %pad.24.w_pix_ref), custom_call_target="tpu_custom_call" | custom-call | tf_op jit(solution)/shard_map/pallas_call | solution.py:83
  67.4 0.5 copy.12
  68.0 0.7 convert_element_type.22
  68.7 1.9 %collective-permute-start.4 = (bf16[2,3,2,624]{3,2,1,0:T(2,128)(2,1)S(1)}, bf16[2,3,2,624]{3,2,1,0:T(2,128)(2,1)S(1)}, u32[]{:S(2)}, u32[]{:S(2)}) collective-permute-start(bf16[2,3,2,624]{3,2,1,0:T(2,128)(2,1)S(1)} %convert_element_type.22), channel_id=1, source_target_pairs={{0,0},{1,8},{2,4},{3,12},{4,2},{5,10},{6,6},{7,14},{8,1},{9,9},{10... | collective-permute-start | bytes 44936 | tf_op jit(solution)/shard_map/ppermute | solution.py:140
  70.6 5.8 %collective-permute-done.4 = bf16[2,3,2,624]{3,2,1,0:T(2,128)(2,1)S(1)} collective-permute-done((bf16[2,3,2,624]{3,2,1,0:T(2,128)(2,1)S(1)}, bf16[2,3,2,624]{3,2,1,0:T(2,128)(2,1)S(1)}, u32[]{:S(2)}, u32[]{:S(2)}) %collective-permute-start.4) | collective-permute-done | bytes 15008 | tf_op jit(solution)/shard_map/ppermute | solution.py:140
  76.4 0.6 copy.14
  (20 shorter events, 0.8 us)
Async XLA Ops:
  1.9 8.8 %copy-start.1 = (bf16[384,12]{0,1:T(8,128)(2,1)S(1)}, bf16[384,12]{0,1:T(8,128)(2,1)}, u32[]{:S(2)}) copy-start(bf16[384,12]{0,1:T(8,128)(2,1)} %param.9) | copy-start | bytes 27652
  1.9 9.0 %copy-start = (bf16[432,384]{1,0:T(8,128)(2,1)S(1)}, bf16[432,384]{1,0:T(8,128)(2,1)}, u32[]{:S(2)}) copy-start(bf16[432,384]{1,0:T(8,128)(2,1)} %param.7) | copy-start | bytes 995332
  1.9 1.7 %collective-permute-start = (bf16[12,2,3,1664]{3,0,2,1:T(8,128)(2,1)S(1)}, bf16[12,2,3,1664]{3,0,2,1:T(8,128)(2,1)S(1)}, u32[]{:S(2)}, u32[]{:S(2)}) collective-permute-start(bf16[12,2,3,1664]{3,0,2,1:T(8,128)(2,1)S(1)} %pad_dynamic-slice_fusion), channel_id=1, source_target_pairs={{0,1},{1,0},{2,3},{3,2},{4,5},{5,4},{6,7},{7,6},{8,9},{9,8},{10,11... | collective-permute-start | bytes 718856 | tf_op jit(solution)/shard_map/ppermute | solution.py:31
  3.8 6.2 %collective-permute-start.1 = (bf16[8,2,3,1664]{3,0,2,1:T(8,128)(2,1)S(1)}, bf16[8,2,3,1664]{3,0,2,1:T(8,128)(2,1)S(1)}, u32[]{:S(2)}, u32[]{:S(2)}) collective-permute-start(bf16[8,2,3,1664]{3,0,2,1:T(8,128)(2,1)S(1)} %constant_dynamic-slice_fusion.2), channel_id=1, source_target_pairs={{0,2},{1,3},{2,0},{3,1},{4,6},{5,7},{6,4},{7,5},{8,10},{9,11},{10,... | collective-permute-start | bytes 479240 | tf_op jit(solution)/shard_map/ppermute | solution.py:31
  10.2 5.4 %collective-permute-start.2 = (bf16[6,2,3,1664]{3,0,2,1:T(8,128)(2,1)S(1)}, bf16[6,2,3,1664]{3,0,2,1:T(8,128)(2,1)S(1)}, u32[]{:S(2)}, u32[]{:S(2)}) collective-permute-start(bf16[6,2,3,1664]{3,0,2,1:T(8,128)(2,1)S(1)} %constant_dynamic-slice_fusion.1), channel_id=1, source_target_pairs={{0,4},{1,5},{2,6},{3,7},{4,0},{5,1},{6,2},{7,3},{8,12},{9,13},{10,... | collective-permute-start | bytes 359432 | tf_op jit(solution)/shard_map/ppermute | solution.py:31
  15.7 8.4 %collective-permute-start.3 = (bf16[5,2,3,1664]{3,0,2,1:T(8,128)(2,1)S(1)}, bf16[5,2,3,1664]{3,0,2,1:T(8,128)(2,1)S(1)}, u32[]{:S(2)}, u32[]{:S(2)}) collective-permute-start(bf16[5,2,3,1664]{3,0,2,1:T(8,128)(2,1)S(1)} %constant_dynamic-slice_fusion), channel_id=1, source_target_pairs={{0,8},{1,9},{2,10},{3,11},{4,12},{5,13},{6,14},{7,15},{8,0},{9,1},... | collective-permute-start | bytes 299528 | tf_op jit(solution)/shard_map/ppermute | solution.py:31
  68.7 7.7 %collective-permute-start.4 = (bf16[2,3,2,624]{3,2,1,0:T(2,128)(2,1)S(1)}, bf16[2,3,2,624]{3,2,1,0:T(2,128)(2,1)S(1)}, u32[]{:S(2)}, u32[]{:S(2)}) collective-permute-start(bf16[2,3,2,624]{3,2,1,0:T(2,128)(2,1)S(1)} %convert_element_type.22), channel_id=1, source_target_pairs={{0,0},{1,8},{2,4},{3,12},{4,2},{5,10},{6,6},{7,14},{8,1},{9,9},{10... | collective-permute-start | bytes 44936 | tf_op jit(solution)/shard_map/ppermute | solution.py:140

commit v6 on v2

--- a/solution.py
+++ b/solution.py
@@ -65,7 +65,18 @@
     x = gather_rows(x, n, rows_dev, slot)
 
     window = jnp.transpose(x, (1, 2, 0, 3)).reshape(groups * frames, rows_dev + 2 * HALO, columns, ZC)
-    first_act = causal_conv(window, conv_in, ZC)
+    steps = groups * frames
+    framed = jnp.pad(window, ((2, 0), (0, 0), (1, 1), (0, 0)))
+    stacked = jnp.concatenate([framed[a : a + steps] for a in range(3)], axis=-1)
+    kernel_in = conv_in.reshape(3, 3, 3, ZC, channels).transpose(1, 2, 0, 3, 4).reshape(3, 3, 3 * ZC, channels)
+    first_act = lax.conv_general_dilated(
+        stacked,
+        kernel_in,
+        window_strides=(1, 1),
+        padding="VALID",
+        dimension_numbers=("NHWC", "HWIO", "NHWC"),
+        preferred_element_type=jnp.float32,
+    )
     activated = jax.nn.silu(rms_scale(first_act)).astype(jnp.bfloat16)
     row_of = slot * rows_dev - 1 + jnp.arange(rows_dev + 2)
     inside = (row_of >= 0) & (row_of < height)

time: 59.5 us -> 74.1 us (1.25)
  other arithmetic: 3.98 us -> 12.3 us
  local copies, waits for them, and re-layouts: 15 us -> 22.6 us
  waiting for transfers between devices: 24.9 us -> 23.6 us
    conv_general_dilated x0 -> x6, local copies, waits for them, and re-layouts: none -> 7.79 us  [local(): lax.conv_general_dilated(stacked, kernel_in, window_strides=(1, 1), paddi...]
    conv_general_dilated x9 -> x3, local copies, waits for them, and re-layouts: 8.41 us -> 1.59 us  [causal_conv(): lax.conv_general_dilated(padded[None], kernel, window_strides=(1, 1, 1),...]
    reduce_sum x2 -> x1, other arithmetic: 0.62 us -> 5.06 us  [rms_scale(): jnp.mean(values * values, axis=-1, keepdims=True) + epsilon]
    rsqrt x0 -> x3, local copies, waits for them, and re-layouts: none -> 3.75 us  [rms_scale(): lax.rsqrt(jnp.mean(values * values, axis=-1, keepdims=True) + epsilon)]
    conv_general_dilated x2 -> x1, matrix products: 10.3 us -> 7.36 us  [causal_conv(): lax.conv_general_dilated(padded[None], kernel, window_strides=(1, 1, 1),...]
    conv_general_dilated x0 -> x1, matrix products: none -> 2.78 us  [local(): lax.conv_general_dilated(stacked, kernel_in, window_strides=(1, 1), paddi...]
    select_n x1, other arithmetic: 0.91 us -> 2.63 us  [local(): jnp.where(inside[None, :, None, None], activated, jnp.zeros_like(activated))]
    slice x0 -> x4, local copies, waits for them, and re-layouts: none -> 1.46 us  [local(): stacked = jnp.concatenate([framed[a:a + steps] for a in range(3)], axis=-1)]
  transfers between devices with their start and end apart: 5 -> 5, of which waited for: 5 -> 5; matrix products, arithmetic and copies ran while one was open for 0% -> 2% of each run, Pallas kernels for 0% -> 0%
where the time goes in v6:
time: 74.1 us; the launch traced here: 73.7 us
  waiting for transfers between devices  23.6 us (32%)
  local copies, waits for them, and re-layouts  22.6 us (30%)
  other arithmetic  12.3 us (17%)
  matrix products  10.5 us (14%)
  starting transfers between devices  4.46 us (6%)
    ppermute x4, waiting for transfers between devices, gather_rows(): x = own + lax.ppermute(send, 'dev', pairs)  17.7 us
    conv_general_dilated x6, local copies, waits for them, and re-layouts, local(): lax.conv_general_dilated(stacked, kernel_in, window_strides=(1, 1), paddi...  7.79 us
    conv_general_dilated x1, matrix products, causal_conv(): lax.conv_general_dilated(padded[None], kernel, window_strides=(1, 1, 1),...  7.36 us
    ppermute x1, waiting for transfers between devices, local(): lax.ppermute(pixels, 'dev', [(i, reverse_bits(i, bits)) for i in range(n)])  5.82 us
    reduce_sum x1, other arithmetic, rms_scale(): jnp.mean(values * values, axis=-1, keepdims=True) + epsilon  5.06 us
    rsqrt x3, local copies, waits for them, and re-layouts, rms_scale(): lax.rsqrt(jnp.mean(values * values, axis=-1, keepdims=True) + epsilon)  3.75 us
    unnamed x22, local copies, waits for them, and re-layouts  3.6 us
    conv_general_dilated x1, matrix products, local(): lax.conv_general_dilated(stacked, kernel_in, window_strides=(1, 1), paddi...  2.78 us
  transfers between devices with their start and end apart: 5, of which 5 were waited for; matrix products, arithmetic and copies ran while one was open for 2% of the time, Pallas kernels for 0%

profile of v6, /device:TPU:24, one launch (start us, length us, event | category | flops | bytes accessed | tf_op | source)
XLA Modules:
  0.0 73.7 jit_solution(17588746400567233193)
XLA Ops:
  0.0 0.7 broadcast_compare_fusion
  0.7 1.1 %fusion.21 = bf16[16,2,3,1664]{3,0,2,1:T(8,128)(2,1)S(1)} fusion(bf16[1,2,3,16,1664]{4,3,2,1,0:T(8,128)(2,1)} %param.5, pred[2]{0:T(512)(128)(4,1)S(1)} %broadcast_compare_fusion), kind=kLoop, calls=%fused_computation.37 | loop fusion | flops 159744 | bytes 638978 | tf_op jit(solution)/shard_map/jit(_where)/select_n | solution.py:63
  2.0 1.6 %collective-permute-done = bf16[12,2,3,1664]{3,0,2,1:T(8,128)(2,1)S(1)} collective-permute-done((bf16[12,2,3,1664]{3,0,2,1:T(8,128)(2,1)S(1)}, bf16[12,2,3,1664]{3,0,2,1:T(8,128)(2,1)S(1)}, u32[]{:S(2)}, u32[]{:S(2)}) %collective-permute-start) | collective-permute-done | bytes 239648 | tf_op jit(solution)/shard_map/ppermute | solution.py:32
  3.9 1.6 %collective-permute-start.1 = (bf16[8,2,3,1664]{3,0,2,1:T(8,128)(2,1)S(1)}, bf16[8,2,3,1664]{3,0,2,1:T(8,128)(2,1)S(1)}, u32[]{:S(2)}, u32[]{:S(2)}) collective-permute-start(bf16[8,2,3,1664]{3,0,2,1:T(8,128)(2,1)S(1)} %constant_dynamic-slice_fusion.2), channel_id=1, source_target_pairs={{0,2},{1,3},{2,0},{3,1},{4,6},{5,7},{6,4},{7,5},{8,10},{9,11},{10,... | collective-permute-start | bytes 479240 | tf_op jit(solution)/shard_map/ppermute | solution.py:32
  5.4 4.7 %collective-permute-done.1 = bf16[8,2,3,1664]{3,0,2,1:T(8,128)(2,1)S(1)} collective-permute-done((bf16[8,2,3,1664]{3,0,2,1:T(8,128)(2,1)S(1)}, bf16[8,2,3,1664]{3,0,2,1:T(8,128)(2,1)S(1)}, u32[]{:S(2)}, u32[]{:S(2)}) %collective-permute-start.1) | collective-permute-done | bytes 159776 | tf_op jit(solution)/shard_map/ppermute | solution.py:32
  11.3 0.8 %copy.24 = bf16[3,3,3,16,384]{4,3,2,1,0:T(8,128)(2,1)} copy(bf16[3,3,3,16,384]{4,3,1,0,2:T(8,128)(2,1)S(1)} %bitcast.84) | data formatting | bytes 663552 | tf_op jit(solution)/shard_map/transpose | solution.py:71
  12.1 3.5 %collective-permute-done.2 = bf16[6,2,3,1664]{3,0,2,1:T(8,128)(2,1)S(1)} collective-permute-done((bf16[6,2,3,1664]{3,0,2,1:T(8,128)(2,1)S(1)}, bf16[6,2,3,1664]{3,0,2,1:T(8,128)(2,1)S(1)}, u32[]{:S(2)}, u32[]{:S(2)}) %collective-permute-start.2) | collective-permute-done | bytes 119840 | tf_op jit(solution)/shard_map/ppermute | solution.py:32
  16.1 8.0 %collective-permute-done.3 = bf16[5,2,3,1664]{3,0,2,1:T(8,128)(2,1)S(1)} collective-permute-done((bf16[5,2,3,1664]{3,0,2,1:T(8,128)(2,1)S(1)}, bf16[5,2,3,1664]{3,0,2,1:T(8,128)(2,1)S(1)}, u32[]{:S(2)}, u32[]{:S(2)}) %collective-permute-start.3) | collective-permute-done | bytes 99872 | tf_op jit(solution)/shard_map/ppermute | solution.py:32
  28.0 2.8 %multiply_reduce_fusion = (f32[3,48,14]{1,2,0:T(8,128)S(1)}, f32[3,48,14,384]{3,1,2,0:T(8,128)S(1)}) fusion(bf16[3,3,48,384]{3,2,1,0:T(8,128)(2,1)S(1)} %bitcast.85, bf16[5,6,8,16,48]{4,3,2,1,0:T(8,128)(2,1)S(1)} %fusion.16, pred[48,14]{0,1:T(8,128)(4,1)S(1)} %copy-done.6), kind=kOutput, calls=%fused_computation.2 | convolution fusion | flops 671180800 | bytes 3805728 | tf_op jit(solution)/shard_map/conv_general_dilated | solution.py:72
  30.8 1.0 %slice.24 = f32[1,48,14,384]{3,1,2,0:T(8,128)} slice(f32[3,48,14,384]{3,1,2,0:T(8,128)S(1)} %get-tuple-element.9), slice={[1:2], [0:48], [0:14], [0:384]} | slice | bytes 2064384 | tf_op jit(solution)/shard_map/conv_general_dilated | solution.py:72
  31.8 1.0 %copy.26 = f32[3,48,14,384]{3,2,1,0:T(8,128)S(1)} copy(f32[3,48,14,384]{3,1,2,0:T(8,128)S(1)} %get-tuple-element.9) | data formatting | bytes 6193152 | tf_op jit(solution)/shard_map/conv_general_dilated | solution.py:72
  33.4 1.5 %copy.27 = f32[3,48,14]{2,1,0:T(8,128)} copy(f32[3,48,14]{1,2,0:T(8,128)} %add_rsqrt_fusion) | data formatting | bytes 16128 | tf_op jit(solution)/shard_map/rsqrt | solution.py:15
  34.9 1.6 %reshape.67 = f32[3,6,112]{2,1,0:T(8,128)} reshape(f32[3,48,14]{2,1,0:T(8,128)} %copy.27) | data formatting | bytes 16128 | tf_op jit(solution)/shard_map/rsqrt | solution.py:15
  36.5 0.7 slice_bitcast_fusion.3
  37.2 3.3 %copy.25 = f32[1,48,14,384]{3,0,2,1:T(1,128)} copy(f32[1,48,14,384]{3,1,2,0:T(8,128)} %slice.24) | data formatting | bytes 2064384 | tf_op jit(solution)/shard_map/conv_general_dilated | solution.py:72
  40.4 2.2 %reshape.65 = f32[3,6,112,384]{3,2,1,0:T(8,128)} reshape(f32[3,48,14,384]{3,2,1,0:T(8,128)S(1)} %copy.26) | data formatting | bytes 6193152 | tf_op jit(solution)/shard_map/conv_general_dilated | solution.py:72
  42.6 2.6 %fusion.10 = bf16[6,3,104,384]{3,2,0,1:T(8,128)(2,1)S(1)} fusion(f32[6,3,104]{2,0,1:T(8,128)S(1)} %slice_bitcast_fusion.3, f32[3,6,112,384]{3,2,1,0:T(8,128)} %reshape.65, pred[3]{0:T(512)(128)(4,1)S(1)} %compare_and_fusion), kind=kLoop, calls=%fused_computation.16 | loop fusion | flops 5031936 | bytes 4320579 | tf_op jit(solution)/shard_map/jit(_where)/select_n | solution.py:83
  47.5 1.4 %slice-done.1 = s8[3768320]{0:T(1024)(128)(4,1)S(1)} async-done(((s8[7962624]{0:T(1024)(128)(4,1)}), s8[3768320]{0:T(1024)(128)(4,1)S(1)}, s32[]{:S(2)}) %slice-start.1) | async-done | bytes 3768344
  48.8 7.4 %fusion.11 = f32[6,1,8,14,384]{4,2,3,1,0:T(8,128)S(1)} fusion(bf16[3,3,3,384,384]{4,3,2,1,0:T(8,128)(2,1)S(1)} %bitcast.89, bf16[8,3,1,7,2,384]{5,3,4,1,0,2:T(8,128)(2,1)S(1)} %slice.28, bf16[8,3,1,8,14,384]{5,3,4,1,0,2:T(8,128)(2,1)S(1)} %copy.30, pred[8,14]{0,1:T(8,128)(4,1)S(1)} %copy-done.5), kind=kOutput, calls=%fused_computation.17 | convolution fusion | flops 5358219264 | bytes 11317360 | tf_op jit(solution)/shard_map/conv_general_dilated | solution.py:39
  56.2 1.1 %copy.31 = f32[6,1,8,14,384]{4,1,3,2,0:T(1,128)S(1)} copy(f32[6,1,8,14,384]{4,2,3,1,0:T(8,128)S(1)} %fusion.11) | data formatting | bytes 2064384 | tf_op jit(solution)/shard_map/conv_general_dilated | solution.py:39
  57.4 5.1 %multiply_reduce_fusion.1 = f32[6,104]{1,0:T(8,128)S(1)} fusion(f32[6,1,1,112,384]{4,1,3,2,0:T(1,128)S(1)} %bitcast.80, f32[1,6,112,384]{3,0,2,1:T(1,128)S(1)} %bitcast.78), kind=kLoop, calls=%fused_computation.31 | loop fusion | flops 718224 | bytes 1919424 | tf_op jit(solution)/shard_map/reduce_sum | solution.py:15
  62.5 1.2 %multiply_convert_fusion.1 = bf16[6,1,104,384]{3,1,2,0:T(2,128)(2,1)S(1)} fusion(f32[6,104]{1,0:T(8,128)S(1)} %add_rsqrt_fusion.1, f32[6,1,1,112,384]{4,1,3,2,0:T(1,128)S(1)} %bitcast.81, f32[1,6,112,384]{3,0,2,1:T(1,128)S(1)} %bitcast.79), kind=kLoop, calls=%fused_computation.30 | loop fusion | flops 718848 | bytes 2398656 | tf_op jit(solution)/shard_map/convert_element_type | solution.py:86
  65.3 1.9 %collective-permute-start.4 = (bf16[2,3,2,624]{3,2,1,0:T(2,128)(2,1)S(1)}, bf16[2,3,2,624]{3,2,1,0:T(2,128)(2,1)S(1)}, u32[]{:S(2)}, u32[]{:S(2)}) collective-permute-start(bf16[2,3,2,624]{3,2,1,0:T(2,128)(2,1)S(1)} %convert_element_type.29), channel_id=1, source_target_pairs={{0,0},{1,8},{2,4},{3,12},{4,2},{5,10},{6,6},{7,14},{8,1},{9,9},{10... | collective-permute-start | bytes 44936 | tf_op jit(solution)/shard_map/ppermute | solution.py:90
  67.3 5.8 %collective-permute-done.4 = bf16[2,3,2,624]{3,2,1,0:T(2,128)(2,1)S(1)} collective-permute-done((bf16[2,3,2,624]{3,2,1,0:T(2,128)(2,1)S(1)}, bf16[2,3,2,624]{3,2,1,0:T(2,128)(2,1)S(1)}, u32[]{:S(2)}, u32[]{:S(2)}) %collective-permute-start.4) | collective-permute-done | bytes 15008 | tf_op jit(solution)/shard_map/ppermute | solution.py:90
  (55 shorter events, 11.1 us)
Async XLA Ops:
  0.0 10.7 %copy-start.4 = (bf16[384,12]{0,1:T(8,128)(2,1)S(1)}, bf16[384,12]{0,1:T(8,128)(2,1)}, u32[]{:S(2)}) copy-start(bf16[384,12]{0,1:T(8,128)(2,1)} %param.9) | copy-start | bytes 27652
  0.0 11.3 %copy-start.1 = (bf16[432,384]{1,0:T(8,128)(2,1)S(1)}, bf16[432,384]{1,0:T(8,128)(2,1)}, u32[]{:S(2)}) copy-start(bf16[432,384]{1,0:T(8,128)(2,1)} %param.7) | copy-start | bytes 995332
  1.9 1.7 %collective-permute-start = (bf16[12,2,3,1664]{3,0,2,1:T(8,128)(2,1)S(1)}, bf16[12,2,3,1664]{3,0,2,1:T(8,128)(2,1)S(1)}, u32[]{:S(2)}, u32[]{:S(2)}) collective-permute-start(bf16[12,2,3,1664]{3,0,2,1:T(8,128)(2,1)S(1)} %pad_dynamic-slice_fusion), channel_id=1, source_target_pairs={{0,1},{1,0},{2,3},{3,2},{4,5},{5,4},{6,7},{7,6},{8,9},{9,8},{10,11... | collective-permute-start | bytes 718856 | tf_op jit(solution)/shard_map/ppermute | solution.py:32
  3.9 6.2 %collective-permute-start.1 = (bf16[8,2,3,1664]{3,0,2,1:T(8,128)(2,1)S(1)}, bf16[8,2,3,1664]{3,0,2,1:T(8,128)(2,1)S(1)}, u32[]{:S(2)}, u32[]{:S(2)}) collective-permute-start(bf16[8,2,3,1664]{3,0,2,1:T(8,128)(2,1)S(1)} %constant_dynamic-slice_fusion.2), channel_id=1, source_target_pairs={{0,2},{1,3},{2,0},{3,1},{4,6},{5,7},{6,4},{7,5},{8,10},{9,11},{10,... | collective-permute-start | bytes 479240 | tf_op jit(solution)/shard_map/ppermute | solution.py:32
  10.2 5.4 %collective-permute-start.2 = (bf16[6,2,3,1664]{3,0,2,1:T(8,128)(2,1)S(1)}, bf16[6,2,3,1664]{3,0,2,1:T(8,128)(2,1)S(1)}, u32[]{:S(2)}, u32[]{:S(2)}) collective-permute-start(bf16[6,2,3,1664]{3,0,2,1:T(8,128)(2,1)S(1)} %constant_dynamic-slice_fusion.1), channel_id=1, source_target_pairs={{0,4},{1,5},{2,6},{3,7},{4,0},{5,1},{6,2},{7,3},{8,12},{9,13},{10,... | collective-permute-start | bytes 359432 | tf_op jit(solution)/shard_map/ppermute | solution.py:32
  15.7 8.4 %collective-permute-start.3 = (bf16[5,2,3,1664]{3,0,2,1:T(8,128)(2,1)S(1)}, bf16[5,2,3,1664]{3,0,2,1:T(8,128)(2,1)S(1)}, u32[]{:S(2)}, u32[]{:S(2)}) collective-permute-start(bf16[5,2,3,1664]{3,0,2,1:T(8,128)(2,1)S(1)} %constant_dynamic-slice_fusion), channel_id=1, source_target_pairs={{0,8},{1,9},{2,10},{3,11},{4,12},{5,13},{6,14},{7,15},{8,0},{9,1},... | collective-permute-start | bytes 299528 | tf_op jit(solution)/shard_map/ppermute | solution.py:32
  27.0 1.0 %copy-start.2 = (bf16[3,3,3,16,384]{4,3,2,1,0:T(8,128)(2,1)S(1)}, bf16[3,3,3,16,384]{4,3,2,1,0:T(8,128)(2,1)}, u32[]{:S(2)}) copy-start(bf16[3,3,3,16,384]{4,3,2,1,0:T(8,128)(2,1)} %copy.24) | copy-start | bytes 995332
  27.0 1.0 %copy-start.6 = (pred[48,14]{0,1:T(8,128)(4,1)S(1)}, pred[48,14]{0,1:T(8,128)(4,1)}, u32[]{:S(2)}) copy-start(pred[48,14]{0,1:T(8,128)(4,1)} %constant.61) | copy-start | bytes 2020
  45.3 2.2 %slice-start = ((s8[7962624]{0:T(1024)(128)(4,1)}), s8[4194304]{0:T(1024)(128)(4,1)S(1)}, s32[]{:S(2)}) async-start(s8[7962624]{0:T(1024)(128)(4,1)} %bitcast.87), calls=%async_computation | async-start | bytes 8388608
  46.3 2.6 %slice-start.1 = ((s8[7962624]{0:T(1024)(128)(4,1)}), s8[3768320]{0:T(1024)(128)(4,1)S(1)}, s32[]{:S(2)}) async-start(s8[7962624]{0:T(1024)(128)(4,1)} %bitcast.87), calls=%async_computation.1 | async-start | bytes 7536640
  46.5 2.4 %copy-start.5 = (pred[8,14]{0,1:T(8,128)(4,1)S(1)}, pred[8,14]{0,1:T(8,128)(4,1)}, u32[]{:S(2)}) copy-start(pred[8,14]{0,1:T(8,128)(4,1)} %constant.62) | copy-start | bytes 340
  56.2 1.2 %copy-start = (f32[1,48,14,384]{3,0,2,1:T(1,128)S(1)}, f32[1,48,14,384]{3,0,2,1:T(1,128)}, u32[]{:S(2)}) copy-start(f32[1,48,14,384]{3,0,2,1:T(1,128)} %copy.25) | copy-start | bytes 3096580
  62.5 1.3 %copy-start.3 = (bf16[2,2,3,384,1,1]{3,2,1,0,4,5:T(4,128)(2,1)S(1)}, bf16[2,2,3,384,1,1]{3,2,1,0,4,5:T(4,128)(2,1)}, u32[]{:S(2)}) copy-start(bf16[2,2,3,384,1,1]{3,2,1,0,4,5:T(4,128)(2,1)} %reshape.91) | copy-start | bytes 27652
  65.3 7.7 %collective-permute-start.4 = (bf16[2,3,2,624]{3,2,1,0:T(2,128)(2,1)S(1)}, bf16[2,3,2,624]{3,2,1,0:T(2,128)(2,1)S(1)}, u32[]{:S(2)}, u32[]{:S(2)}) collective-permute-start(bf16[2,3,2,624]{3,2,1,0:T(2,128)(2,1)S(1)} %convert_element_type.29), channel_id=1, source_target_pairs={{0,0},{1,8},{2,4},{3,12},{4,2},{5,10},{6,6},{7,14},{8,1},{9,9},{10... | collective-permute-start | bytes 44936 | tf_op jit(solution)/shard_map/ppermute | solution.py:90

commit v7 on v4

--- a/solution.py
+++ b/solution.py
@@ -64,25 +64,29 @@
     x = jnp.pad(x, ((HALO, HALO), (0, 0), (0, 0), (0, 0)))
     x = gather_rows(x, n, rows_dev, slot)
 
-    window = jnp.transpose(x, (1, 2, 0, 3)).reshape(groups * frames, rows_dev + 2 * HALO, columns, ZC)
     steps = groups * frames
     rows_in = rows_dev + 2
-    padded = jnp.pad(window, ((2, 0), (0, 0), (1, 1), (0, 0)))
+    window = x.reshape(rows_dev + 2 * HALO, steps, columns, ZC).transpose(1, 0, 3, 2)
+    window = jnp.pad(window, ((2, 0), (0, 0), (0, 0), (1, 1)))
     pieces = [
-        padded[a : a + steps, b : b + rows_in, e : e + columns]
+        window[a : a + steps, b : b + rows_in, :, e : e + columns]
         for a in range(3)
         for b in range(3)
         for e in range(3)
     ]
-    xcol = jnp.concatenate(pieces, axis=-1).reshape(-1, 27 * ZC)
-    first_act = jnp.dot(xcol, conv_in, preferred_element_type=jnp.float32)
-    first_act = first_act.reshape(steps, rows_in, columns, channels)
-    activated = jax.nn.silu(rms_scale(first_act)).astype(jnp.bfloat16)
+    xcol = jnp.concatenate(pieces, axis=2)
+    first_cm = lax.dot_general(
+        conv_in, xcol, (((0,), (2,)), ((), ())), preferred_element_type=jnp.float32
+    )
+    scale = lax.rsqrt(jnp.mean(first_cm * first_cm, axis=0, keepdims=True) + epsilon)
+    activated = jax.nn.silu(first_cm * scale).astype(jnp.bfloat16)
+    activated = jnp.transpose(activated, (1, 2, 3, 0))
+    first_act = jnp.transpose(first_cm[:, :, 1 : 1 + rows_dev], (1, 2, 3, 0))
     row_of = slot * rows_dev - 1 + jnp.arange(rows_dev + 2)
     inside = (row_of >= 0) & (row_of < height)
     activated = jnp.where(inside[None, :, None, None], activated, jnp.zeros_like(activated))
     second_act = causal_conv(activated, conv_mid, channels)
-    summed = first_act[:, 1 : 1 + rows_dev] + second_act
+    summed = first_act + second_act
     normed = rms_scale(summed).astype(jnp.bfloat16)
     projected = jnp.dot(normed.reshape(-1, channels), to_pixels, preferred_element_type=jnp.float32)
     projected = projected.reshape(groups, frames, rows_dev, columns, 2, 2, 3).transpose(0, 1, 2, 4, 3, 5, 6)

time: 69.7 us -> 69.7 us (level)
  no operation moved by 1% of the time
where the time goes in v7:
time: 69.7 us; the launch traced here: 68.5 us
  local copies, waits for them, and re-layouts  26.3 us (38%)
  waiting for transfers between devices  24.9 us (36%)
  matrix products  9 us (13%)
  starting transfers between devices  4.46 us (6%)
  other arithmetic  3.6 us (5%)
    ppermute x4, waiting for transfers between devices, gather_rows(): x = own + lax.ppermute(send, 'dev', pairs)  19.1 us
    concatenate x1, local copies, waits for them, and re-layouts, local(): xcol = jnp.concatenate(pieces, axis=2)  11.7 us
    conv_general_dilated x1, matrix products, causal_conv(): lax.conv_general_dilated(padded[None], kernel, window_strides=(1, 1, 1),...  7.41 us
    slice x2, local copies, waits for them, and re-layouts, local(): window[a:a + steps, b:b + rows_in, :, e:e + columns]  6.4 us
    ppermute x1, waiting for transfers between devices, local(): lax.ppermute(pixels, 'dev', [(i, reverse_bits(i, bits)) for i in range(n)])  5.82 us
    unnamed x12, local copies, waits for them, and re-layouts  2.85 us
    ppermute x4, starting transfers between devices, gather_rows(): x = own + lax.ppermute(send, 'dev', pairs)  2.54 us
    conv_general_dilated x4, local copies, waits for them, and re-layouts, causal_conv(): lax.conv_general_dilated(padded[None], kernel, window_strides=(1, 1, 1),...  2.47 us
  transfers between devices with their start and end apart: 5, of which 5 were waited for; matrix products, arithmetic and copies ran while one was open for 0% of the time, Pallas kernels for 0%

profile of v7, /device:TPU:24, one launch (start us, length us, event | category | flops | bytes accessed | tf_op | source)
XLA Modules:
  0.0 68.5 jit_solution(13883880185090431355)
XLA Ops:
  0.0 0.7 %broadcast_compare_fusion = pred[2]{0:T(512)(128)(4,1)S(1)} fusion(s32[2]{0:T(128)} %param.6, s32[]{:T(128)S(6)} %axis_index.12), kind=kLoop, calls=%fused_computation.62 | loop fusion | flops 2 | bytes 14 | tf_op jit(solution)/shard_map/eq | solution.py:62
  0.7 1.1 %fusion.18 = bf16[16,2,3,1664]{3,0,2,1:T(8,128)(2,1)S(1)} fusion(bf16[1,2,3,16,1664]{4,3,2,1,0:T(8,128)(2,1)} %param.5, pred[2]{0:T(512)(128)(4,1)S(1)} %broadcast_compare_fusion), kind=kLoop, calls=%fused_computation.51 | loop fusion | flops 159744 | bytes 638978 | tf_op jit(solution)/shard_map/jit(_where)/select_n | solution.py:63
  2.0 1.6 %collective-permute-done = bf16[12,2,3,1664]{3,0,2,1:T(8,128)(2,1)S(1)} collective-permute-done((bf16[12,2,3,1664]{3,0,2,1:T(8,128)(2,1)S(1)}, bf16[12,2,3,1664]{3,0,2,1:T(8,128)(2,1)S(1)}, u32[]{:S(2)}, u32[]{:S(2)}) %collective-permute-start) | collective-permute-done | bytes 239648 | tf_op jit(solution)/shard_map/ppermute | solution.py:32
  3.9 1.6 %collective-permute-start.1 = (bf16[8,2,3,1664]{3,0,2,1:T(8,128)(2,1)S(1)}, bf16[8,2,3,1664]{3,0,2,1:T(8,128)(2,1)S(1)}, u32[]{:S(2)}, u32[]{:S(2)}) collective-permute-start(bf16[8,2,3,1664]{3,0,2,1:T(8,128)(2,1)S(1)} %constant_dynamic-slice_fusion.2), channel_id=1, source_target_pairs={{0,2},{1,3},{2,0},{3,1},{4,6},{5,7},{6,4},{7,5},{8,10},{9,11},{10,... | collective-permute-start | bytes 479240 | tf_op jit(solution)/shard_map/ppermute | solution.py:32
  5.4 4.7 %collective-permute-done.1 = bf16[8,2,3,1664]{3,0,2,1:T(8,128)(2,1)S(1)} collective-permute-done((bf16[8,2,3,1664]{3,0,2,1:T(8,128)(2,1)S(1)}, bf16[8,2,3,1664]{3,0,2,1:T(8,128)(2,1)S(1)}, u32[]{:S(2)}, u32[]{:S(2)}) %collective-permute-start.1) | collective-permute-done | bytes 159776 | tf_op jit(solution)/shard_map/ppermute | solution.py:32
  10.2 0.5 collective-permute-start.2
  10.8 4.8 %collective-permute-done.2 = bf16[6,2,3,1664]{3,0,2,1:T(8,128)(2,1)S(1)} collective-permute-done((bf16[6,2,3,1664]{3,0,2,1:T(8,128)(2,1)S(1)}, bf16[6,2,3,1664]{3,0,2,1:T(8,128)(2,1)S(1)}, u32[]{:S(2)}, u32[]{:S(2)}) %collective-permute-start.2) | collective-permute-done | bytes 119840 | tf_op jit(solution)/shard_map/ppermute | solution.py:32
  16.1 8.0 %collective-permute-done.3 = bf16[5,2,3,1664]{3,0,2,1:T(8,128)(2,1)S(1)} collective-permute-done((bf16[5,2,3,1664]{3,0,2,1:T(8,128)(2,1)S(1)}, bf16[5,2,3,1664]{3,0,2,1:T(8,128)(2,1)S(1)}, u32[]{:S(2)}, u32[]{:S(2)}) %collective-permute-start.3) | collective-permute-done | bytes 99872 | tf_op jit(solution)/shard_map/ppermute | solution.py:32
  24.2 0.6 reshape.68
  24.8 4.3 %pad_slice_fusion = (bf16[6,3,16,104]{2,3,1,0:T(8,128)(2,1)S(1)}, bf16[6,3,16,104]{2,3,1,0:T(8,128)(2,1)S(1)}, bf16[6,3,16,104]{2,3,1,0:T(8,128)(2,1)}, bf16[6,3...) fusion(bf16[6,5,16,104]{2,3,1,0:T(8,128)(2,1)S(1)} %bitcast.64), kind=kLoop, calls=%fused_computation.11 | loop fusion | bytes 1238016 | tf_op jit(solution)/shard_map/slice | solution.py:72
  29.1 2.1 %fusion.23 = (bf16[6,3,16,104]{2,3,1,0:T(8,128)(2,1)}, bf16[6,3,16,104]{2,3,1,0:T(8,128)(2,1)}, bf16[6,3,16,104]{2,3,1,0:T(8,128)(2,1)}, bf16[6,3,16,104]{2,3,1,...) fusion(bf16[6,5,16,104]{2,3,1,0:T(8,128)(2,1)S(1)} %bitcast.65), kind=kLoop, calls=%fused_computation.66 | loop fusion | bytes 2715648 | tf_op jit(solution)/shard_map/slice | solution.py:72
  31.2 11.7 %concatenate.3 = bf16[6,3,432,104]{2,3,1,0:T(8,128)(2,1)S(1)} concatenate(bf16[6,3,16,104]{2,3,1,0:T(8,128)(2,1)} %get-tuple-element.31, bf16[6,3,16,104]{2,3,1,0:T(8,128)(2,1)S(1)} %get-tuple-element.6, bf16[6,3,16,104]{2,3,1,0:T(8,128)(2,1)} %get-tuple-element.7, bf16[6,3,16,104]{2,3,1,0:T(8,128)(2,1)} %get-tuple-element.8, bf16[6,3,16,104]{2,3,1,0:T(8,128)(2,1)} %get-tuple-element.9, ...), dimensions={2} | concatenate | bytes 3234816 | tf_op jit(solution)/shard_map/concatenate | solution.py:77
  42.9 1.3 %multiply_reduce_fusion = (f32[6,3,104]{2,1,0:T(4,128)S(1)}, f32[6,3,104,384]{3,2,1,0:T(8,128)S(1)}) fusion(bf16[6,3,432,104]{2,3,1,0:T(8,128)(2,1)S(1)} %concatenate.3, bf16[432,384]{1,0:T(8,128)(2,1)S(1)} %copy-done), kind=kOutput, calls=%fused_computation.3 | convolution fusion | flops 622520512 | bytes 4832064 | tf_op jit(solution)/shard_map/dot_general | solution.py:78
  44.2 0.9 %fusion.8 = bf16[6,3,104,384]{3,2,1,0:T(8,128)(2,1)S(1)} fusion(f32[6,3,104,384]{3,2,1,0:T(8,128)S(1)} %get-tuple-element.33, f32[6,3,104]{2,1,0:T(4,128)S(1)} %add_rsqrt_fusion, pred[3]{0:T(512)(128)(4,1)S(1)} %compare_and_fusion), kind=kLoop, calls=%fused_computation.35 | loop fusion | flops 5031936 | bytes 4320579 | tf_op jit(solution)/shard_map/jit(_where)/select_n | solution.py:87
  45.2 0.6 pad_bitcast_fusion
  47.3 1.4 %slice-done.1 = s8[3768320]{0:T(1024)(128)(4,1)S(1)} async-done(((s8[7962624]{0:T(1024)(128)(4,1)}), s8[3768320]{0:T(1024)(128)(4,1)S(1)}, s32[]{:S(2)}) %slice-start.1) | async-done | bytes 3768344
  48.7 7.4 %fusion.9 = f32[6,1,8,14,384]{4,2,3,1,0:T(8,128)S(1)} fusion(bf16[3,3,3,384,384]{4,3,2,1,0:T(8,128)(2,1)S(1)} %bitcast.72, bf16[8,3,1,7,2,384]{5,3,4,1,0,2:T(8,128)(2,1)S(1)} %slice.121, bf16[8,3,1,8,14,384]{5,3,4,1,0,2:T(8,128)(2,1)S(1)} %copy.13, pred[8,14]{0,1:T(8,128)(4,1)S(1)} %copy-done.2), kind=kOutput, calls=%fused_computation.36 | convolution fusion | flops 5358219264 | bytes 11317360 | tf_op jit(solution)/shard_map/conv_general_dilated | solution.py:39
  56.2 1.3 %copy.14 = f32[6,1,8,14,384]{4,1,3,2,0:T(1,128)S(1)} copy(f32[6,1,8,14,384]{4,2,3,1,0:T(8,128)S(1)} %fusion.9) | data formatting | bytes 2064384 | tf_op jit(solution)/shard_map/conv_general_dilated | solution.py:39
  57.4 0.7 slice.122
  58.9 0.5 copy.16
  59.5 0.7 %convert_element_type.30 = bf16[2,3,2,624]{3,2,1,0:T(2,128)(2,1)S(1)} reshape(bf16[2,3,1,2,104,2,3]{6,5,4,3,1,0,2:T(2,128)(2,1)S(1)} %copy.16) | data formatting | bytes 29952 | tf_op jit(solution)/shard_map/convert_element_type | solution.py:93
  60.2 1.9 %collective-permute-start.4 = (bf16[2,3,2,624]{3,2,1,0:T(2,128)(2,1)S(1)}, bf16[2,3,2,624]{3,2,1,0:T(2,128)(2,1)S(1)}, u32[]{:S(2)}, u32[]{:S(2)}) collective-permute-start(bf16[2,3,2,624]{3,2,1,0:T(2,128)(2,1)S(1)} %convert_element_type.30), channel_id=1, source_target_pairs={{0,0},{1,8},{2,4},{3,12},{4,2},{5,10},{6,6},{7,14},{8,1},{9,9},{10... | collective-permute-start | bytes 44936 | tf_op jit(solution)/shard_map/ppermute | solution.py:94
  62.1 5.8 %collective-permute-done.4 = bf16[2,3,2,624]{3,2,1,0:T(2,128)(2,1)S(1)} collective-permute-done((bf16[2,3,2,624]{3,2,1,0:T(2,128)(2,1)S(1)}, bf16[2,3,2,624]{3,2,1,0:T(2,128)(2,1)S(1)}, u32[]{:S(2)}, u32[]{:S(2)}) %collective-permute-start.4) | collective-permute-done | bytes 15008 | tf_op jit(solution)/shard_map/ppermute | solution.py:94
  67.9 0.6 copy.31
  (31 shorter events, 3.6 us)
Async XLA Ops:
  0.0 42.9 %copy-start = (bf16[432,384]{1,0:T(8,128)(2,1)S(1)}, bf16[432,384]{1,0:T(8,128)(2,1)}, u32[]{:S(2)}) copy-start(bf16[432,384]{1,0:T(8,128)(2,1)} %param.7) | copy-start | bytes 995332
  0.0 10.7 %copy-start.1 = (bf16[384,12]{0,1:T(8,128)(2,1)S(1)}, bf16[384,12]{0,1:T(8,128)(2,1)}, u32[]{:S(2)}) copy-start(bf16[384,12]{0,1:T(8,128)(2,1)} %param.9) | copy-start | bytes 27652
  1.9 1.7 %collective-permute-start = (bf16[12,2,3,1664]{3,0,2,1:T(8,128)(2,1)S(1)}, bf16[12,2,3,1664]{3,0,2,1:T(8,128)(2,1)S(1)}, u32[]{:S(2)}, u32[]{:S(2)}) collective-permute-start(bf16[12,2,3,1664]{3,0,2,1:T(8,128)(2,1)S(1)} %pad_dynamic-slice_fusion), channel_id=1, source_target_pairs={{0,1},{1,0},{2,3},{3,2},{4,5},{5,4},{6,7},{7,6},{8,9},{9,8},{10,11... | collective-permute-start | bytes 718856 | tf_op jit(solution)/shard_map/ppermute | solution.py:32
  3.9 6.2 %collective-permute-start.1 = (bf16[8,2,3,1664]{3,0,2,1:T(8,128)(2,1)S(1)}, bf16[8,2,3,1664]{3,0,2,1:T(8,128)(2,1)S(1)}, u32[]{:S(2)}, u32[]{:S(2)}) collective-permute-start(bf16[8,2,3,1664]{3,0,2,1:T(8,128)(2,1)S(1)} %constant_dynamic-slice_fusion.2), channel_id=1, source_target_pairs={{0,2},{1,3},{2,0},{3,1},{4,6},{5,7},{6,4},{7,5},{8,10},{9,11},{10,... | collective-permute-start | bytes 479240 | tf_op jit(solution)/shard_map/ppermute | solution.py:32
  10.2 5.4 %collective-permute-start.2 = (bf16[6,2,3,1664]{3,0,2,1:T(8,128)(2,1)S(1)}, bf16[6,2,3,1664]{3,0,2,1:T(8,128)(2,1)S(1)}, u32[]{:S(2)}, u32[]{:S(2)}) collective-permute-start(bf16[6,2,3,1664]{3,0,2,1:T(8,128)(2,1)S(1)} %constant_dynamic-slice_fusion.1), channel_id=1, source_target_pairs={{0,4},{1,5},{2,6},{3,7},{4,0},{5,1},{6,2},{7,3},{8,12},{9,13},{10,... | collective-permute-start | bytes 359432 | tf_op jit(solution)/shard_map/ppermute | solution.py:32
  15.7 8.4 %collective-permute-start.3 = (bf16[5,2,3,1664]{3,0,2,1:T(8,128)(2,1)S(1)}, bf16[5,2,3,1664]{3,0,2,1:T(8,128)(2,1)S(1)}, u32[]{:S(2)}, u32[]{:S(2)}) collective-permute-start(bf16[5,2,3,1664]{3,0,2,1:T(8,128)(2,1)S(1)} %constant_dynamic-slice_fusion), channel_id=1, source_target_pairs={{0,8},{1,9},{2,10},{3,11},{4,12},{5,13},{6,14},{7,15},{8,0},{9,1},... | collective-permute-start | bytes 299528 | tf_op jit(solution)/shard_map/ppermute | solution.py:32
  45.2 2.2 %slice-start = ((s8[7962624]{0:T(1024)(128)(4,1)}), s8[4194304]{0:T(1024)(128)(4,1)S(1)}, s32[]{:S(2)}) async-start(s8[7962624]{0:T(1024)(128)(4,1)} %bitcast.70), calls=%async_computation | async-start | bytes 8388608
  46.2 2.6 %slice-start.1 = ((s8[7962624]{0:T(1024)(128)(4,1)}), s8[3768320]{0:T(1024)(128)(4,1)S(1)}, s32[]{:S(2)}) async-start(s8[7962624]{0:T(1024)(128)(4,1)} %bitcast.70), calls=%async_computation.1 | async-start | bytes 7536640
  46.4 2.4 %copy-start.2 = (pred[8,14]{0,1:T(8,128)(4,1)S(1)}, pred[8,14]{0,1:T(8,128)(4,1)}, u32[]{:S(2)}) copy-start(pred[8,14]{0,1:T(8,128)(4,1)} %constant.57) | copy-start | bytes 340
  60.2 7.7 %collective-permute-start.4 = (bf16[2,3,2,624]{3,2,1,0:T(2,128)(2,1)S(1)}, bf16[2,3,2,624]{3,2,1,0:T(2,128)(2,1)S(1)}, u32[]{:S(2)}, u32[]{:S(2)}) collective-permute-start(bf16[2,3,2,624]{3,2,1,0:T(2,128)(2,1)S(1)} %convert_element_type.30), channel_id=1, source_target_pairs={{0,0},{1,8},{2,4},{3,12},{4,2},{5,10},{6,6},{7,14},{8,1},{9,9},{10... | collective-permute-start | bytes 44936 | tf_op jit(solution)/shard_map/ppermute | solution.py:94

commit v8 on v1

--- a/solution.py
+++ b/solution.py
@@ -15,17 +15,28 @@
     return values * lax.rsqrt(jnp.mean(values * values, axis=-1, keepdims=True) + epsilon)
 
 
-def gather_rows(x, n, rows_dev, position):
+def scatter_rows(x, n, position):
     bits = n.bit_length() - 1
-    for k in reversed(range(bits)):
-        half = (1 << k) * rows_dev
-        size = half + 2 * HALO
+    for k in range(bits):
         bit = (position >> k) & 1
-        own = lax.dynamic_slice_in_dim(x, bit * half, size, 0)
-        send = lax.dynamic_slice_in_dim(x, (1 - bit) * half, size, 0)
+        split = x.reshape((x.shape[0] // 2, 2) + x.shape[1:])
+        low, high = split[:, 0], split[:, 1]
+        own = jnp.where(bit == 1, high, low)
+        send = jnp.where(bit == 1, low, high)
         pairs = [(i, i ^ (1 << k)) for i in range(n)]
         x = own + lax.ppermute(send, "dev", pairs)
-    return x
+    return x[0]
+
+
+def with_halo(block, n, halo):
+    rows_dev = block.shape[0]
+    reach = -(-halo // rows_dev)
+    below, above = [], []
+    for d in range(1, reach + 1):
+        below.insert(0, lax.ppermute(block, "dev", [(i, i + d) for i in range(n - d)]))
+        above.append(lax.ppermute(block, "dev", [(i + d, i) for i in range(n - d)]))
+    joined = jnp.concatenate(below + [block] + above, axis=0)
+    return joined[reach * rows_dev - halo : (reach + 1) * rows_dev + halo]
 
 
 def causal_conv(source, weights, channels):
@@ -50,12 +61,11 @@
     columns = width // ZC
     channels = conv_mid.shape[1]
     rows_dev = height // n
-
     x = jnp.transpose(latents[0], (2, 0, 1, 3))
     keep = owners == position
     x = jnp.where(keep[None, :, None, None], x, jnp.zeros_like(x))
-    x = jnp.pad(x, ((HALO, HALO), (0, 0), (0, 0), (0, 0)))
-    x = gather_rows(x, n, rows_dev, position)
+    x = scatter_rows(x.reshape((n, rows_dev) + x.shape[1:]), n, position)
+    x = with_halo(x, n, HALO)
 
     window = jnp.transpose(x, (1, 2, 0, 3)).reshape(groups * frames, rows_dev + 2 * HALO, columns, ZC)
     first_act = causal_conv(window, conv_in, ZC)
@@ -68,7 +78,8 @@
     normed = rms_scale(summed).astype(jnp.bfloat16)
     projected = jnp.dot(normed.reshape(-1, channels), to_pixels, preferred_element_type=jnp.float32)
     projected = projected.reshape(groups, frames, rows_dev, columns, 2, 2, 3).transpose(0, 1, 2, 4, 3, 5, 6)
-    return projected.reshape(groups, frames, 2 * rows_dev, 6 * columns).astype(jnp.bfloat16)
+    pixels = projected.reshape(groups, frames, 2 * rows_dev, 6 * columns).astype(jnp.bfloat16)
+    return pixels
 
 
 def solution(mesh):

time: 60.7 us -> 61.3 us (level); the launches traced: 59.7 us -> 61 us
  starting transfers between devices: 2.1 us -> 14.8 us
  waiting for transfers between devices: 27.7 us -> 15.4 us
    ppermute x4 -> x8, starting transfers between devices: 2.1 us -> 14.8 us  [the longest x2 6.98 us: with_halo(): above.append(lax.ppermute(block, 'dev', [(i + d, i) for i in range(n - d)]))]
    ppermute x4 -> x8, waiting for transfers between devices: 27.7 us -> 15.4 us  [the longest x4 12.3 us: scatter_rows(): x = own + lax.ppermute(send, 'dev', pairs)]
    unnamed x11 -> x15, local copies, waits for them, and re-layouts: 2.26 us -> 2.36 us
  transfers between devices with their start and end apart: 4 -> 8, of which waited for: 4 -> 5; matrix products, arithmetic and copies ran while one was open for 0% -> 0% of each run, Pallas kernels for 0% -> 0%
where the time goes in v8:
time: 61.3 us; the launch traced here: 61 us
  waiting for transfers between devices  15.4 us (25%)
  local copies, waits for them, and re-layouts  15.3 us (25%)
  starting transfers between devices  14.8 us (24%)
  matrix products  10.7 us (17%)
  other arithmetic  4.36 us (7%)
    ppermute x4, waiting for transfers between devices, scatter_rows(): x = own + lax.ppermute(send, 'dev', pairs)  12.3 us
    conv_general_dilated x2, matrix products, causal_conv(): lax.conv_general_dilated(padded[None], kernel, window_strides=(1, 1, 1),...  10.3 us
    conv_general_dilated x9, local copies, waits for them, and re-layouts, causal_conv(): lax.conv_general_dilated(padded[None], kernel, window_strides=(1, 1, 1),...  8.41 us
    ppermute x2, starting transfers between devices, with_halo(): above.append(lax.ppermute(block, 'dev', [(i + d, i) for i in range(n - d)]))  6.98 us
    ppermute x2, starting transfers between devices, with_halo(): lax.ppermute(block, 'dev', [(i, i + d) for i in range(n - d)])  5.32 us
    ppermute x2, waiting for transfers between devices, with_halo(): above.append(lax.ppermute(block, 'dev', [(i + d, i) for i in range(n - d)]))  3.08 us
    ppermute x4, starting transfers between devices, scatter_rows(): x = own + lax.ppermute(send, 'dev', pairs)  2.54 us
    unnamed x15, local copies, waits for them, and re-layouts  2.36 us
  transfers between devices with their start and end apart: 8, of which 5 were waited for; matrix products, arithmetic and copies ran while one was open for 0% of the time, Pallas kernels for 0%

profile of v8, /device:TPU:24, one launch (start us, length us, event | category | flops | bytes accessed | tf_op | source)
XLA Modules:
  0.0 61.0 jit_solution(6280249003052097689)
XLA Ops:
  0.0 0.7 %broadcast_compare_fusion = pred[2]{0:T(512)(128)(4,1)S(1)} fusion(s32[2]{0:T(128)} %param.6, s32[]{:T(128)S(6)} %axis_index.12), kind=kLoop, calls=%fused_computation.61 | loop fusion | flops 2 | bytes 14 | tf_op jit(solution)/shard_map/eq | solution.py:65
  0.7 1.1 %fusion.22 = bf16[16,2,3,1664]{3,0,2,1:T(8,128)(2,1)S(1)} fusion(bf16[1,2,3,16,1664]{4,3,2,1,0:T(8,128)(2,1)} %param.5, pred[2]{0:T(512)(128)(4,1)S(1)} %broadcast_compare_fusion), kind=kLoop, calls=%fused_computation.32 | loop fusion | flops 159744 | bytes 638978 | tf_op jit(solution)/shard_map/jit(_where)/select_n | solution.py:66
  2.3 1.4 %collective-permute-done = bf16[8,1,2,3,1664]{4,2,3,0,1:T(2,128)(2,1)S(1)} collective-permute-done((bf16[8,1,2,3,1664]{4,2,3,0,1:T(2,128)(2,1)S(1)}, bf16[8,1,2,3,1664]{4,2,3,0,1:T(2,128)(2,1)S(1)}, u32[]{:S(2)}, u32[]{:S(2)}) %collective-permute-start) | collective-permute-done | bytes 159776 | tf_op jit(solution)/shard_map/ppermute | solution.py:27
  4.1 1.6 %collective-permute-start.1 = (bf16[4,1,2,3,1664]{4,0,3,2,1:T(4,128)(2,1)S(1)}, bf16[4,1,2,3,1664]{4,0,3,2,1:T(4,128)(2,1)S(1)}, u32[]{:S(2)}, u32[]{:S(2)}) collective-permute-start(bf16[4,1,2,3,1664]{4,0,3,2,1:T(4,128)(2,1)S(1)} %select_bitcast_fusion), channel_id=1, source_target_pairs={{0,2},{1,3},{2,0},{3,1},{4,6},{5,7},{6,4},{7,5},{8,10},{9,11},{10,... | collective-permute-start | bytes 239624 | tf_op jit(solution)/shard_map/ppermute | solution.py:27
  5.7 3.0 %collective-permute-done.1 = bf16[4,1,2,3,1664]{4,0,3,2,1:T(4,128)(2,1)S(1)} collective-permute-done((bf16[4,1,2,3,1664]{4,0,3,2,1:T(4,128)(2,1)S(1)}, bf16[4,1,2,3,1664]{4,0,3,2,1:T(4,128)(2,1)S(1)}, u32[]{:S(2)}, u32[]{:S(2)}) %collective-permute-start.1) | collective-permute-done | bytes 79904 | tf_op jit(solution)/shard_map/ppermute | solution.py:27
  9.5 3.5 %collective-permute-done.2 = bf16[2,1,2,3,1664]{4,2,3,0,1:T(2,128)(2,1)S(1)} collective-permute-done((bf16[2,1,2,3,1664]{4,2,3,0,1:T(2,128)(2,1)S(1)}, bf16[2,1,2,3,1664]{4,2,3,0,1:T(2,128)(2,1)S(1)}, u32[]{:S(2)}, u32[]{:S(2)}) %collective-permute-start.2) | collective-permute-done | bytes 39968 | tf_op jit(solution)/shard_map/ppermute | solution.py:27
  13.5 4.4 %collective-permute-done.3 = bf16[1,1,2,3,1664]{4,2,3,1,0:T(2,128)(2,1)S(1)} collective-permute-done((bf16[1,1,2,3,1664]{4,2,3,1,0:T(2,128)(2,1)S(1)}, bf16[1,1,2,3,1664]{4,2,3,1,0:T(2,128)(2,1)S(1)}, u32[]{:S(2)}, u32[]{:S(2)}) %collective-permute-start.3) | collective-permute-done | bytes 20000 | tf_op jit(solution)/shard_map/ppermute | solution.py:27
  18.0 3.4 %collective-permute-start.4 = (bf16[1,2,3,1664]{3,1,2,0:T(2,128)(2,1)S(1)}, bf16[1,2,3,1664]{3,1,2,0:T(2,128)(2,1)S(1)}, u32[]{:S(2)}, u32[]{:S(2)}) collective-permute-start(bf16[1,2,3,1664]{3,1,2,0:T(2,128)(2,1)S(1)} %fusion.32), channel_id=1, source_target_pairs={{0,2},{1,3},{2,4},{3,5},{4,6},{5,7},{6,8},{7,9},{8,10},{9,11},{10,... | collective-permute-start | bytes 59912 | tf_op jit(solution)/shard_map/ppermute | solution.py:36
  21.5 1.9 %collective-permute-start.5 = (bf16[1,2,3,1664]{3,1,2,0:T(2,128)(2,1)S(1)}, bf16[1,2,3,1664]{3,1,2,0:T(2,128)(2,1)S(1)}, u32[]{:S(2)}, u32[]{:S(2)}) collective-permute-start(bf16[1,2,3,1664]{3,1,2,0:T(2,128)(2,1)S(1)} %fusion.32), channel_id=1, source_target_pairs={{0,1},{1,2},{2,3},{3,4},{4,5},{5,6},{6,7},{7,8},{8,9},{9,10},{10,1... | collective-permute-start | bytes 59912 | tf_op jit(solution)/shard_map/ppermute | solution.py:36
  23.4 4.5 %collective-permute-start.6 = (bf16[1,2,3,1664]{3,1,2,0:T(2,128)(2,1)S(1)}, bf16[1,2,3,1664]{3,1,2,0:T(2,128)(2,1)S(1)}, u32[]{:S(2)}, u32[]{:S(2)}) collective-permute-start(bf16[1,2,3,1664]{3,1,2,0:T(2,128)(2,1)S(1)} %fusion.32), channel_id=1, source_target_pairs={{1,0},{2,1},{3,2},{4,3},{5,4},{6,5},{7,6},{8,7},{9,8},{10,9},{11,1... | collective-permute-start | bytes 59912 | tf_op jit(solution)/shard_map/ppermute | solution.py:37
  27.9 2.4 %collective-permute-start.7 = (bf16[1,2,3,1664]{3,1,2,0:T(2,128)(2,1)S(1)}, bf16[1,2,3,1664]{3,1,2,0:T(2,128)(2,1)S(1)}, u32[]{:S(2)}, u32[]{:S(2)}) collective-permute-start(bf16[1,2,3,1664]{3,1,2,0:T(2,128)(2,1)S(1)} %fusion.32), channel_id=1, source_target_pairs={{2,0},{3,1},{4,2},{5,3},{6,4},{7,5},{8,6},{9,7},{10,8},{11,9},{12,... | collective-permute-start | bytes 59912 | tf_op jit(solution)/shard_map/ppermute | solution.py:37
  30.5 3.1 %collective-permute-done.7 = bf16[1,2,3,1664]{3,1,2,0:T(2,128)(2,1)S(1)} collective-permute-done((bf16[1,2,3,1664]{3,1,2,0:T(2,128)(2,1)S(1)}, bf16[1,2,3,1664]{3,1,2,0:T(2,128)(2,1)S(1)}, u32[]{:S(2)}, u32[]{:S(2)}) %collective-permute-start.7) | collective-permute-done | bytes 20000 | tf_op jit(solution)/shard_map/ppermute | solution.py:37
  33.7 0.6 %reshape.239 = bf16[6,5,104,16]{3,2,0,1:T(8,128)(2,1)S(1)} reshape(bf16[2,3,5,1664]{3,1,0,2:T(4,128)(2,1)S(1)} %copy.44) | data formatting | bytes 199680 | tf_op jit(solution)/shard_map/reshape | solution.py:70
  35.7 2.9 %convolution_select_fusion = f32[6,3,8,14,384]{4,2,3,1,0:T(8,128)S(1)} fusion(bf16[3,3,3,16,384]{4,3,2,1,0:T(8,128)(2,1)S(1)} %bitcast.95, pred[8,14]{0,1:T(8,128)(4,1)S(1)} %copy-done.2, bf16[8,5,1,7,2,16]{5,3,4,1,0,2:T(8,128)(2,1)S(1)} %slice.48, bf16[8,5,1,8,14,16]{5,3,4,1,0,2:T(8,128)(2,1)S(1)} %copy.47), kind=kOutput, calls=%fused_computation.14 | convolution fusion | flops 670126080 | bytes 3589744 | tf_op jit(solution)/shard_map/conv_general_dilated | solution.py:45
  38.6 2.4 %copy.48 = f32[6,3,8,14,384]{4,3,2,1,0:T(8,128)} copy(f32[6,3,8,14,384]{4,2,3,1,0:T(8,128)S(1)} %convolution_select_fusion) | data formatting | bytes 6193152 | tf_op jit(solution)/shard_map/conv_general_dilated | solution.py:45
  41.0 3.0 %reshape.249 = f32[6,3,1,112,384]{4,3,1,0,2:T(8,128)S(1)} reshape(f32[6,3,8,14,384]{4,3,2,1,0:T(8,128)} %copy.48) | data formatting | bytes 6193152 | tf_op jit(solution)/shard_map/conv_general_dilated | solution.py:45
  44.6 0.9 %fusion.9 = bf16[6,3,104,384]{3,2,1,0:T(8,128)(2,1)S(1)} fusion(f32[6,3,104]{2,1,0:T(4,128)S(1)} %add_rsqrt_fusion, pred[3]{0:T(512)(128)(4,1)S(1)} %compare_and_fusion, f32[6,3,1,112,384]{4,3,1,0,2:T(8,128)S(1)} %reshape.249), kind=kLoop, calls=%fused_computation.15 | loop fusion | flops 5031936 | bytes 4320579 | tf_op jit(solution)/shard_map/jit(_where)/select_n | solution.py:75
  45.6 0.6 pad_bitcast_fusion
  47.8 1.4 %slice-done.1 = s8[3768320]{0:T(1024)(128)(4,1)S(1)} async-done(((s8[7962624]{0:T(1024)(128)(4,1)}), s8[3768320]{0:T(1024)(128)(4,1)S(1)}, s32[]{:S(2)}) %slice-start.1) | async-done | bytes 3768344
  49.1 7.4 %fusion.10 = f32[6,1,8,14,384]{4,2,3,1,0:T(8,128)S(1)} fusion(bf16[3,3,3,384,384]{4,3,2,1,0:T(8,128)(2,1)S(1)} %bitcast.106, bf16[8,3,1,7,2,384]{5,3,4,1,0,2:T(8,128)(2,1)S(1)} %slice.51, bf16[8,3,1,8,14,384]{5,3,4,1,0,2:T(8,128)(2,1)S(1)} %copy.51, pred[8,14]{0,1:T(8,128)(4,1)S(1)} %copy-done.2), kind=kOutput, calls=%fused_computation.16 | convolution fusion | flops 5358219264 | bytes 11317360 | tf_op jit(solution)/shard_map/conv_general_dilated | solution.py:45
  56.6 1.1 %copy.52 = f32[6,1,8,14,384]{4,1,3,2,0:T(1,128)S(1)} copy(f32[6,1,8,14,384]{4,2,3,1,0:T(8,128)S(1)} %fusion.10) | data formatting | bytes 2064384 | tf_op jit(solution)/shard_map/conv_general_dilated | solution.py:45
  57.6 0.7 %slice.52 = f32[6,1,1,104,384]{4,1,3,0,2:T(1,128)S(1)} slice(f32[6,1,1,112,384]{4,1,3,0,2:T(1,128)S(1)} %bitcast.97), slice={[0:6], [0:1], [0:1], [0:104], [0:384]} | slice | bytes 1916928 | tf_op jit(solution)/shard_map/conv_general_dilated | solution.py:45
  59.1 0.5 copy.54
  59.7 1.3 %convert_element_type.27 = bf16[2,3,2,624]{3,2,1,0:T(2,128)(2,1)} reshape(bf16[2,3,1,2,104,2,3]{6,5,4,3,1,0,2:T(2,128)(2,1)S(1)} %copy.54) | data formatting | bytes 29952 | tf_op jit(solution)/shard_map/convert_element_type | solution.py:81
  (52 shorter events, 6.7 us)
Async XLA Ops:
  0.0 35.6 %copy-start = (bf16[432,384]{1,0:T(8,128)(2,1)S(1)}, bf16[432,384]{1,0:T(8,128)(2,1)}, u32[]{:S(2)}) copy-start(bf16[432,384]{1,0:T(8,128)(2,1)} %param.7) | copy-start | bytes 995332
  0.0 21.4 %copy-start.1 = (bf16[384,12]{0,1:T(8,128)(2,1)S(1)}, bf16[384,12]{0,1:T(8,128)(2,1)}, u32[]{:S(2)}) copy-start(bf16[384,12]{0,1:T(8,128)(2,1)} %param.9) | copy-start | bytes 27652
  2.2 1.5 %collective-permute-start = (bf16[8,1,2,3,1664]{4,2,3,0,1:T(2,128)(2,1)S(1)}, bf16[8,1,2,3,1664]{4,2,3,0,1:T(2,128)(2,1)S(1)}, u32[]{:S(2)}, u32[]{:S(2)}) collective-permute-start(bf16[8,1,2,3,1664]{4,2,3,0,1:T(2,128)(2,1)S(1)} %fusion.25), channel_id=1, source_target_pairs={{0,1},{1,0},{2,3},{3,2},{4,5},{5,4},{6,7},{7,6},{8,9},{9,8},{10,11... | collective-permute-start | bytes 479240 | tf_op jit(solution)/shard_map/ppermute | solution.py:27
  4.1 4.5 %collective-permute-start.1 = (bf16[4,1,2,3,1664]{4,0,3,2,1:T(4,128)(2,1)S(1)}, bf16[4,1,2,3,1664]{4,0,3,2,1:T(4,128)(2,1)S(1)}, u32[]{:S(2)}, u32[]{:S(2)}) collective-permute-start(bf16[4,1,2,3,1664]{4,0,3,2,1:T(4,128)(2,1)S(1)} %select_bitcast_fusion), channel_id=1, source_target_pairs={{0,2},{1,3},{2,0},{3,1},{4,6},{5,7},{6,4},{7,5},{8,10},{9,11},{10,... | collective-permute-start | bytes 239624 | tf_op jit(solution)/shard_map/ppermute | solution.py:27
  8.9 4.1 %collective-permute-start.2 = (bf16[2,1,2,3,1664]{4,2,3,0,1:T(2,128)(2,1)S(1)}, bf16[2,1,2,3,1664]{4,2,3,0,1:T(2,128)(2,1)S(1)}, u32[]{:S(2)}, u32[]{:S(2)}) collective-permute-start(bf16[2,1,2,3,1664]{4,2,3,0,1:T(2,128)(2,1)S(1)} %fusion.29), channel_id=1, source_target_pairs={{0,4},{1,5},{2,6},{3,7},{4,0},{5,1},{6,2},{7,3},{8,12},{9,13},{10,... | collective-permute-start | bytes 119816 | tf_op jit(solution)/shard_map/ppermute | solution.py:27
  13.1 4.8 %collective-permute-start.3 = (bf16[1,1,2,3,1664]{4,2,3,1,0:T(2,128)(2,1)S(1)}, bf16[1,1,2,3,1664]{4,2,3,1,0:T(2,128)(2,1)S(1)}, u32[]{:S(2)}, u32[]{:S(2)}) collective-permute-start(bf16[1,1,2,3,1664]{4,2,3,1,0:T(2,128)(2,1)S(1)} %fusion.33), channel_id=1, source_target_pairs={{0,8},{1,9},{2,10},{3,11},{4,12},{5,13},{6,14},{7,15},{8,0},{9,1},... | collective-permute-start | bytes 59912 | tf_op jit(solution)/shard_map/ppermute | solution.py:27
  18.0 12.4 %collective-permute-start.4 = (bf16[1,2,3,1664]{3,1,2,0:T(2,128)(2,1)S(1)}, bf16[1,2,3,1664]{3,1,2,0:T(2,128)(2,1)S(1)}, u32[]{:S(2)}, u32[]{:S(2)}) collective-permute-start(bf16[1,2,3,1664]{3,1,2,0:T(2,128)(2,1)S(1)} %fusion.32), channel_id=1, source_target_pairs={{0,2},{1,3},{2,4},{3,5},{4,6},{5,7},{6,8},{7,9},{8,10},{9,11},{10,... | collective-permute-start | bytes 59912 | tf_op jit(solution)/shard_map/ppermute | solution.py:36
  21.5 9.0 %collective-permute-start.5 = (bf16[1,2,3,1664]{3,1,2,0:T(2,128)(2,1)S(1)}, bf16[1,2,3,1664]{3,1,2,0:T(2,128)(2,1)S(1)}, u32[]{:S(2)}, u32[]{:S(2)}) collective-permute-start(bf16[1,2,3,1664]{3,1,2,0:T(2,128)(2,1)S(1)} %fusion.32), channel_id=1, source_target_pairs={{0,1},{1,2},{2,3},{3,4},{4,5},{5,6},{6,7},{7,8},{8,9},{9,10},{10,1... | collective-permute-start | bytes 59912 | tf_op jit(solution)/shard_map/ppermute | solution.py:36
  23.4 7.1 %collective-permute-start.6 = (bf16[1,2,3,1664]{3,1,2,0:T(2,128)(2,1)S(1)}, bf16[1,2,3,1664]{3,1,2,0:T(2,128)(2,1)S(1)}, u32[]{:S(2)}, u32[]{:S(2)}) collective-permute-start(bf16[1,2,3,1664]{3,1,2,0:T(2,128)(2,1)S(1)} %fusion.32), channel_id=1, source_target_pairs={{1,0},{2,1},{3,2},{4,3},{5,4},{6,5},{7,6},{8,7},{9,8},{10,9},{11,1... | collective-permute-start | bytes 59912 | tf_op jit(solution)/shard_map/ppermute | solution.py:37
  27.9 5.7 %collective-permute-start.7 = (bf16[1,2,3,1664]{3,1,2,0:T(2,128)(2,1)S(1)}, bf16[1,2,3,1664]{3,1,2,0:T(2,128)(2,1)S(1)}, u32[]{:S(2)}, u32[]{:S(2)}) collective-permute-start(bf16[1,2,3,1664]{3,1,2,0:T(2,128)(2,1)S(1)} %fusion.32), channel_id=1, source_target_pairs={{2,0},{3,1},{4,2},{5,3},{6,4},{7,5},{8,6},{9,7},{10,8},{11,9},{12,... | collective-permute-start | bytes 59912 | tf_op jit(solution)/shard_map/ppermute | solution.py:37
  34.9 0.8 %copy-start.2 = (pred[8,14]{0,1:T(8,128)(4,1)S(1)}, pred[8,14]{0,1:T(8,128)(4,1)}, u32[]{:S(2)}) copy-start(pred[8,14]{0,1:T(8,128)(4,1)} %constant.47) | copy-start | bytes 340
  45.6 2.2 %slice-start = ((s8[7962624]{0:T(1024)(128)(4,1)}), s8[4194304]{0:T(1024)(128)(4,1)S(1)}, s32[]{:S(2)}) async-start(s8[7962624]{0:T(1024)(128)(4,1)} %bitcast.104), calls=%async_computation | async-start | bytes 8388608
  46.6 2.6 %slice-start.1 = ((s8[7962624]{0:T(1024)(128)(4,1)}), s8[3768320]{0:T(1024)(128)(4,1)S(1)}, s32[]{:S(2)}) async-start(s8[7962624]{0:T(1024)(128)(4,1)} %bitcast.104), calls=%async_computation.1 | async-start | bytes 7536640

commit v9 on v5

v9 whole, which is shorter than its diff:
```python
import functools

import jax
import jax.numpy as jnp
from jax import lax
from jax.experimental import pallas as pl
from jax.experimental.pallas import tpu as pltpu
from jax.sharding import PartitionSpec as P

ZC = 16
HALO = 2

epsilon = 1e-06

def rms_scale(values):
    return values * lax.rsqrt(jnp.mean(values * values, axis=-1, keepdims=True) + epsilon)


def reverse_bits(value, bits):
    return sum(((value >> b) & 1) << (bits - 1 - b) for b in range(bits))


def gather_rows(x, n, rows_dev, slot):
    bits = n.bit_length() - 1
    for k in reversed(range(bits)):
        half = (1 << k) * rows_dev
        size = half + 2 * HALO
        bit = (slot >> k) & 1
        own = lax.dynamic_slice_in_dim(x, bit * half, size, 0)
        send = lax.dynamic_slice_in_dim(x, (1 - bit) * half, size, 0)
        flip = 1 << (bits - 1 - k)
        pairs = [(i, i ^ flip) for i in range(n)]
        x = own + lax.ppermute(send, "dev", pairs)
    return x


LANE = 128


def decode_kernel(columns, row_ok_ref, xt_ref, w_in_ref, w_hbm, w_pix_ref, out_ref, w_vmem, act_ref, center_ref, sem):
    rows_in = act_ref.shape[1]
    rows_out = rows_in - 2
    lead = 2 * LANE
    span = act_ref.shape[2] - lead
    channels = act_ref.shape[3]
    taps = w_vmem.shape[0] // 3
    copies = [
        pltpu.make_async_copy(w_hbm.at[pl.ds(a * taps, taps)], w_vmem.at[pl.ds(a * taps, taps)], sem.at[a])
        for a in range(3)
    ]
    for copy in copies:
        copy.start()
    zeros = jnp.zeros((lead, channels), act_ref.dtype)
    for e in range(3):
        for j in range(rows_in):
            act_ref[e, j, 0:lead, :] = zeros
    column = lax.broadcasted_iota(jnp.int32, (span, 1), 0) % LANE
    valid = column < columns
    w_in = w_in_ref[...]
    for j in range(rows_in):
        pieces = []
        for a in range(3):
            for b in range(3):
                src = xt_ref[j + b, :, a * LANE : a * LANE + span].astype(jnp.float32)
                for e in range(3):
                    shifted = src if e == 1 else pltpu.roll(src, (1 - e) % span, 1)
                    pieces.append(shifted.astype(jnp.bfloat16))
        patches = jnp.concatenate(pieces, axis=0)
        first_t = jnp.dot(w_in, patches, preferred_element_type=jnp.float32)
        first = jnp.where(valid, first_t.T, 0.0)
        if 1 <= j <= rows_out:
            center_ref[j - 1] = first
        scaled = first * lax.rsqrt(jnp.mean(first * first, axis=-1, keepdims=True) + epsilon)
        act = scaled / (1.0 + jnp.exp(-scaled)) * row_ok_ref[j]
        act_ref[1, j, lead:, :] = act.astype(act_ref.dtype)
        act_ref[0, j, lead:, :] = pltpu.roll(act, 1, 0).astype(act_ref.dtype)
        act_ref[2, j, lead:, :] = pltpu.roll(act, span - 1, 0).astype(act_ref.dtype)
    for copy in copies:
        copy.wait()
    for jo in range(rows_out):

        def time_tap(a, acc):
            start = pl.multiple_of(a * LANE, LANE)
            for b in range(3):
                for e in range(3):
                    piece = act_ref[e, jo + b, pl.ds(start, span), :]
                    acc = acc + jnp.dot(piece, w_vmem[a * taps + b * 3 + e], preferred_element_type=jnp.float32)
            return acc

        acc = lax.fori_loop(0, 3, time_tap, center_ref[jo])
        scale = lax.rsqrt(jnp.mean(acc * acc, axis=-1, keepdims=True) + epsilon)
        normed = (acc * scale).astype(jnp.bfloat16)
        out_ref[jo] = jnp.dot(normed, w_pix_ref[...], preferred_element_type=jnp.float32)


def decode(row_ok, xt, conv_in, conv_mid, to_pixels, columns):
    rows_in = xt.shape[0] - 2
    span = xt.shape[2] - 2 * LANE
    channels = conv_mid.shape[1]
    w_mid = conv_mid.reshape(27, channels, channels)
    w_in_t = conv_in.T
    n_pix = to_pixels.shape[1]
    w_pix = jnp.pad(to_pixels, ((0, 0), (0, LANE - n_pix)))
    vmem = pltpu.MemorySpace.VMEM
    out = pl.pallas_call(
        functools.partial(decode_kernel, columns),
        out_shape=jax.ShapeDtypeStruct((rows_in - 2, span, LANE), jnp.float32),
        in_specs=[
            pl.BlockSpec(memory_space=pltpu.MemorySpace.SMEM),
            pl.BlockSpec(memory_space=vmem),
            pl.BlockSpec(memory_space=vmem),
            pl.BlockSpec(memory_space=pl.ANY),
            pl.BlockSpec(memory_space=vmem),
        ],
        out_specs=pl.BlockSpec(memory_space=vmem),
        scratch_shapes=[
            pltpu.VMEM((27, channels, channels), jnp.bfloat16),
            pltpu.VMEM((3, rows_in, span + 2 * LANE, channels), jnp.bfloat16),
            pltpu.VMEM((rows_in - 2, span, channels), jnp.float32),
            pltpu.SemaphoreType.DMA((3,)),
        ],
        compiler_params=pltpu.CompilerParams(vmem_limit_bytes=48 * 1024 * 1024),
    )(row_ok, xt, w_in_t, w_mid, w_pix)
    return out[:, :, :n_pix]


def local(latents, owners, conv_in, conv_mid, to_pixels):
    n = lax.axis_size("dev")
    assert n & (n - 1) == 0
    position = lax.axis_index("dev")
    groups, frames, height, width = latents.shape[1:]
    columns = width // ZC
    rows_dev = height // n
    bits = n.bit_length() - 1
    slot = reverse_bits(position, bits)
    steps = groups * frames
    assert columns < LANE

    x = jnp.transpose(latents[0], (2, 0, 1, 3))
    keep = owners == position
    x = jnp.where(keep[None, :, None, None], x, jnp.zeros_like(x))
    x = jnp.pad(x, ((HALO, HALO), (0, 0), (0, 0), (0, 0)))
    x = gather_rows(x, n, rows_dev, slot)

    rows_in = rows_dev + 2
    xt = x.reshape(rows_dev + 2 * HALO, steps, columns, ZC).transpose(0, 3, 1, 2)
    xt = jnp.pad(xt, ((0, 0), (0, 0), (2, 0), (0, LANE - columns)))
    xt = xt.reshape(rows_dev + 2 * HALO, ZC, (steps + 2) * LANE)
    row_of = slot * rows_dev - 1 + jnp.arange(rows_in)
    row_ok = ((row_of >= 0) & (row_of < height)).astype(jnp.float32)

    projected = decode(row_ok, xt, conv_in, conv_mid, to_pixels, columns)
    projected = projected.reshape(rows_dev, groups, frames, LANE, 2, 2, 3)[:, :, :, :columns]
    projected = projected.transpose(1, 2, 0, 4, 3, 5, 6)
    pixels = projected.reshape(groups, frames, 2 * rows_dev, 6 * columns).astype(jnp.bfloat16)
    return lax.ppermute(pixels, "dev", [(i, reverse_bits(i, bits)) for i in range(n)])


def solution(mesh):
    in_specs = (P(("stream", "dev"), None, None, None, None), P("stream"), P(), P(), P())
    out_specs = P("stream", None, "dev", None)
    return jax.shard_map(local, mesh=mesh, in_specs=in_specs, out_specs=out_specs, check_vma=False)
```

time: 78.2 us -> 51.7 us (0.66); the launches traced: 77 us -> 51.4 us
  local copies, waits for them, and re-layouts: 23.5 us -> 5.68 us
  Pallas kernels: 21.8 us -> 16.1 us
  waiting for transfers between devices: 24.7 us -> 22.9 us
    concatenate x1 -> x0, local copies, waits for them, and re-layouts: 12.2 us -> none  [local(): xcol = jnp.concatenate(pieces, axis=-1)]
    slice x4 -> x2, local copies, waits for them, and re-layouts: 7.9 us -> 0.14 us  [decode(): return out[:, :, :n_pix]]
    pallas_call x1, Pallas kernels: 21.8 us -> 16.1 us  [decode(): pl.pallas_call(functools.partial(decode_kernel, columns), out_shape=jax.S...]
    unnamed x6 -> x3, local copies, waits for them, and re-layouts: 0.76 us -> 2.59 us
    ppermute x4, waiting for transfers between devices: 18.9 us -> 17.1 us  [gather_rows(): x = own + lax.ppermute(send, 'dev', pairs)]
  transfers between devices with their start and end apart: 5 -> 5, of which waited for: 5 -> 5; matrix products, arithmetic and copies ran while one was open for 0% -> 4% of each run, Pallas kernels for 0% -> 0%
where the time goes in v9:
time: 51.7 us; the launch traced here: 51.4 us
  waiting for transfers between devices  22.9 us (44%)
  Pallas kernels  16.1 us (31%)
  local copies, waits for them, and re-layouts  5.68 us (11%)
  starting transfers between devices  4.46 us (9%)
  other arithmetic  2.12 us (4%)
    ppermute x4, waiting for transfers between devices, gather_rows(): x = own + lax.ppermute(send, 'dev', pairs)  17.1 us
    pallas_call x1, Pallas kernels, decode(): pl.pallas_call(functools.partial(decode_kernel, columns), out_shape=jax.S...  16.1 us
    ppermute x1, waiting for transfers between devices, local(): lax.ppermute(pixels, 'dev', [(i, reverse_bits(i, bits)) for i in range(n)])  5.82 us
    unnamed x3, local copies, waits for them, and re-layouts  2.59 us
    ppermute x4, starting transfers between devices, gather_rows(): x = own + lax.ppermute(send, 'dev', pairs)  2.54 us
    ppermute x1, starting transfers between devices, local(): lax.ppermute(pixels, 'dev', [(i, reverse_bits(i, bits)) for i in range(n)])  1.92 us
    convert_element_type x3, local copies, waits for them, and re-layouts, local(): projected.reshape(groups, frames, 2 * rows_dev, 6 * columns)  1.23 us
    select_n x1, other arithmetic, local(): x = jnp.where(keep[None, :, None, None], x, jnp.zeros_like(x))  1.07 us
  transfers between devices with their start and end apart: 5, of which 5 were waited for; matrix products, arithmetic and copies ran while one was open for 4% of the time, Pallas kernels for 0%

profile of v9, /device:TPU:24, one launch (start us, length us, event | category | flops | bytes accessed | tf_op | source)
XLA Modules:
  0.0 51.4 jit_solution(2882769389166691505)
XLA Ops:
  0.0 0.7 %broadcast_compare_fusion = pred[2]{0:T(512)(128)(4,1)S(1)} fusion(s32[2]{0:T(128)} %param.6, s32[]{:T(128)S(6)} %axis_index.12), kind=kLoop, calls=%fused_computation.14 | loop fusion | flops 2 | bytes 14 | tf_op jit(solution)/shard_map/eq | solution.py:140
  0.7 1.1 %fusion.1 = bf16[16,2,3,1664]{3,0,2,1:T(8,128)(2,1)S(1)} fusion(bf16[1,2,3,16,1664]{4,3,2,1,0:T(8,128)(2,1)} %param.5, pred[2]{0:T(512)(128)(4,1)S(1)} %broadcast_compare_fusion), kind=kLoop, calls=%fused_computation.5 | loop fusion | flops 159744 | bytes 638978 | tf_op jit(solution)/shard_map/jit(_where)/select_n | solution.py:141
  1.7 0.1 pad_dynamic-slice_fusion
  2.0 1.6 %collective-permute-done = bf16[12,2,3,1664]{3,0,2,1:T(8,128)(2,1)S(1)} collective-permute-done((bf16[12,2,3,1664]{3,0,2,1:T(8,128)(2,1)S(1)}, bf16[12,2,3,1664]{3,0,2,1:T(8,128)(2,1)S(1)}, u32[]{:S(2)}, u32[]{:S(2)}) %collective-permute-start) | collective-permute-done | bytes 239648 | tf_op jit(solution)/shard_map/ppermute | solution.py:33
  3.6 0.2 fusion
  3.8 1.6 %collective-permute-start.1 = (bf16[8,2,3,1664]{3,0,2,1:T(8,128)(2,1)S(1)}, bf16[8,2,3,1664]{3,0,2,1:T(8,128)(2,1)S(1)}, u32[]{:S(2)}, u32[]{:S(2)}) collective-permute-start(bf16[8,2,3,1664]{3,0,2,1:T(8,128)(2,1)S(1)} %constant_dynamic-slice_fusion.2), channel_id=1, source_target_pairs={{0,2},{1,3},{2,0},{3,1},{4,6},{5,7},{6,4},{7,5},{8,10},{9,11},{10,... | collective-permute-start | bytes 479240 | tf_op jit(solution)/shard_map/ppermute | solution.py:33
  5.4 4.7 %collective-permute-done.1 = bf16[8,2,3,1664]{3,0,2,1:T(8,128)(2,1)S(1)} collective-permute-done((bf16[8,2,3,1664]{3,0,2,1:T(8,128)(2,1)S(1)}, bf16[8,2,3,1664]{3,0,2,1:T(8,128)(2,1)S(1)}, u32[]{:S(2)}, u32[]{:S(2)}) %collective-permute-start.1) | collective-permute-done | bytes 159776 | tf_op jit(solution)/shard_map/ppermute | solution.py:33
  10.0 0.1 dynamic-slice_add_fusion.2
  10.2 0.5 %collective-permute-start.2 = (bf16[6,2,3,1664]{3,0,2,1:T(8,128)(2,1)S(1)}, bf16[6,2,3,1664]{3,0,2,1:T(8,128)(2,1)S(1)}, u32[]{:S(2)}, u32[]{:S(2)}) collective-permute-start(bf16[6,2,3,1664]{3,0,2,1:T(8,128)(2,1)S(1)} %constant_dynamic-slice_fusion.1), channel_id=1, source_target_pairs={{0,4},{1,5},{2,6},{3,7},{4,0},{5,1},{6,2},{7,3},{8,12},{9,13},{10,... | collective-permute-start | bytes 359432 | tf_op jit(solution)/shard_map/ppermute | solution.py:33
  10.7 1.1 %copy.12 = bf16[432,384]{0,1:T(8,128)(2,1)S(1)} copy(bf16[432,384]{1,0:T(8,128)(2,1)} %param.7) | data formatting | bytes 663552 | tf_op args[2]
  11.8 0.8 %copy.13 = bf16[384,12]{1,0:T(8,128)(2,1)S(1)} copy(bf16[384,12]{0,1:T(8,128)(2,1)} %param.9) | data formatting | bytes 18432 | tf_op args[4]
  12.7 2.8 %collective-permute-done.2 = bf16[6,2,3,1664]{3,0,2,1:T(8,128)(2,1)S(1)} collective-permute-done((bf16[6,2,3,1664]{3,0,2,1:T(8,128)(2,1)S(1)}, bf16[6,2,3,1664]{3,0,2,1:T(8,128)(2,1)S(1)}, u32[]{:S(2)}, u32[]{:S(2)}) %collective-permute-start.2) | collective-permute-done | bytes 119840 | tf_op jit(solution)/shard_map/ppermute | solution.py:33
  15.7 0.4 collective-permute-start.3
  16.1 8.0 %collective-permute-done.3 = bf16[5,2,3,1664]{3,0,2,1:T(8,128)(2,1)S(1)} collective-permute-done((bf16[5,2,3,1664]{3,0,2,1:T(8,128)(2,1)S(1)}, bf16[5,2,3,1664]{3,0,2,1:T(8,128)(2,1)S(1)}, u32[]{:S(2)}, u32[]{:S(2)}) %collective-permute-start.3) | collective-permute-done | bytes 99872 | tf_op jit(solution)/shard_map/ppermute | solution.py:33
  24.2 0.6 %reshape.16 = bf16[5,6,104,16]{3,2,1,0:T(8,128)(2,1)S(1)} reshape(bf16[5,2,3,1664]{3,2,1,0:T(4,128)(2,1)S(1)} %copy.10) | data formatting | bytes 199680 | tf_op jit(solution)/shard_map/reshape | solution.py:146
  24.8 0.3 pad.13
  25.1 0.4 copy.16.xt_ref
  25.5 16.1 %shard_map.55 = f32[1,768,128]{2,1,0:T(8,128)S(1)} custom-call(f32[3]{0:T(128)S(1)} %and_convert_fusion.row_ok_ref, bf16[5,16,1024]{2,1,0:T(8,128)(2,1)S(1)} %copy.16.xt_ref, bf16[384,432]{1,0:T(8,128)(2,1)S(1)} %bitcast.16, bf16[27,384,384]{2,1,0:T(8,128)(2,1)} %bitcast.17, bf16[384,128]{1,0:T(8,128)(2,1)S(1)} %pad.14.w_pix_ref), custom_call_target="tpu_custom_call" | custom-call | tf_op jit(solution)/shard_map/pallas_call | solution.py:105
  41.6 0.1 copy.14
  41.8 0.5 %copy.15 = bf16[2,3,1,2,104,2,3]{6,5,4,3,1,0,2:T(2,128)(2,1)S(1)} copy(bf16[2,3,1,2,104,2,3]{4,1,0,6,5,3,2:T(4,128)(2,1)S(1)} %slice_bitcast_fusion) | data formatting | bytes 29952 | tf_op jit(solution)/shard_map/convert_element_type | solution.py:155
  42.4 0.7 %convert_element_type.18 = bf16[2,3,2,624]{3,2,1,0:T(2,128)(2,1)S(1)} reshape(bf16[2,3,1,2,104,2,3]{6,5,4,3,1,0,2:T(2,128)(2,1)S(1)} %copy.15) | data formatting | bytes 29952 | tf_op jit(solution)/shard_map/convert_element_type | solution.py:155
  43.0 1.9 %collective-permute-start.4 = (bf16[2,3,2,624]{3,2,1,0:T(2,128)(2,1)S(1)}, bf16[2,3,2,624]{3,2,1,0:T(2,128)(2,1)S(1)}, u32[]{:S(2)}, u32[]{:S(2)}) collective-permute-start(bf16[2,3,2,624]{3,2,1,0:T(2,128)(2,1)S(1)} %convert_element_type.18), channel_id=1, source_target_pairs={{0,0},{1,8},{2,4},{3,12},{4,2},{5,10},{6,6},{7,14},{8,1},{9,9},{10... | collective-permute-start | bytes 44936 | tf_op jit(solution)/shard_map/ppermute | solution.py:156
  45.0 5.8 %collective-permute-done.4 = bf16[2,3,2,624]{3,2,1,0:T(2,128)(2,1)S(1)} collective-permute-done((bf16[2,3,2,624]{3,2,1,0:T(2,128)(2,1)S(1)}, bf16[2,3,2,624]{3,2,1,0:T(2,128)(2,1)S(1)}, u32[]{:S(2)}, u32[]{:S(2)}) %collective-permute-start.4) | collective-permute-done | bytes 15008 | tf_op jit(solution)/shard_map/ppermute | solution.py:156
  50.8 0.6 %copy.18 = bf16[2,3,2,624]{3,2,1,0:T(2,128)(2,1)} copy(bf16[2,3,2,624]{3,2,1,0:T(2,128)(2,1)S(1)} %collective-permute-done.4) | data formatting | bytes 29952
  (12 shorter events, 0.5 us)
Async XLA Ops:
  1.9 1.7 %collective-permute-start = (bf16[12,2,3,1664]{3,0,2,1:T(8,128)(2,1)S(1)}, bf16[12,2,3,1664]{3,0,2,1:T(8,128)(2,1)S(1)}, u32[]{:S(2)}, u32[]{:S(2)}) collective-permute-start(bf16[12,2,3,1664]{3,0,2,1:T(8,128)(2,1)S(1)} %pad_dynamic-slice_fusion), channel_id=1, source_target_pairs={{0,1},{1,0},{2,3},{3,2},{4,5},{5,4},{6,7},{7,6},{8,9},{9,8},{10,11... | collective-permute-start | bytes 718856 | tf_op jit(solution)/shard_map/ppermute | solution.py:33
  3.8 6.2 %collective-permute-start.1 = (bf16[8,2,3,1664]{3,0,2,1:T(8,128)(2,1)S(1)}, bf16[8,2,3,1664]{3,0,2,1:T(8,128)(2,1)S(1)}, u32[]{:S(2)}, u32[]{:S(2)}) collective-permute-start(bf16[8,2,3,1664]{3,0,2,1:T(8,128)(2,1)S(1)} %constant_dynamic-slice_fusion.2), channel_id=1, source_target_pairs={{0,2},{1,3},{2,0},{3,1},{4,6},{5,7},{6,4},{7,5},{8,10},{9,11},{10,... | collective-permute-start | bytes 479240 | tf_op jit(solution)/shard_map/ppermute | solution.py:33
  10.2 5.4 %collective-permute-start.2 = (bf16[6,2,3,1664]{3,0,2,1:T(8,128)(2,1)S(1)}, bf16[6,2,3,1664]{3,0,2,1:T(8,128)(2,1)S(1)}, u32[]{:S(2)}, u32[]{:S(2)}) collective-permute-start(bf16[6,2,3,1664]{3,0,2,1:T(8,128)(2,1)S(1)} %constant_dynamic-slice_fusion.1), channel_id=1, source_target_pairs={{0,4},{1,5},{2,6},{3,7},{4,0},{5,1},{6,2},{7,3},{8,12},{9,13},{10,... | collective-permute-start | bytes 359432 | tf_op jit(solution)/shard_map/ppermute | solution.py:33
  15.7 8.4 %collective-permute-start.3 = (bf16[5,2,3,1664]{3,0,2,1:T(8,128)(2,1)S(1)}, bf16[5,2,3,1664]{3,0,2,1:T(8,128)(2,1)S(1)}, u32[]{:S(2)}, u32[]{:S(2)}) collective-permute-start(bf16[5,2,3,1664]{3,0,2,1:T(8,128)(2,1)S(1)} %constant_dynamic-slice_fusion), channel_id=1, source_target_pairs={{0,8},{1,9},{2,10},{3,11},{4,12},{5,13},{6,14},{7,15},{8,0},{9,1},... | collective-permute-start | bytes 299528 | tf_op jit(solution)/shard_map/ppermute | solution.py:33
  43.0 7.7 %collective-permute-start.4 = (bf16[2,3,2,624]{3,2,1,0:T(2,128)(2,1)S(1)}, bf16[2,3,2,624]{3,2,1,0:T(2,128)(2,1)S(1)}, u32[]{:S(2)}, u32[]{:S(2)}) collective-permute-start(bf16[2,3,2,624]{3,2,1,0:T(2,128)(2,1)S(1)} %convert_element_type.18), channel_id=1, source_target_pairs={{0,0},{1,8},{2,4},{3,12},{4,2},{5,10},{6,6},{7,14},{8,1},{9,9},{10... | collective-permute-start | bytes 44936 | tf_op jit(solution)/shard_map/ppermute | solution.py:156

commit v10 on v9

--- a/solution.py
+++ b/solution.py
@@ -38,11 +38,11 @@
 
 
 def decode_kernel(columns, row_ok_ref, xt_ref, w_in_ref, w_hbm, w_pix_ref, out_ref, w_vmem, act_ref, center_ref, sem):
-    rows_in = act_ref.shape[1]
+    rows_in = act_ref.shape[0]
     rows_out = rows_in - 2
     lead = 2 * LANE
-    span = act_ref.shape[2] - lead
-    channels = act_ref.shape[3]
+    span = act_ref.shape[1] - lead
+    channels = w_vmem.shape[2]
     taps = w_vmem.shape[0] // 3
     copies = [
         pltpu.make_async_copy(w_hbm.at[pl.ds(a * taps, taps)], w_vmem.at[pl.ds(a * taps, taps)], sem.at[a])
@@ -50,10 +50,9 @@
     ]
     for copy in copies:
         copy.start()
-    zeros = jnp.zeros((lead, channels), act_ref.dtype)
-    for e in range(3):
-        for j in range(rows_in):
-            act_ref[e, j, 0:lead, :] = zeros
+    zeros = jnp.zeros((lead, 3 * channels), act_ref.dtype)
+    for j in range(rows_in):
+        act_ref[j, 0:lead, :] = zeros
     column = lax.broadcasted_iota(jnp.int32, (span, 1), 0) % LANE
     valid = column < columns
     w_in = w_in_ref[...]
@@ -72,9 +71,9 @@
             center_ref[j - 1] = first
         scaled = first * lax.rsqrt(jnp.mean(first * first, axis=-1, keepdims=True) + epsilon)
         act = scaled / (1.0 + jnp.exp(-scaled)) * row_ok_ref[j]
-        act_ref[1, j, lead:, :] = act.astype(act_ref.dtype)
-        act_ref[0, j, lead:, :] = pltpu.roll(act, 1, 0).astype(act_ref.dtype)
-        act_ref[2, j, lead:, :] = pltpu.roll(act, span - 1, 0).astype(act_ref.dtype)
+        act_ref[j, lead:, 0:channels] = pltpu.roll(act, 1, 0).astype(act_ref.dtype)
+        act_ref[j, lead:, channels : 2 * channels] = act.astype(act_ref.dtype)
+        act_ref[j, lead:, 2 * channels :] = pltpu.roll(act, span - 1, 0).astype(act_ref.dtype)
     for copy in copies:
         copy.wait()
     for jo in range(rows_out):
@@ -82,9 +81,8 @@
         def time_tap(a, acc):
             start = pl.multiple_of(a * LANE, LANE)
             for b in range(3):
-                for e in range(3):
-                    piece = act_ref[e, jo + b, pl.ds(start, span), :]
-                    acc = acc + jnp.dot(piece, w_vmem[a * taps + b * 3 + e], preferred_element_type=jnp.float32)
+                piece = act_ref[jo + b, pl.ds(start, span), :]
+                acc = acc + jnp.dot(piece, w_vmem[a * taps + b], preferred_element_type=jnp.float32)
             return acc
 
         acc = lax.fori_loop(0, 3, time_tap, center_ref[jo])
@@ -97,7 +95,7 @@
     rows_in = xt.shape[0] - 2
     span = xt.shape[2] - 2 * LANE
     channels = conv_mid.shape[1]
-    w_mid = conv_mid.reshape(27, channels, channels)
+    w_mid = conv_mid.reshape(9, 3 * channels, channels)
     w_in_t = conv_in.T
     n_pix = to_pixels.shape[1]
     w_pix = jnp.pad(to_pixels, ((0, 0), (0, LANE - n_pix)))
@@ -114,8 +112,8 @@
         ],
         out_specs=pl.BlockSpec(memory_space=vmem),
         scratch_shapes=[
-            pltpu.VMEM((27, channels, channels), jnp.bfloat16),
-            pltpu.VMEM((3, rows_in, span + 2 * LANE, channels), jnp.bfloat16),
+            pltpu.VMEM((9, 3 * channels, channels), jnp.bfloat16),
+            pltpu.VMEM((rows_in, span + 2 * LANE, 3 * channels), jnp.bfloat16),
             pltpu.VMEM((rows_in - 2, span, channels), jnp.float32),
             pltpu.SemaphoreType.DMA((3,)),
         ],

time: 51.7 us -> 50.6 us (0.979)
  Pallas kernels: 16.1 us -> 15 us
    pallas_call x1, Pallas kernels: 16.1 us -> 15 us  [decode(): pl.pallas_call(functools.partial(decode_kernel, columns), out_shape=jax.S...]
where the time goes in v10:
time: 50.6 us; the launch traced here: 50.3 us
  waiting for transfers between devices  22.9 us (45%)
  Pallas kernels  15 us (30%)
  local copies, waits for them, and re-layouts  5.68 us (11%)
  starting transfers between devices  4.46 us (9%)
  other arithmetic  2.12 us (4%)
    ppermute x4, waiting for transfers between devices, gather_rows(): x = own + lax.ppermute(send, 'dev', pairs)  17.1 us
    pallas_call x1, Pallas kernels, decode(): pl.pallas_call(functools.partial(decode_kernel, columns), out_shape=jax.S...  15 us
    ppermute x1, waiting for transfers between devices, local(): lax.ppermute(pixels, 'dev', [(i, reverse_bits(i, bits)) for i in range(n)])  5.82 us
    unnamed x3, local copies, waits for them, and re-layouts  2.59 us
    ppermute x4, starting transfers between devices, gather_rows(): x = own + lax.ppermute(send, 'dev', pairs)  2.54 us
    ppermute x1, starting transfers between devices, local(): lax.ppermute(pixels, 'dev', [(i, reverse_bits(i, bits)) for i in range(n)])  1.92 us
    convert_element_type x3, local copies, waits for them, and re-layouts, local(): projected.reshape(groups, frames, 2 * rows_dev, 6 * columns)  1.23 us
    select_n x1, other arithmetic, local(): x = jnp.where(keep[None, :, None, None], x, jnp.zeros_like(x))  1.07 us
  transfers between devices with their start and end apart: 5, of which 5 were waited for; matrix products, arithmetic and copies ran while one was open for 4% of the time, Pallas kernels for 0%

profile of v10, /device:TPU:24, one launch (start us, length us, event | category | flops | bytes accessed | tf_op | source)
XLA Modules:
  0.0 50.3 jit_solution(1240326092139427020)
XLA Ops:
  0.0 0.7 %broadcast_compare_fusion = pred[2]{0:T(512)(128)(4,1)S(1)} fusion(s32[2]{0:T(128)} %param.6, s32[]{:T(128)S(6)} %axis_index.12), kind=kLoop, calls=%fused_computation.14 | loop fusion | flops 2 | bytes 14 | tf_op jit(solution)/shard_map/eq | solution.py:138
  0.7 1.1 %fusion.1 = bf16[16,2,3,1664]{3,0,2,1:T(8,128)(2,1)S(1)} fusion(bf16[1,2,3,16,1664]{4,3,2,1,0:T(8,128)(2,1)} %param.5, pred[2]{0:T(512)(128)(4,1)S(1)} %broadcast_compare_fusion), kind=kLoop, calls=%fused_computation.5 | loop fusion | flops 159744 | bytes 638978 | tf_op jit(solution)/shard_map/jit(_where)/select_n | solution.py:139
  1.7 0.1 pad_dynamic-slice_fusion
  2.0 1.6 %collective-permute-done = bf16[12,2,3,1664]{3,0,2,1:T(8,128)(2,1)S(1)} collective-permute-done((bf16[12,2,3,1664]{3,0,2,1:T(8,128)(2,1)S(1)}, bf16[12,2,3,1664]{3,0,2,1:T(8,128)(2,1)S(1)}, u32[]{:S(2)}, u32[]{:S(2)}) %collective-permute-start) | collective-permute-done | bytes 239648 | tf_op jit(solution)/shard_map/ppermute | solution.py:33
  3.6 0.2 fusion
  3.8 1.6 %collective-permute-start.1 = (bf16[8,2,3,1664]{3,0,2,1:T(8,128)(2,1)S(1)}, bf16[8,2,3,1664]{3,0,2,1:T(8,128)(2,1)S(1)}, u32[]{:S(2)}, u32[]{:S(2)}) collective-permute-start(bf16[8,2,3,1664]{3,0,2,1:T(8,128)(2,1)S(1)} %constant_dynamic-slice_fusion.2), channel_id=1, source_target_pairs={{0,2},{1,3},{2,0},{3,1},{4,6},{5,7},{6,4},{7,5},{8,10},{9,11},{10,... | collective-permute-start | bytes 479240 | tf_op jit(solution)/shard_map/ppermute | solution.py:33
  5.4 4.7 %collective-permute-done.1 = bf16[8,2,3,1664]{3,0,2,1:T(8,128)(2,1)S(1)} collective-permute-done((bf16[8,2,3,1664]{3,0,2,1:T(8,128)(2,1)S(1)}, bf16[8,2,3,1664]{3,0,2,1:T(8,128)(2,1)S(1)}, u32[]{:S(2)}, u32[]{:S(2)}) %collective-permute-start.1) | collective-permute-done | bytes 159776 | tf_op jit(solution)/shard_map/ppermute | solution.py:33
  10.0 0.1 dynamic-slice_add_fusion.2
  10.2 0.5 %collective-permute-start.2 = (bf16[6,2,3,1664]{3,0,2,1:T(8,128)(2,1)S(1)}, bf16[6,2,3,1664]{3,0,2,1:T(8,128)(2,1)S(1)}, u32[]{:S(2)}, u32[]{:S(2)}) collective-permute-start(bf16[6,2,3,1664]{3,0,2,1:T(8,128)(2,1)S(1)} %constant_dynamic-slice_fusion.1), channel_id=1, source_target_pairs={{0,4},{1,5},{2,6},{3,7},{4,0},{5,1},{6,2},{7,3},{8,12},{9,13},{10,... | collective-permute-start | bytes 359432 | tf_op jit(solution)/shard_map/ppermute | solution.py:33
  10.7 1.1 %copy.12 = bf16[432,384]{0,1:T(8,128)(2,1)S(1)} copy(bf16[432,384]{1,0:T(8,128)(2,1)} %param.7) | data formatting | bytes 663552 | tf_op args[2]
  11.8 0.8 %copy.13 = bf16[384,12]{1,0:T(8,128)(2,1)S(1)} copy(bf16[384,12]{0,1:T(8,128)(2,1)} %param.9) | data formatting | bytes 18432 | tf_op args[4]
  12.7 2.8 %collective-permute-done.2 = bf16[6,2,3,1664]{3,0,2,1:T(8,128)(2,1)S(1)} collective-permute-done((bf16[6,2,3,1664]{3,0,2,1:T(8,128)(2,1)S(1)}, bf16[6,2,3,1664]{3,0,2,1:T(8,128)(2,1)S(1)}, u32[]{:S(2)}, u32[]{:S(2)}) %collective-permute-start.2) | collective-permute-done | bytes 119840 | tf_op jit(solution)/shard_map/ppermute | solution.py:33
  15.7 0.4 collective-permute-start.3
  16.1 8.0 %collective-permute-done.3 = bf16[5,2,3,1664]{3,0,2,1:T(8,128)(2,1)S(1)} collective-permute-done((bf16[5,2,3,1664]{3,0,2,1:T(8,128)(2,1)S(1)}, bf16[5,2,3,1664]{3,0,2,1:T(8,128)(2,1)S(1)}, u32[]{:S(2)}, u32[]{:S(2)}) %collective-permute-start.3) | collective-permute-done | bytes 99872 | tf_op jit(solution)/shard_map/ppermute | solution.py:33
  24.2 0.6 %reshape.16 = bf16[5,6,104,16]{3,2,1,0:T(8,128)(2,1)S(1)} reshape(bf16[5,2,3,1664]{3,2,1,0:T(4,128)(2,1)S(1)} %copy.10) | data formatting | bytes 199680 | tf_op jit(solution)/shard_map/reshape | solution.py:144
  24.8 0.3 pad.13
  25.1 0.4 copy.16.xt_ref
  25.5 15.0 %shard_map.55 = f32[1,768,128]{2,1,0:T(8,128)S(1)} custom-call(f32[3]{0:T(128)S(1)} %and_convert_fusion.row_ok_ref, bf16[5,16,1024]{2,1,0:T(8,128)(2,1)S(1)} %copy.16.xt_ref, bf16[384,432]{1,0:T(8,128)(2,1)S(1)} %bitcast.16, bf16[9,1152,384]{2,1,0:T(8,128)(2,1)} %bitcast.17, bf16[384,128]{1,0:T(8,128)(2,1)S(1)} %pad.14.w_pix_ref), custom_call_target="tpu_custom_call" | custom-call | tf_op jit(solution)/shard_map/pallas_call | solution.py:103
  40.6 0.1 copy.14
  40.8 0.5 %copy.15 = bf16[2,3,1,2,104,2,3]{6,5,4,3,1,0,2:T(2,128)(2,1)S(1)} copy(bf16[2,3,1,2,104,2,3]{4,1,0,6,5,3,2:T(4,128)(2,1)S(1)} %slice_bitcast_fusion) | data formatting | bytes 29952 | tf_op jit(solution)/shard_map/convert_element_type | solution.py:153
  41.3 0.7 %convert_element_type.18 = bf16[2,3,2,624]{3,2,1,0:T(2,128)(2,1)S(1)} reshape(bf16[2,3,1,2,104,2,3]{6,5,4,3,1,0,2:T(2,128)(2,1)S(1)} %copy.15) | data formatting | bytes 29952 | tf_op jit(solution)/shard_map/convert_element_type | solution.py:153
  42.0 1.9 %collective-permute-start.4 = (bf16[2,3,2,624]{3,2,1,0:T(2,128)(2,1)S(1)}, bf16[2,3,2,624]{3,2,1,0:T(2,128)(2,1)S(1)}, u32[]{:S(2)}, u32[]{:S(2)}) collective-permute-start(bf16[2,3,2,624]{3,2,1,0:T(2,128)(2,1)S(1)} %convert_element_type.18), channel_id=1, source_target_pairs={{0,0},{1,8},{2,4},{3,12},{4,2},{5,10},{6,6},{7,14},{8,1},{9,9},{10... | collective-permute-start | bytes 44936 | tf_op jit(solution)/shard_map/ppermute | solution.py:154
  43.9 5.8 %collective-permute-done.4 = bf16[2,3,2,624]{3,2,1,0:T(2,128)(2,1)S(1)} collective-permute-done((bf16[2,3,2,624]{3,2,1,0:T(2,128)(2,1)S(1)}, bf16[2,3,2,624]{3,2,1,0:T(2,128)(2,1)S(1)}, u32[]{:S(2)}, u32[]{:S(2)}) %collective-permute-start.4) | collective-permute-done | bytes 15008 | tf_op jit(solution)/shard_map/ppermute | solution.py:154
  49.7 0.6 %copy.18 = bf16[2,3,2,624]{3,2,1,0:T(2,128)(2,1)} copy(bf16[2,3,2,624]{3,2,1,0:T(2,128)(2,1)S(1)} %collective-permute-done.4) | data formatting | bytes 29952
  (12 shorter events, 0.5 us)
Async XLA Ops:
  1.9 1.7 %collective-permute-start = (bf16[12,2,3,1664]{3,0,2,1:T(8,128)(2,1)S(1)}, bf16[12,2,3,1664]{3,0,2,1:T(8,128)(2,1)S(1)}, u32[]{:S(2)}, u32[]{:S(2)}) collective-permute-start(bf16[12,2,3,1664]{3,0,2,1:T(8,128)(2,1)S(1)} %pad_dynamic-slice_fusion), channel_id=1, source_target_pairs={{0,1},{1,0},{2,3},{3,2},{4,5},{5,4},{6,7},{7,6},{8,9},{9,8},{10,11... | collective-permute-start | bytes 718856 | tf_op jit(solution)/shard_map/ppermute | solution.py:33
  3.8 6.2 %collective-permute-start.1 = (bf16[8,2,3,1664]{3,0,2,1:T(8,128)(2,1)S(1)}, bf16[8,2,3,1664]{3,0,2,1:T(8,128)(2,1)S(1)}, u32[]{:S(2)}, u32[]{:S(2)}) collective-permute-start(bf16[8,2,3,1664]{3,0,2,1:T(8,128)(2,1)S(1)} %constant_dynamic-slice_fusion.2), channel_id=1, source_target_pairs={{0,2},{1,3},{2,0},{3,1},{4,6},{5,7},{6,4},{7,5},{8,10},{9,11},{10,... | collective-permute-start | bytes 479240 | tf_op jit(solution)/shard_map/ppermute | solution.py:33
  10.2 5.4 %collective-permute-start.2 = (bf16[6,2,3,1664]{3,0,2,1:T(8,128)(2,1)S(1)}, bf16[6,2,3,1664]{3,0,2,1:T(8,128)(2,1)S(1)}, u32[]{:S(2)}, u32[]{:S(2)}) collective-permute-start(bf16[6,2,3,1664]{3,0,2,1:T(8,128)(2,1)S(1)} %constant_dynamic-slice_fusion.1), channel_id=1, source_target_pairs={{0,4},{1,5},{2,6},{3,7},{4,0},{5,1},{6,2},{7,3},{8,12},{9,13},{10,... | collective-permute-start | bytes 359432 | tf_op jit(solution)/shard_map/ppermute | solution.py:33
  15.7 8.4 %collective-permute-start.3 = (bf16[5,2,3,1664]{3,0,2,1:T(8,128)(2,1)S(1)}, bf16[5,2,3,1664]{3,0,2,1:T(8,128)(2,1)S(1)}, u32[]{:S(2)}, u32[]{:S(2)}) collective-permute-start(bf16[5,2,3,1664]{3,0,2,1:T(8,128)(2,1)S(1)} %constant_dynamic-slice_fusion), channel_id=1, source_target_pairs={{0,8},{1,9},{2,10},{3,11},{4,12},{5,13},{6,14},{7,15},{8,0},{9,1},... | collective-permute-start | bytes 299528 | tf_op jit(solution)/shard_map/ppermute | solution.py:33
  42.0 7.7 %collective-permute-start.4 = (bf16[2,3,2,624]{3,2,1,0:T(2,128)(2,1)S(1)}, bf16[2,3,2,624]{3,2,1,0:T(2,128)(2,1)S(1)}, u32[]{:S(2)}, u32[]{:S(2)}) collective-permute-start(bf16[2,3,2,624]{3,2,1,0:T(2,128)(2,1)S(1)} %convert_element_type.18), channel_id=1, source_target_pairs={{0,0},{1,8},{2,4},{3,12},{4,2},{5,10},{6,6},{7,14},{8,1},{9,9},{10... | collective-permute-start | bytes 44936 | tf_op jit(solution)/shard_map/ppermute | solution.py:154

commit v11 on v10

--- a/solution.py
+++ b/solution.py
@@ -74,18 +74,14 @@
         act_ref[j, lead:, 0:channels] = pltpu.roll(act, 1, 0).astype(act_ref.dtype)
         act_ref[j, lead:, channels : 2 * channels] = act.astype(act_ref.dtype)
         act_ref[j, lead:, 2 * channels :] = pltpu.roll(act, span - 1, 0).astype(act_ref.dtype)
-    for copy in copies:
-        copy.wait()
     for jo in range(rows_out):
-
-        def time_tap(a, acc):
-            start = pl.multiple_of(a * LANE, LANE)
+        acc = center_ref[jo]
+        for a in range(3):
+            if jo == 0:
+                copies[a].wait()
             for b in range(3):
-                piece = act_ref[jo + b, pl.ds(start, span), :]
+                piece = act_ref[jo + b, a * LANE : a * LANE + span, :]
                 acc = acc + jnp.dot(piece, w_vmem[a * taps + b], preferred_element_type=jnp.float32)
-            return acc
-
-        acc = lax.fori_loop(0, 3, time_tap, center_ref[jo])
         scale = lax.rsqrt(jnp.mean(acc * acc, axis=-1, keepdims=True) + epsilon)
         normed = (acc * scale).astype(jnp.bfloat16)
         out_ref[jo] = jnp.dot(normed, w_pix_ref[...], preferred_element_type=jnp.float32)

time: 50.6 us -> 49.7 us (0.982)
  Pallas kernels: 15 us -> 14.1 us
    pallas_call x1, Pallas kernels: 15 us -> 14.1 us  [decode(): pl.pallas_call(functools.partial(decode_kernel, columns), out_shape=jax.S...]
where the time goes in v11:
time: 49.7 us; the launch traced here: 49.5 us
  waiting for transfers between devices  22.9 us (46%)
  Pallas kernels  14.1 us (28%)
  local copies, waits for them, and re-layouts  5.68 us (11%)
  starting transfers between devices  4.46 us (9%)
  other arithmetic  2.12 us (4%)
    ppermute x4, waiting for transfers between devices, gather_rows(): x = own + lax.ppermute(send, 'dev', pairs)  17.1 us
    pallas_call x1, Pallas kernels, decode(): pl.pallas_call(functools.partial(decode_kernel, columns), out_shape=jax.S...  14.1 us
    ppermute x1, waiting for transfers between devices, local(): lax.ppermute(pixels, 'dev', [(i, reverse_bits(i, bits)) for i in range(n)])  5.82 us
    unnamed x3, local copies, waits for them, and re-layouts  2.59 us
    ppermute x4, starting transfers between devices, gather_rows(): x = own + lax.ppermute(send, 'dev', pairs)  2.54 us
    ppermute x1, starting transfers between devices, local(): lax.ppermute(pixels, 'dev', [(i, reverse_bits(i, bits)) for i in range(n)])  1.92 us
    convert_element_type x3, local copies, waits for them, and re-layouts, local(): projected.reshape(groups, frames, 2 * rows_dev, 6 * columns)  1.23 us
    select_n x1, other arithmetic, local(): x = jnp.where(keep[None, :, None, None], x, jnp.zeros_like(x))  1.07 us
  transfers between devices with their start and end apart: 5, of which 5 were waited for; matrix products, arithmetic and copies ran while one was open for 4% of the time, Pallas kernels for 0%

profile of v11, /device:TPU:24, one launch (start us, length us, event | category | flops | bytes accessed | tf_op | source)
XLA Modules:
  0.0 49.5 jit_solution(17686409686264789566)
XLA Ops:
  0.0 0.7 %broadcast_compare_fusion = pred[2]{0:T(512)(128)(4,1)S(1)} fusion(s32[2]{0:T(128)} %param.6, s32[]{:T(128)S(6)} %axis_index.12), kind=kLoop, calls=%fused_computation.14 | loop fusion | flops 2 | bytes 14 | tf_op jit(solution)/shard_map/eq | solution.py:134
  0.7 1.1 %fusion.1 = bf16[16,2,3,1664]{3,0,2,1:T(8,128)(2,1)S(1)} fusion(bf16[1,2,3,16,1664]{4,3,2,1,0:T(8,128)(2,1)} %param.5, pred[2]{0:T(512)(128)(4,1)S(1)} %broadcast_compare_fusion), kind=kLoop, calls=%fused_computation.5 | loop fusion | flops 159744 | bytes 638978 | tf_op jit(solution)/shard_map/jit(_where)/select_n | solution.py:135
  1.7 0.1 pad_dynamic-slice_fusion
  2.0 1.6 %collective-permute-done = bf16[12,2,3,1664]{3,0,2,1:T(8,128)(2,1)S(1)} collective-permute-done((bf16[12,2,3,1664]{3,0,2,1:T(8,128)(2,1)S(1)}, bf16[12,2,3,1664]{3,0,2,1:T(8,128)(2,1)S(1)}, u32[]{:S(2)}, u32[]{:S(2)}) %collective-permute-start) | collective-permute-done | bytes 239648 | tf_op jit(solution)/shard_map/ppermute | solution.py:33
  3.6 0.2 fusion
  3.8 1.6 %collective-permute-start.1 = (bf16[8,2,3,1664]{3,0,2,1:T(8,128)(2,1)S(1)}, bf16[8,2,3,1664]{3,0,2,1:T(8,128)(2,1)S(1)}, u32[]{:S(2)}, u32[]{:S(2)}) collective-permute-start(bf16[8,2,3,1664]{3,0,2,1:T(8,128)(2,1)S(1)} %constant_dynamic-slice_fusion.2), channel_id=1, source_target_pairs={{0,2},{1,3},{2,0},{3,1},{4,6},{5,7},{6,4},{7,5},{8,10},{9,11},{10,... | collective-permute-start | bytes 479240 | tf_op jit(solution)/shard_map/ppermute | solution.py:33
  5.4 4.7 %collective-permute-done.1 = bf16[8,2,3,1664]{3,0,2,1:T(8,128)(2,1)S(1)} collective-permute-done((bf16[8,2,3,1664]{3,0,2,1:T(8,128)(2,1)S(1)}, bf16[8,2,3,1664]{3,0,2,1:T(8,128)(2,1)S(1)}, u32[]{:S(2)}, u32[]{:S(2)}) %collective-permute-start.1) | collective-permute-done | bytes 159776 | tf_op jit(solution)/shard_map/ppermute | solution.py:33
  10.0 0.1 dynamic-slice_add_fusion.2
  10.2 0.5 %collective-permute-start.2 = (bf16[6,2,3,1664]{3,0,2,1:T(8,128)(2,1)S(1)}, bf16[6,2,3,1664]{3,0,2,1:T(8,128)(2,1)S(1)}, u32[]{:S(2)}, u32[]{:S(2)}) collective-permute-start(bf16[6,2,3,1664]{3,0,2,1:T(8,128)(2,1)S(1)} %constant_dynamic-slice_fusion.1), channel_id=1, source_target_pairs={{0,4},{1,5},{2,6},{3,7},{4,0},{5,1},{6,2},{7,3},{8,12},{9,13},{10,... | collective-permute-start | bytes 359432 | tf_op jit(solution)/shard_map/ppermute | solution.py:33
  10.7 1.1 %copy.12 = bf16[432,384]{0,1:T(8,128)(2,1)S(1)} copy(bf16[432,384]{1,0:T(8,128)(2,1)} %param.7) | data formatting | bytes 663552 | tf_op args[2]
  11.8 0.8 %copy.13 = bf16[384,12]{1,0:T(8,128)(2,1)S(1)} copy(bf16[384,12]{0,1:T(8,128)(2,1)} %param.9) | data formatting | bytes 18432 | tf_op args[4]
  12.7 2.8 %collective-permute-done.2 = bf16[6,2,3,1664]{3,0,2,1:T(8,128)(2,1)S(1)} collective-permute-done((bf16[6,2,3,1664]{3,0,2,1:T(8,128)(2,1)S(1)}, bf16[6,2,3,1664]{3,0,2,1:T(8,128)(2,1)S(1)}, u32[]{:S(2)}, u32[]{:S(2)}) %collective-permute-start.2) | collective-permute-done | bytes 119840 | tf_op jit(solution)/shard_map/ppermute | solution.py:33
  15.7 0.4 collective-permute-start.3
  16.1 8.0 %collective-permute-done.3 = bf16[5,2,3,1664]{3,0,2,1:T(8,128)(2,1)S(1)} collective-permute-done((bf16[5,2,3,1664]{3,0,2,1:T(8,128)(2,1)S(1)}, bf16[5,2,3,1664]{3,0,2,1:T(8,128)(2,1)S(1)}, u32[]{:S(2)}, u32[]{:S(2)}) %collective-permute-start.3) | collective-permute-done | bytes 99872 | tf_op jit(solution)/shard_map/ppermute | solution.py:33
  24.2 0.6 %reshape.16 = bf16[5,6,104,16]{3,2,1,0:T(8,128)(2,1)S(1)} reshape(bf16[5,2,3,1664]{3,2,1,0:T(4,128)(2,1)S(1)} %copy.10) | data formatting | bytes 199680 | tf_op jit(solution)/shard_map/reshape | solution.py:140
  24.8 0.3 pad.13
  25.1 0.4 copy.16.xt_ref
  25.5 14.1 %shard_map.55 = f32[1,768,128]{2,1,0:T(8,128)S(1)} custom-call(f32[3]{0:T(128)S(1)} %and_convert_fusion.row_ok_ref, bf16[5,16,1024]{2,1,0:T(8,128)(2,1)S(1)} %copy.16.xt_ref, bf16[384,432]{1,0:T(8,128)(2,1)S(1)} %bitcast.16, bf16[9,1152,384]{2,1,0:T(8,128)(2,1)} %bitcast.17, bf16[384,128]{1,0:T(8,128)(2,1)S(1)} %pad.14.w_pix_ref), custom_call_target="tpu_custom_call" | custom-call | tf_op jit(solution)/shard_map/pallas_call | solution.py:99
  39.7 0.1 copy.14
  39.9 0.5 %copy.15 = bf16[2,3,1,2,104,2,3]{6,5,4,3,1,0,2:T(2,128)(2,1)S(1)} copy(bf16[2,3,1,2,104,2,3]{4,1,0,6,5,3,2:T(4,128)(2,1)S(1)} %slice_bitcast_fusion) | data formatting | bytes 29952 | tf_op jit(solution)/shard_map/convert_element_type | solution.py:149
  40.5 0.7 %convert_element_type.18 = bf16[2,3,2,624]{3,2,1,0:T(2,128)(2,1)S(1)} reshape(bf16[2,3,1,2,104,2,3]{6,5,4,3,1,0,2:T(2,128)(2,1)S(1)} %copy.15) | data formatting | bytes 29952 | tf_op jit(solution)/shard_map/convert_element_type | solution.py:149
  41.1 1.9 %collective-permute-start.4 = (bf16[2,3,2,624]{3,2,1,0:T(2,128)(2,1)S(1)}, bf16[2,3,2,624]{3,2,1,0:T(2,128)(2,1)S(1)}, u32[]{:S(2)}, u32[]{:S(2)}) collective-permute-start(bf16[2,3,2,624]{3,2,1,0:T(2,128)(2,1)S(1)} %convert_element_type.18), channel_id=1, source_target_pairs={{0,0},{1,8},{2,4},{3,12},{4,2},{5,10},{6,6},{7,14},{8,1},{9,9},{10... | collective-permute-start | bytes 44936 | tf_op jit(solution)/shard_map/ppermute | solution.py:150
  43.1 5.8 %collective-permute-done.4 = bf16[2,3,2,624]{3,2,1,0:T(2,128)(2,1)S(1)} collective-permute-done((bf16[2,3,2,624]{3,2,1,0:T(2,128)(2,1)S(1)}, bf16[2,3,2,624]{3,2,1,0:T(2,128)(2,1)S(1)}, u32[]{:S(2)}, u32[]{:S(2)}) %collective-permute-start.4) | collective-permute-done | bytes 15008 | tf_op jit(solution)/shard_map/ppermute | solution.py:150
  48.9 0.6 %copy.18 = bf16[2,3,2,624]{3,2,1,0:T(2,128)(2,1)} copy(bf16[2,3,2,624]{3,2,1,0:T(2,128)(2,1)S(1)} %collective-permute-done.4) | data formatting | bytes 29952
  (12 shorter events, 0.5 us)
Async XLA Ops:
  1.9 1.7 %collective-permute-start = (bf16[12,2,3,1664]{3,0,2,1:T(8,128)(2,1)S(1)}, bf16[12,2,3,1664]{3,0,2,1:T(8,128)(2,1)S(1)}, u32[]{:S(2)}, u32[]{:S(2)}) collective-permute-start(bf16[12,2,3,1664]{3,0,2,1:T(8,128)(2,1)S(1)} %pad_dynamic-slice_fusion), channel_id=1, source_target_pairs={{0,1},{1,0},{2,3},{3,2},{4,5},{5,4},{6,7},{7,6},{8,9},{9,8},{10,11... | collective-permute-start | bytes 718856 | tf_op jit(solution)/shard_map/ppermute | solution.py:33
  3.8 6.2 %collective-permute-start.1 = (bf16[8,2,3,1664]{3,0,2,1:T(8,128)(2,1)S(1)}, bf16[8,2,3,1664]{3,0,2,1:T(8,128)(2,1)S(1)}, u32[]{:S(2)}, u32[]{:S(2)}) collective-permute-start(bf16[8,2,3,1664]{3,0,2,1:T(8,128)(2,1)S(1)} %constant_dynamic-slice_fusion.2), channel_id=1, source_target_pairs={{0,2},{1,3},{2,0},{3,1},{4,6},{5,7},{6,4},{7,5},{8,10},{9,11},{10,... | collective-permute-start | bytes 479240 | tf_op jit(solution)/shard_map/ppermute | solution.py:33
  10.2 5.4 %collective-permute-start.2 = (bf16[6,2,3,1664]{3,0,2,1:T(8,128)(2,1)S(1)}, bf16[6,2,3,1664]{3,0,2,1:T(8,128)(2,1)S(1)}, u32[]{:S(2)}, u32[]{:S(2)}) collective-permute-start(bf16[6,2,3,1664]{3,0,2,1:T(8,128)(2,1)S(1)} %constant_dynamic-slice_fusion.1), channel_id=1, source_target_pairs={{0,4},{1,5},{2,6},{3,7},{4,0},{5,1},{6,2},{7,3},{8,12},{9,13},{10,... | collective-permute-start | bytes 359432 | tf_op jit(solution)/shard_map/ppermute | solution.py:33
  15.7 8.4 %collective-permute-start.3 = (bf16[5,2,3,1664]{3,0,2,1:T(8,128)(2,1)S(1)}, bf16[5,2,3,1664]{3,0,2,1:T(8,128)(2,1)S(1)}, u32[]{:S(2)}, u32[]{:S(2)}) collective-permute-start(bf16[5,2,3,1664]{3,0,2,1:T(8,128)(2,1)S(1)} %constant_dynamic-slice_fusion), channel_id=1, source_target_pairs={{0,8},{1,9},{2,10},{3,11},{4,12},{5,13},{6,14},{7,15},{8,0},{9,1},... | collective-permute-start | bytes 299528 | tf_op jit(solution)/shard_map/ppermute | solution.py:33
  41.1 7.7 %collective-permute-start.4 = (bf16[2,3,2,624]{3,2,1,0:T(2,128)(2,1)S(1)}, bf16[2,3,2,624]{3,2,1,0:T(2,128)(2,1)S(1)}, u32[]{:S(2)}, u32[]{:S(2)}) collective-permute-start(bf16[2,3,2,624]{3,2,1,0:T(2,128)(2,1)S(1)} %convert_element_type.18), channel_id=1, source_target_pairs={{0,0},{1,8},{2,4},{3,12},{4,2},{5,10},{6,6},{7,14},{8,1},{9,9},{10... | collective-permute-start | bytes 44936 | tf_op jit(solution)/shard_map/ppermute | solution.py:150

commit v12 on v11

--- a/solution.py
+++ b/solution.py
@@ -84,7 +84,7 @@
                 acc = acc + jnp.dot(piece, w_vmem[a * taps + b], preferred_element_type=jnp.float32)
         scale = lax.rsqrt(jnp.mean(acc * acc, axis=-1, keepdims=True) + epsilon)
         normed = (acc * scale).astype(jnp.bfloat16)
-        out_ref[jo] = jnp.dot(normed, w_pix_ref[...], preferred_element_type=jnp.float32)
+        out_ref[jo] = jnp.dot(normed, w_pix_ref[...], preferred_element_type=jnp.float32).astype(out_ref.dtype)
 
 
 def decode(row_ok, xt, conv_in, conv_mid, to_pixels, columns):
@@ -98,7 +98,7 @@
     vmem = pltpu.MemorySpace.VMEM
     out = pl.pallas_call(
         functools.partial(decode_kernel, columns),
-        out_shape=jax.ShapeDtypeStruct((rows_in - 2, span, LANE), jnp.float32),
+        out_shape=jax.ShapeDtypeStruct((rows_in - 2, span, LANE), jnp.bfloat16),
         in_specs=[
             pl.BlockSpec(memory_space=pltpu.MemorySpace.SMEM),
             pl.BlockSpec(memory_space=vmem),
@@ -146,7 +146,7 @@
     projected = decode(row_ok, xt, conv_in, conv_mid, to_pixels, columns)
     projected = projected.reshape(rows_dev, groups, frames, LANE, 2, 2, 3)[:, :, :, :columns]
     projected = projected.transpose(1, 2, 0, 4, 3, 5, 6)
-    pixels = projected.reshape(groups, frames, 2 * rows_dev, 6 * columns).astype(jnp.bfloat16)
+    pixels = projected.reshape(groups, frames, 2 * rows_dev, 6 * columns)
     return lax.ppermute(pixels, "dev", [(i, reverse_bits(i, bits)) for i in range(n)])
 
 

time: 49.7 us -> 49.7 us (level)
    convert_element_type x3 -> x0, local copies, waits for them, and re-layouts: 1.23 us -> none  [local(): projected.reshape(groups, frames, 2 * rows_dev, 6 * columns)]
    reshape x0 -> x1, local copies, waits for them, and re-layouts: none -> 0.67 us  [local(): pixels = projected.reshape(groups, frames, 2 * rows_dev, 6 * columns)]
    transpose x0 -> x2, local copies, waits for them, and re-layouts: none -> 0.55 us  [local(): projected = projected.transpose(1, 2, 0, 4, 3, 5, 6)]
where the time goes in v12:
time: 49.7 us; the launch traced here: 49.4 us
  waiting for transfers between devices  22.9 us (46%)
  Pallas kernels  14.1 us (28%)
  local copies, waits for them, and re-layouts  5.66 us (11%)
  starting transfers between devices  4.46 us (9%)
  other arithmetic  2.12 us (4%)
    ppermute x4, waiting for transfers between devices, gather_rows(): x = own + lax.ppermute(send, 'dev', pairs)  17.1 us
    pallas_call x1, Pallas kernels, decode(): pl.pallas_call(functools.partial(decode_kernel, columns), out_shape=jax.S...  14.1 us
    ppermute x1, waiting for transfers between devices, local(): lax.ppermute(pixels, 'dev', [(i, reverse_bits(i, bits)) for i in range(n)])  5.82 us
    unnamed x3, local copies, waits for them, and re-layouts  2.59 us
    ppermute x4, starting transfers between devices, gather_rows(): x = own + lax.ppermute(send, 'dev', pairs)  2.54 us
    ppermute x1, starting transfers between devices, local(): lax.ppermute(pixels, 'dev', [(i, reverse_bits(i, bits)) for i in range(n)])  1.92 us
    select_n x1, other arithmetic, local(): x = jnp.where(keep[None, :, None, None], x, jnp.zeros_like(x))  1.07 us
  transfers between devices with their start and end apart: 5, of which 5 were waited for; matrix products, arithmetic and copies ran while one was open for 4% of the time, Pallas kernels for 0%

profile of v12, /device:TPU:24, one launch (start us, length us, event | category | flops | bytes accessed | tf_op | source)
XLA Modules:
  0.0 49.4 jit_solution(6436087715805494353)
XLA Ops:
  0.0 0.7 %broadcast_compare_fusion = pred[2]{0:T(512)(128)(4,1)S(1)} fusion(s32[2]{0:T(128)} %param.6, s32[]{:T(128)S(6)} %axis_index.12), kind=kLoop, calls=%fused_computation.13 | loop fusion | flops 2 | bytes 14 | tf_op jit(solution)/shard_map/eq | solution.py:134
  0.7 1.1 %fusion.1 = bf16[16,2,3,1664]{3,0,2,1:T(8,128)(2,1)S(1)} fusion(bf16[1,2,3,16,1664]{4,3,2,1,0:T(8,128)(2,1)} %param.5, pred[2]{0:T(512)(128)(4,1)S(1)} %broadcast_compare_fusion), kind=kLoop, calls=%fused_computation.4 | loop fusion | flops 159744 | bytes 638978 | tf_op jit(solution)/shard_map/jit(_where)/select_n | solution.py:135
  1.7 0.1 pad_dynamic-slice_fusion
  2.0 1.6 %collective-permute-done = bf16[12,2,3,1664]{3,0,2,1:T(8,128)(2,1)S(1)} collective-permute-done((bf16[12,2,3,1664]{3,0,2,1:T(8,128)(2,1)S(1)}, bf16[12,2,3,1664]{3,0,2,1:T(8,128)(2,1)S(1)}, u32[]{:S(2)}, u32[]{:S(2)}) %collective-permute-start) | collective-permute-done | bytes 239648 | tf_op jit(solution)/shard_map/ppermute | solution.py:33
  3.6 0.2 fusion
  3.8 1.6 %collective-permute-start.1 = (bf16[8,2,3,1664]{3,0,2,1:T(8,128)(2,1)S(1)}, bf16[8,2,3,1664]{3,0,2,1:T(8,128)(2,1)S(1)}, u32[]{:S(2)}, u32[]{:S(2)}) collective-permute-start(bf16[8,2,3,1664]{3,0,2,1:T(8,128)(2,1)S(1)} %constant_dynamic-slice_fusion.2), channel_id=1, source_target_pairs={{0,2},{1,3},{2,0},{3,1},{4,6},{5,7},{6,4},{7,5},{8,10},{9,11},{10,... | collective-permute-start | bytes 479240 | tf_op jit(solution)/shard_map/ppermute | solution.py:33
  5.4 4.7 %collective-permute-done.1 = bf16[8,2,3,1664]{3,0,2,1:T(8,128)(2,1)S(1)} collective-permute-done((bf16[8,2,3,1664]{3,0,2,1:T(8,128)(2,1)S(1)}, bf16[8,2,3,1664]{3,0,2,1:T(8,128)(2,1)S(1)}, u32[]{:S(2)}, u32[]{:S(2)}) %collective-permute-start.1) | collective-permute-done | bytes 159776 | tf_op jit(solution)/shard_map/ppermute | solution.py:33
  10.0 0.1 dynamic-slice_add_fusion.2
  10.2 0.5 %collective-permute-start.2 = (bf16[6,2,3,1664]{3,0,2,1:T(8,128)(2,1)S(1)}, bf16[6,2,3,1664]{3,0,2,1:T(8,128)(2,1)S(1)}, u32[]{:S(2)}, u32[]{:S(2)}) collective-permute-start(bf16[6,2,3,1664]{3,0,2,1:T(8,128)(2,1)S(1)} %constant_dynamic-slice_fusion.1), channel_id=1, source_target_pairs={{0,4},{1,5},{2,6},{3,7},{4,0},{5,1},{6,2},{7,3},{8,12},{9,13},{10,... | collective-permute-start | bytes 359432 | tf_op jit(solution)/shard_map/ppermute | solution.py:33
  10.7 1.1 %copy.12 = bf16[432,384]{0,1:T(8,128)(2,1)S(1)} copy(bf16[432,384]{1,0:T(8,128)(2,1)} %param.7) | data formatting | bytes 663552 | tf_op args[2]
  11.8 0.8 %copy.13 = bf16[384,12]{1,0:T(8,128)(2,1)S(1)} copy(bf16[384,12]{0,1:T(8,128)(2,1)} %param.9) | data formatting | bytes 18432 | tf_op args[4]
  12.7 2.8 %collective-permute-done.2 = bf16[6,2,3,1664]{3,0,2,1:T(8,128)(2,1)S(1)} collective-permute-done((bf16[6,2,3,1664]{3,0,2,1:T(8,128)(2,1)S(1)}, bf16[6,2,3,1664]{3,0,2,1:T(8,128)(2,1)S(1)}, u32[]{:S(2)}, u32[]{:S(2)}) %collective-permute-start.2) | collective-permute-done | bytes 119840 | tf_op jit(solution)/shard_map/ppermute | solution.py:33
  15.7 0.4 collective-permute-start.3
  16.1 8.0 %collective-permute-done.3 = bf16[5,2,3,1664]{3,0,2,1:T(8,128)(2,1)S(1)} collective-permute-done((bf16[5,2,3,1664]{3,0,2,1:T(8,128)(2,1)S(1)}, bf16[5,2,3,1664]{3,0,2,1:T(8,128)(2,1)S(1)}, u32[]{:S(2)}, u32[]{:S(2)}) %collective-permute-start.3) | collective-permute-done | bytes 99872 | tf_op jit(solution)/shard_map/ppermute | solution.py:33
  24.2 0.6 %reshape.16 = bf16[5,6,104,16]{3,2,1,0:T(8,128)(2,1)S(1)} reshape(bf16[5,2,3,1664]{3,2,1,0:T(4,128)(2,1)S(1)} %copy.10) | data formatting | bytes 199680 | tf_op jit(solution)/shard_map/reshape | solution.py:140
  24.8 0.3 pad.13
  25.1 0.4 copy.16.xt_ref
  25.5 14.1 %shard_map.55 = bf16[1,768,128]{2,1,0:T(8,128)(2,1)S(1)} custom-call(f32[3]{0:T(128)S(1)} %and_convert_fusion.row_ok_ref, bf16[5,16,1024]{2,1,0:T(8,128)(2,1)S(1)} %copy.16.xt_ref, bf16[384,432]{1,0:T(8,128)(2,1)S(1)} %bitcast.17, bf16[9,1152,384]{2,1,0:T(8,128)(2,1)} %bitcast.19, bf16[384,128]{1,0:T(8,128)(2,1)S(1)} %pad.14.w_pix_ref), custom_call_target="tpu_custom_call" | custom-call | tf_op jit(solution)/shard_map/pallas_call | solution.py:99
  39.7 0.1 copy.14
  39.9 0.5 %copy.15 = bf16[2,3,1,2,104,2,3]{6,5,4,3,1,0,2:T(2,128)(2,1)S(1)} copy(bf16[2,3,1,2,104,2,3]{4,1,0,6,5,3,2:T(4,128)(2,1)S(1)} %slice_bitcast_fusion) | data formatting | bytes 29952 | tf_op jit(solution)/shard_map/transpose | solution.py:148
  40.4 0.7 %reshape.20 = bf16[2,3,2,624]{3,2,1,0:T(2,128)(2,1)S(1)} reshape(bf16[2,3,1,2,104,2,3]{6,5,4,3,1,0,2:T(2,128)(2,1)S(1)} %copy.15) | data formatting | bytes 29952 | tf_op jit(solution)/shard_map/reshape | solution.py:149
  41.1 1.9 %collective-permute-start.4 = (bf16[2,3,2,624]{3,2,1,0:T(2,128)(2,1)S(1)}, bf16[2,3,2,624]{3,2,1,0:T(2,128)(2,1)S(1)}, u32[]{:S(2)}, u32[]{:S(2)}) collective-permute-start(bf16[2,3,2,624]{3,2,1,0:T(2,128)(2,1)S(1)} %reshape.20), channel_id=1, source_target_pairs={{0,0},{1,8},{2,4},{3,12},{4,2},{5,10},{6,6},{7,14},{8,1},{9,9},{10... | collective-permute-start | bytes 44936 | tf_op jit(solution)/shard_map/ppermute | solution.py:150
  43.0 5.8 %collective-permute-done.4 = bf16[2,3,2,624]{3,2,1,0:T(2,128)(2,1)S(1)} collective-permute-done((bf16[2,3,2,624]{3,2,1,0:T(2,128)(2,1)S(1)}, bf16[2,3,2,624]{3,2,1,0:T(2,128)(2,1)S(1)}, u32[]{:S(2)}, u32[]{:S(2)}) %collective-permute-start.4) | collective-permute-done | bytes 15008 | tf_op jit(solution)/shard_map/ppermute | solution.py:150
  48.8 0.6 %copy.18 = bf16[2,3,2,624]{3,2,1,0:T(2,128)(2,1)} copy(bf16[2,3,2,624]{3,2,1,0:T(2,128)(2,1)S(1)} %collective-permute-done.4) | data formatting | bytes 29952
  (11 shorter events, 0.5 us)
Async XLA Ops:
  1.9 1.7 %collective-permute-start = (bf16[12,2,3,1664]{3,0,2,1:T(8,128)(2,1)S(1)}, bf16[12,2,3,1664]{3,0,2,1:T(8,128)(2,1)S(1)}, u32[]{:S(2)}, u32[]{:S(2)}) collective-permute-start(bf16[12,2,3,1664]{3,0,2,1:T(8,128)(2,1)S(1)} %pad_dynamic-slice_fusion), channel_id=1, source_target_pairs={{0,1},{1,0},{2,3},{3,2},{4,5},{5,4},{6,7},{7,6},{8,9},{9,8},{10,11... | collective-permute-start | bytes 718856 | tf_op jit(solution)/shard_map/ppermute | solution.py:33
  3.8 6.2 %collective-permute-start.1 = (bf16[8,2,3,1664]{3,0,2,1:T(8,128)(2,1)S(1)}, bf16[8,2,3,1664]{3,0,2,1:T(8,128)(2,1)S(1)}, u32[]{:S(2)}, u32[]{:S(2)}) collective-permute-start(bf16[8,2,3,1664]{3,0,2,1:T(8,128)(2,1)S(1)} %constant_dynamic-slice_fusion.2), channel_id=1, source_target_pairs={{0,2},{1,3},{2,0},{3,1},{4,6},{5,7},{6,4},{7,5},{8,10},{9,11},{10,... | collective-permute-start | bytes 479240 | tf_op jit(solution)/shard_map/ppermute | solution.py:33
  10.2 5.4 %collective-permute-start.2 = (bf16[6,2,3,1664]{3,0,2,1:T(8,128)(2,1)S(1)}, bf16[6,2,3,1664]{3,0,2,1:T(8,128)(2,1)S(1)}, u32[]{:S(2)}, u32[]{:S(2)}) collective-permute-start(bf16[6,2,3,1664]{3,0,2,1:T(8,128)(2,1)S(1)} %constant_dynamic-slice_fusion.1), channel_id=1, source_target_pairs={{0,4},{1,5},{2,6},{3,7},{4,0},{5,1},{6,2},{7,3},{8,12},{9,13},{10,... | collective-permute-start | bytes 359432 | tf_op jit(solution)/shard_map/ppermute | solution.py:33
  15.7 8.4 %collective-permute-start.3 = (bf16[5,2,3,1664]{3,0,2,1:T(8,128)(2,1)S(1)}, bf16[5,2,3,1664]{3,0,2,1:T(8,128)(2,1)S(1)}, u32[]{:S(2)}, u32[]{:S(2)}) collective-permute-start(bf16[5,2,3,1664]{3,0,2,1:T(8,128)(2,1)S(1)} %constant_dynamic-slice_fusion), channel_id=1, source_target_pairs={{0,8},{1,9},{2,10},{3,11},{4,12},{5,13},{6,14},{7,15},{8,0},{9,1},... | collective-permute-start | bytes 299528 | tf_op jit(solution)/shard_map/ppermute | solution.py:33
  41.1 7.7 %collective-permute-start.4 = (bf16[2,3,2,624]{3,2,1,0:T(2,128)(2,1)S(1)}, bf16[2,3,2,624]{3,2,1,0:T(2,128)(2,1)S(1)}, u32[]{:S(2)}, u32[]{:S(2)}) collective-permute-start(bf16[2,3,2,624]{3,2,1,0:T(2,128)(2,1)S(1)} %reshape.20), channel_id=1, source_target_pairs={{0,0},{1,8},{2,4},{3,12},{4,2},{5,10},{6,6},{7,14},{8,1},{9,9},{10... | collective-permute-start | bytes 44936 | tf_op jit(solution)/shard_map/ppermute | solution.py:150

commit v13 on v12

--- a/solution.py
+++ b/solution.py
@@ -20,14 +20,14 @@
     return sum(((value >> b) & 1) << (bits - 1 - b) for b in range(bits))
 
 
-def gather_rows(x, n, rows_dev, slot):
+def gather_rows(x, n, rows_dev, slot, axis=0):
     bits = n.bit_length() - 1
     for k in reversed(range(bits)):
         half = (1 << k) * rows_dev
         size = half + 2 * HALO
         bit = (slot >> k) & 1
-        own = lax.dynamic_slice_in_dim(x, bit * half, size, 0)
-        send = lax.dynamic_slice_in_dim(x, (1 - bit) * half, size, 0)
+        own = lax.dynamic_slice_in_dim(x, bit * half, size, axis)
+        send = lax.dynamic_slice_in_dim(x, (1 - bit) * half, size, axis)
         flip = 1 << (bits - 1 - k)
         pairs = [(i, i ^ flip) for i in range(n)]
         x = own + lax.ppermute(send, "dev", pairs)
@@ -130,14 +130,13 @@
     steps = groups * frames
     assert columns < LANE
 
-    x = jnp.transpose(latents[0], (2, 0, 1, 3))
     keep = owners == position
-    x = jnp.where(keep[None, :, None, None], x, jnp.zeros_like(x))
-    x = jnp.pad(x, ((HALO, HALO), (0, 0), (0, 0), (0, 0)))
-    x = gather_rows(x, n, rows_dev, slot)
+    x = jnp.where(keep[:, None, None, None], latents[0], jnp.zeros_like(latents[0]))
+    x = jnp.pad(x, ((0, 0), (0, 0), (HALO, HALO), (0, 0)))
+    x = gather_rows(x, n, rows_dev, slot, axis=2)
 
     rows_in = rows_dev + 2
-    xt = x.reshape(rows_dev + 2 * HALO, steps, columns, ZC).transpose(0, 3, 1, 2)
+    xt = x.reshape(steps, rows_dev + 2 * HALO, columns, ZC).transpose(1, 3, 0, 2)
     xt = jnp.pad(xt, ((0, 0), (0, 0), (2, 0), (0, LANE - columns)))
     xt = xt.reshape(rows_dev + 2 * HALO, ZC, (steps + 2) * LANE)
     row_of = slot * rows_dev - 1 + jnp.arange(rows_in)

time: 49.7 us -> 49.7 us (level)
  no operation moved by 1% of the time
where the time goes in v13:
time: 49.7 us; the launch traced here: 49.4 us
  waiting for transfers between devices  22.9 us (46%)
  Pallas kernels  14.1 us (28%)
  local copies, waits for them, and re-layouts  5.66 us (11%)
  starting transfers between devices  4.46 us (9%)
  other arithmetic  2.12 us (4%)
    ppermute x4, waiting for transfers between devices, gather_rows(): x = own + lax.ppermute(send, 'dev', pairs)  17.1 us
    pallas_call x1, Pallas kernels, decode(): pl.pallas_call(functools.partial(decode_kernel, columns), out_shape=jax.S...  14.1 us
    ppermute x1, waiting for transfers between devices, local(): lax.ppermute(pixels, 'dev', [(i, reverse_bits(i, bits)) for i in range(n)])  5.82 us
    unnamed x3, local copies, waits for them, and re-layouts  2.59 us
    ppermute x4, starting transfers between devices, gather_rows(): x = own + lax.ppermute(send, 'dev', pairs)  2.54 us
    ppermute x1, starting transfers between devices, local(): lax.ppermute(pixels, 'dev', [(i, reverse_bits(i, bits)) for i in range(n)])  1.92 us
    select_n x1, other arithmetic, local(): jnp.where(keep[:, None, None, None], latents[0], jnp.zeros_like(latents[0]))  1.07 us
  transfers between devices with their start and end apart: 5, of which 5 were waited for; matrix products, arithmetic and copies ran while one was open for 4% of the time, Pallas kernels for 0%

profile of v13, /device:TPU:24, one launch (start us, length us, event | category | flops | bytes accessed | tf_op | source)
XLA Modules:
  0.0 49.4 jit_solution(6436087715805494353)
XLA Ops:
  0.0 0.7 %broadcast_compare_fusion = pred[2]{0:T(512)(128)(4,1)S(1)} fusion(s32[2]{0:T(128)} %param.6, s32[]{:T(128)S(6)} %axis_index.12), kind=kLoop, calls=%fused_computation.12 | loop fusion | flops 2 | bytes 14 | tf_op jit(solution)/shard_map/eq | solution.py:133
  0.7 1.1 %bitcast_select_fusion = bf16[2,3,16,1664]{3,2,1,0:T(8,128)(2,1)S(1)} fusion(bf16[1,2,3,16,1664]{4,3,2,1,0:T(8,128)(2,1)} %param.5, pred[2]{0:T(512)(128)(4,1)S(1)} %broadcast_compare_fusion), kind=kLoop, calls=%fused_computation.3 | loop fusion | flops 159744 | bytes 638978 | tf_op jit(solution)/shard_map/jit(_where)/select_n | solution.py:134
  1.7 0.1 pad_dynamic-slice_fusion
  2.0 1.6 %collective-permute-done = bf16[2,3,12,1664]{3,2,1,0:T(8,128)(2,1)S(1)} collective-permute-done((bf16[2,3,12,1664]{3,2,1,0:T(8,128)(2,1)S(1)}, bf16[2,3,12,1664]{3,2,1,0:T(8,128)(2,1)S(1)}, u32[]{:S(2)}, u32[]{:S(2)}) %collective-permute-start) | collective-permute-done | bytes 239648 | tf_op jit(solution)/shard_map/ppermute | solution.py:33
  3.6 0.2 fusion
  3.8 1.6 %collective-permute-start.1 = (bf16[2,3,8,1664]{3,2,1,0:T(8,128)(2,1)S(1)}, bf16[2,3,8,1664]{3,2,1,0:T(8,128)(2,1)S(1)}, u32[]{:S(2)}, u32[]{:S(2)}) collective-permute-start(bf16[2,3,8,1664]{3,2,1,0:T(8,128)(2,1)S(1)} %constant_dynamic-slice_fusion.2), channel_id=1, source_target_pairs={{0,2},{1,3},{2,0},{3,1},{4,6},{5,7},{6,4},{7,5},{8,10},{9,11},{10,... | collective-permute-start | bytes 479240 | tf_op jit(solution)/shard_map/ppermute | solution.py:33
  5.4 4.7 %collective-permute-done.1 = bf16[2,3,8,1664]{3,2,1,0:T(8,128)(2,1)S(1)} collective-permute-done((bf16[2,3,8,1664]{3,2,1,0:T(8,128)(2,1)S(1)}, bf16[2,3,8,1664]{3,2,1,0:T(8,128)(2,1)S(1)}, u32[]{:S(2)}, u32[]{:S(2)}) %collective-permute-start.1) | collective-permute-done | bytes 159776 | tf_op jit(solution)/shard_map/ppermute | solution.py:33
  10.0 0.1 dynamic-slice_add_fusion.2
  10.2 0.5 %collective-permute-start.2 = (bf16[2,3,6,1664]{3,2,1,0:T(8,128)(2,1)S(1)}, bf16[2,3,6,1664]{3,2,1,0:T(8,128)(2,1)S(1)}, u32[]{:S(2)}, u32[]{:S(2)}) collective-permute-start(bf16[2,3,6,1664]{3,2,1,0:T(8,128)(2,1)S(1)} %constant_dynamic-slice_fusion.1), channel_id=1, source_target_pairs={{0,4},{1,5},{2,6},{3,7},{4,0},{5,1},{6,2},{7,3},{8,12},{9,13},{10,... | collective-permute-start | bytes 359432 | tf_op jit(solution)/shard_map/ppermute | solution.py:33
  10.7 1.1 %copy.12 = bf16[432,384]{0,1:T(8,128)(2,1)S(1)} copy(bf16[432,384]{1,0:T(8,128)(2,1)} %param.7) | data formatting | bytes 663552 | tf_op args[2]
  11.8 0.8 %copy.13 = bf16[384,12]{1,0:T(8,128)(2,1)S(1)} copy(bf16[384,12]{0,1:T(8,128)(2,1)} %param.9) | data formatting | bytes 18432 | tf_op args[4]
  12.7 2.8 %collective-permute-done.2 = bf16[2,3,6,1664]{3,2,1,0:T(8,128)(2,1)S(1)} collective-permute-done((bf16[2,3,6,1664]{3,2,1,0:T(8,128)(2,1)S(1)}, bf16[2,3,6,1664]{3,2,1,0:T(8,128)(2,1)S(1)}, u32[]{:S(2)}, u32[]{:S(2)}) %collective-permute-start.2) | collective-permute-done | bytes 119840 | tf_op jit(solution)/shard_map/ppermute | solution.py:33
  15.7 0.4 collective-permute-start.3
  16.1 8.0 %collective-permute-done.3 = bf16[2,3,5,1664]{3,2,1,0:T(8,128)(2,1)S(1)} collective-permute-done((bf16[2,3,5,1664]{3,2,1,0:T(8,128)(2,1)S(1)}, bf16[2,3,5,1664]{3,2,1,0:T(8,128)(2,1)S(1)}, u32[]{:S(2)}, u32[]{:S(2)}) %collective-permute-start.3) | collective-permute-done | bytes 99872 | tf_op jit(solution)/shard_map/ppermute | solution.py:33
  24.2 0.6 %reshape.16 = bf16[6,5,104,16]{3,2,0,1:T(8,128)(2,1)S(1)} reshape(bf16[2,3,5,1664]{3,1,0,2:T(4,128)(2,1)S(1)} %copy.10) | data formatting | bytes 199680 | tf_op jit(solution)/shard_map/reshape | solution.py:139
  24.8 0.3 pad.13
  25.1 0.4 copy.16.xt_ref
  25.5 14.1 %shard_map.55 = bf16[1,768,128]{2,1,0:T(8,128)(2,1)S(1)} custom-call(f32[3]{0:T(128)S(1)} %and_convert_fusion.row_ok_ref, bf16[5,16,1024]{2,1,0:T(8,128)(2,1)S(1)} %copy.16.xt_ref, bf16[384,432]{1,0:T(8,128)(2,1)S(1)} %bitcast.15, bf16[9,1152,384]{2,1,0:T(8,128)(2,1)} %bitcast.17, bf16[384,128]{1,0:T(8,128)(2,1)S(1)} %pad.14.w_pix_ref), custom_call_target="tpu_custom_call" | custom-call | tf_op jit(solution)/shard_map/pallas_call | solution.py:99
  39.7 0.1 copy.14
  39.9 0.5 %copy.15 = bf16[2,3,1,2,104,2,3]{6,5,4,3,1,0,2:T(2,128)(2,1)S(1)} copy(bf16[2,3,1,2,104,2,3]{4,1,0,6,5,3,2:T(4,128)(2,1)S(1)} %slice_bitcast_fusion) | data formatting | bytes 29952 | tf_op jit(solution)/shard_map/transpose | solution.py:147
  40.4 0.7 %reshape.20 = bf16[2,3,2,624]{3,2,1,0:T(2,128)(2,1)S(1)} reshape(bf16[2,3,1,2,104,2,3]{6,5,4,3,1,0,2:T(2,128)(2,1)S(1)} %copy.15) | data formatting | bytes 29952 | tf_op jit(solution)/shard_map/reshape | solution.py:148
  41.1 1.9 %collective-permute-start.4 = (bf16[2,3,2,624]{3,2,1,0:T(2,128)(2,1)S(1)}, bf16[2,3,2,624]{3,2,1,0:T(2,128)(2,1)S(1)}, u32[]{:S(2)}, u32[]{:S(2)}) collective-permute-start(bf16[2,3,2,624]{3,2,1,0:T(2,128)(2,1)S(1)} %reshape.20), channel_id=1, source_target_pairs={{0,0},{1,8},{2,4},{3,12},{4,2},{5,10},{6,6},{7,14},{8,1},{9,9},{10... | collective-permute-start | bytes 44936 | tf_op jit(solution)/shard_map/ppermute | solution.py:149
  43.0 5.8 %collective-permute-done.4 = bf16[2,3,2,624]{3,2,1,0:T(2,128)(2,1)S(1)} collective-permute-done((bf16[2,3,2,624]{3,2,1,0:T(2,128)(2,1)S(1)}, bf16[2,3,2,624]{3,2,1,0:T(2,128)(2,1)S(1)}, u32[]{:S(2)}, u32[]{:S(2)}) %collective-permute-start.4) | collective-permute-done | bytes 15008 | tf_op jit(solution)/shard_map/ppermute | solution.py:149
  48.8 0.6 %copy.18 = bf16[2,3,2,624]{3,2,1,0:T(2,128)(2,1)} copy(bf16[2,3,2,624]{3,2,1,0:T(2,128)(2,1)S(1)} %collective-permute-done.4) | data formatting | bytes 29952
  (11 shorter events, 0.5 us)
Async XLA Ops:
  1.9 1.7 %collective-permute-start = (bf16[2,3,12,1664]{3,2,1,0:T(8,128)(2,1)S(1)}, bf16[2,3,12,1664]{3,2,1,0:T(8,128)(2,1)S(1)}, u32[]{:S(2)}, u32[]{:S(2)}) collective-permute-start(bf16[2,3,12,1664]{3,2,1,0:T(8,128)(2,1)S(1)} %pad_dynamic-slice_fusion), channel_id=1, source_target_pairs={{0,1},{1,0},{2,3},{3,2},{4,5},{5,4},{6,7},{7,6},{8,9},{9,8},{10,11... | collective-permute-start | bytes 718856 | tf_op jit(solution)/shard_map/ppermute | solution.py:33
  3.8 6.2 %collective-permute-start.1 = (bf16[2,3,8,1664]{3,2,1,0:T(8,128)(2,1)S(1)}, bf16[2,3,8,1664]{3,2,1,0:T(8,128)(2,1)S(1)}, u32[]{:S(2)}, u32[]{:S(2)}) collective-permute-start(bf16[2,3,8,1664]{3,2,1,0:T(8,128)(2,1)S(1)} %constant_dynamic-slice_fusion.2), channel_id=1, source_target_pairs={{0,2},{1,3},{2,0},{3,1},{4,6},{5,7},{6,4},{7,5},{8,10},{9,11},{10,... | collective-permute-start | bytes 479240 | tf_op jit(solution)/shard_map/ppermute | solution.py:33
  10.2 5.4 %collective-permute-start.2 = (bf16[2,3,6,1664]{3,2,1,0:T(8,128)(2,1)S(1)}, bf16[2,3,6,1664]{3,2,1,0:T(8,128)(2,1)S(1)}, u32[]{:S(2)}, u32[]{:S(2)}) collective-permute-start(bf16[2,3,6,1664]{3,2,1,0:T(8,128)(2,1)S(1)} %constant_dynamic-slice_fusion.1), channel_id=1, source_target_pairs={{0,4},{1,5},{2,6},{3,7},{4,0},{5,1},{6,2},{7,3},{8,12},{9,13},{10,... | collective-permute-start | bytes 359432 | tf_op jit(solution)/shard_map/ppermute | solution.py:33
  15.7 8.4 %collective-permute-start.3 = (bf16[2,3,5,1664]{3,2,1,0:T(8,128)(2,1)S(1)}, bf16[2,3,5,1664]{3,2,1,0:T(8,128)(2,1)S(1)}, u32[]{:S(2)}, u32[]{:S(2)}) collective-permute-start(bf16[2,3,5,1664]{3,2,1,0:T(8,128)(2,1)S(1)} %constant_dynamic-slice_fusion), channel_id=1, source_target_pairs={{0,8},{1,9},{2,10},{3,11},{4,12},{5,13},{6,14},{7,15},{8,0},{9,1},... | collective-permute-start | bytes 299528 | tf_op jit(solution)/shard_map/ppermute | solution.py:33
  41.1 7.7 %collective-permute-start.4 = (bf16[2,3,2,624]{3,2,1,0:T(2,128)(2,1)S(1)}, bf16[2,3,2,624]{3,2,1,0:T(2,128)(2,1)S(1)}, u32[]{:S(2)}, u32[]{:S(2)}) collective-permute-start(bf16[2,3,2,624]{3,2,1,0:T(2,128)(2,1)S(1)} %reshape.20), channel_id=1, source_target_pairs={{0,0},{1,8},{2,4},{3,12},{4,2},{5,10},{6,6},{7,14},{8,1},{9,9},{10... | collective-permute-start | bytes 44936 | tf_op jit(solution)/shard_map/ppermute | solution.py:149

commit v14 on v13

--- a/solution.py
+++ b/solution.py
@@ -60,10 +60,8 @@
         pieces = []
         for a in range(3):
             for b in range(3):
-                src = xt_ref[j + b, :, a * LANE : a * LANE + span].astype(jnp.float32)
                 for e in range(3):
-                    shifted = src if e == 1 else pltpu.roll(src, (1 - e) % span, 1)
-                    pieces.append(shifted.astype(jnp.bfloat16))
+                    pieces.append(xt_ref[j + b, e, :, a * LANE : a * LANE + span])
         patches = jnp.concatenate(pieces, axis=0)
         first_t = jnp.dot(w_in, patches, preferred_element_type=jnp.float32)
         first = jnp.where(valid, first_t.T, 0.0)
@@ -89,7 +87,7 @@
 
 def decode(row_ok, xt, conv_in, conv_mid, to_pixels, columns):
     rows_in = xt.shape[0] - 2
-    span = xt.shape[2] - 2 * LANE
+    span = xt.shape[3] - 2 * LANE
     channels = conv_mid.shape[1]
     w_mid = conv_mid.reshape(9, 3 * channels, channels)
     w_in_t = conv_in.T
@@ -139,6 +137,7 @@
     xt = x.reshape(steps, rows_dev + 2 * HALO, columns, ZC).transpose(1, 3, 0, 2)
     xt = jnp.pad(xt, ((0, 0), (0, 0), (2, 0), (0, LANE - columns)))
     xt = xt.reshape(rows_dev + 2 * HALO, ZC, (steps + 2) * LANE)
+    xt = jnp.stack([jnp.roll(xt, 1 - e, axis=2) for e in range(3)], axis=1)
     row_of = slot * rows_dev - 1 + jnp.arange(rows_in)
     row_ok = ((row_of >= 0) & (row_of < height)).astype(jnp.float32)
 

time: 49.7 us -> 49.2 us (0.990)
  Pallas kernels: 14.1 us -> 13.4 us
    pallas_call x1, Pallas kernels: 14.1 us -> 13.4 us  [decode(): pl.pallas_call(functools.partial(decode_kernel, columns), out_shape=jax.S...]
    unnamed x3 -> x4, local copies, waits for them, and re-layouts: 2.59 us -> 2.96 us
where the time goes in v14:
time: 49.2 us; the launch traced here: 48.9 us
  waiting for transfers between devices  22.9 us (47%)
  Pallas kernels  13.4 us (27%)
  local copies, waits for them, and re-layouts  5.72 us (12%)
  starting transfers between devices  4.46 us (9%)
  other arithmetic  2.29 us (5%)
    ppermute x4, waiting for transfers between devices, gather_rows(): x = own + lax.ppermute(send, 'dev', pairs)  17.1 us
    pallas_call x1, Pallas kernels, decode(): pl.pallas_call(functools.partial(decode_kernel, columns), out_shape=jax.S...  13.4 us
    ppermute x1, waiting for transfers between devices, local(): lax.ppermute(pixels, 'dev', [(i, reverse_bits(i, bits)) for i in range(n)])  5.82 us
    unnamed x4, local copies, waits for them, and re-layouts  2.96 us
    ppermute x4, starting transfers between devices, gather_rows(): x = own + lax.ppermute(send, 'dev', pairs)  2.54 us
    ppermute x1, starting transfers between devices, local(): lax.ppermute(pixels, 'dev', [(i, reverse_bits(i, bits)) for i in range(n)])  1.92 us
    select_n x1, other arithmetic, local(): jnp.where(keep[:, None, None, None], latents[0], jnp.zeros_like(latents[0]))  1.07 us
  transfers between devices with their start and end apart: 5, of which 5 were waited for; matrix products, arithmetic and copies ran while one was open for 4% of the time, Pallas kernels for 0%

profile of v14, /device:TPU:24, one launch (start us, length us, event | category | flops | bytes accessed | tf_op | source)
XLA Modules:
  0.0 48.9 jit_solution(2727162755616606578)
XLA Ops:
  0.0 0.7 %broadcast_compare_fusion = pred[2]{0:T(512)(128)(4,1)S(1)} fusion(s32[2]{0:T(128)} %param.6, s32[]{:T(128)S(6)} %axis_index.12), kind=kLoop, calls=%fused_computation.15 | loop fusion | flops 2 | bytes 14 | tf_op jit(solution)/shard_map/eq | solution.py:131
  0.7 1.1 %bitcast_select_fusion = bf16[2,3,16,1664]{3,2,1,0:T(8,128)(2,1)S(1)} fusion(bf16[1,2,3,16,1664]{4,3,2,1,0:T(8,128)(2,1)} %param.5, pred[2]{0:T(512)(128)(4,1)S(1)} %broadcast_compare_fusion), kind=kLoop, calls=%fused_computation.4 | loop fusion | flops 159744 | bytes 638978 | tf_op jit(solution)/shard_map/jit(_where)/select_n | solution.py:132
  1.7 0.1 pad_dynamic-slice_fusion
  2.0 1.6 %collective-permute-done = bf16[2,3,12,1664]{3,2,1,0:T(8,128)(2,1)S(1)} collective-permute-done((bf16[2,3,12,1664]{3,2,1,0:T(8,128)(2,1)S(1)}, bf16[2,3,12,1664]{3,2,1,0:T(8,128)(2,1)S(1)}, u32[]{:S(2)}, u32[]{:S(2)}) %collective-permute-start) | collective-permute-done | bytes 239648 | tf_op jit(solution)/shard_map/ppermute | solution.py:33
  3.6 0.2 fusion
  3.8 1.6 %collective-permute-start.1 = (bf16[2,3,8,1664]{3,2,1,0:T(8,128)(2,1)S(1)}, bf16[2,3,8,1664]{3,2,1,0:T(8,128)(2,1)S(1)}, u32[]{:S(2)}, u32[]{:S(2)}) collective-permute-start(bf16[2,3,8,1664]{3,2,1,0:T(8,128)(2,1)S(1)} %constant_dynamic-slice_fusion.2), channel_id=1, source_target_pairs={{0,2},{1,3},{2,0},{3,1},{4,6},{5,7},{6,4},{7,5},{8,10},{9,11},{10,... | collective-permute-start | bytes 479240 | tf_op jit(solution)/shard_map/ppermute | solution.py:33
  5.4 4.7 %collective-permute-done.1 = bf16[2,3,8,1664]{3,2,1,0:T(8,128)(2,1)S(1)} collective-permute-done((bf16[2,3,8,1664]{3,2,1,0:T(8,128)(2,1)S(1)}, bf16[2,3,8,1664]{3,2,1,0:T(8,128)(2,1)S(1)}, u32[]{:S(2)}, u32[]{:S(2)}) %collective-permute-start.1) | collective-permute-done | bytes 159776 | tf_op jit(solution)/shard_map/ppermute | solution.py:33
  10.2 0.5 %collective-permute-start.2 = (bf16[2,3,6,1664]{3,2,1,0:T(8,128)(2,1)S(1)}, bf16[2,3,6,1664]{3,2,1,0:T(8,128)(2,1)S(1)}, u32[]{:S(2)}, u32[]{:S(2)}) collective-permute-start(bf16[2,3,6,1664]{3,2,1,0:T(8,128)(2,1)S(1)} %constant_dynamic-slice_fusion.1), channel_id=1, source_target_pairs={{0,4},{1,5},{2,6},{3,7},{4,0},{5,1},{6,2},{7,3},{8,12},{9,13},{10,... | collective-permute-start | bytes 359432 | tf_op jit(solution)/shard_map/ppermute | solution.py:33
  10.7 1.1 %copy.15 = bf16[432,384]{0,1:T(8,128)(2,1)S(1)} copy(bf16[432,384]{1,0:T(8,128)(2,1)} %param.7) | data formatting | bytes 663552 | tf_op args[2]
  11.8 0.8 %copy.16 = bf16[384,12]{1,0:T(8,128)(2,1)S(1)} copy(bf16[384,12]{0,1:T(8,128)(2,1)} %param.9) | data formatting | bytes 18432 | tf_op args[4]
  12.7 2.8 %collective-permute-done.2 = bf16[2,3,6,1664]{3,2,1,0:T(8,128)(2,1)S(1)} collective-permute-done((bf16[2,3,6,1664]{3,2,1,0:T(8,128)(2,1)S(1)}, bf16[2,3,6,1664]{3,2,1,0:T(8,128)(2,1)S(1)}, u32[]{:S(2)}, u32[]{:S(2)}) %collective-permute-start.2) | collective-permute-done | bytes 119840 | tf_op jit(solution)/shard_map/ppermute | solution.py:33
  15.7 0.4 collective-permute-start.3
  16.1 8.0 %collective-permute-done.3 = bf16[2,3,5,1664]{3,2,1,0:T(8,128)(2,1)S(1)} collective-permute-done((bf16[2,3,5,1664]{3,2,1,0:T(8,128)(2,1)S(1)}, bf16[2,3,5,1664]{3,2,1,0:T(8,128)(2,1)S(1)}, u32[]{:S(2)}, u32[]{:S(2)}) %collective-permute-start.3) | collective-permute-done | bytes 99872 | tf_op jit(solution)/shard_map/ppermute | solution.py:33
  24.2 0.6 %reshape.17 = bf16[6,5,104,16]{3,2,0,1:T(8,128)(2,1)S(1)} reshape(bf16[2,3,5,1664]{3,1,0,2:T(4,128)(2,1)S(1)} %copy.11) | data formatting | bytes 199680 | tf_op jit(solution)/shard_map/reshape | solution.py:137
  24.8 0.4 copy.19
  25.3 0.1 fusion.2
  25.6 0.1 maximum_bitcast_fusion
  25.8 13.4 %shard_map.55 = bf16[1,768,128]{2,1,0:T(8,128)(2,1)S(1)} custom-call(f32[3]{0:T(128)S(1)} %and_convert_fusion.row_ok_ref, bf16[5,3,16,1024]{3,2,1,0:T(8,128)(2,1)S(1)} %pad_maximum_fusion.xt_ref, bf16[384,432]{1,0:T(8,128)(2,1)S(1)} %bitcast.24, bf16[9,1152,384]{2,1,0:T(8,128)(2,1)} %bitcast.26, bf16[384,128]{1,0:T(8,128)(2,1)S(1)} %pad.14.w_pix_ref), custom_call_target="tpu_custom_call" | custom-call | tf_op jit(solution)/shard_map/pallas_call | solution.py:97
  39.2 0.1 copy.17
  39.4 0.5 %copy.18 = bf16[2,3,1,2,104,2,3]{6,5,4,3,1,0,2:T(2,128)(2,1)S(1)} copy(bf16[2,3,1,2,104,2,3]{4,1,0,6,5,3,2:T(4,128)(2,1)S(1)} %slice_bitcast_fusion) | data formatting | bytes 29952 | tf_op jit(solution)/shard_map/transpose | solution.py:146
  39.9 0.7 %reshape.21 = bf16[2,3,2,624]{3,2,1,0:T(2,128)(2,1)S(1)} reshape(bf16[2,3,1,2,104,2,3]{6,5,4,3,1,0,2:T(2,128)(2,1)S(1)} %copy.18) | data formatting | bytes 29952 | tf_op jit(solution)/shard_map/reshape | solution.py:147
  40.6 1.9 %collective-permute-start.4 = (bf16[2,3,2,624]{3,2,1,0:T(2,128)(2,1)S(1)}, bf16[2,3,2,624]{3,2,1,0:T(2,128)(2,1)S(1)}, u32[]{:S(2)}, u32[]{:S(2)}) collective-permute-start(bf16[2,3,2,624]{3,2,1,0:T(2,128)(2,1)S(1)} %reshape.21), channel_id=1, source_target_pairs={{0,0},{1,8},{2,4},{3,12},{4,2},{5,10},{6,6},{7,14},{8,1},{9,9},{10... | collective-permute-start | bytes 44936 | tf_op jit(solution)/shard_map/ppermute | solution.py:148
  42.5 5.8 %collective-permute-done.4 = bf16[2,3,2,624]{3,2,1,0:T(2,128)(2,1)S(1)} collective-permute-done((bf16[2,3,2,624]{3,2,1,0:T(2,128)(2,1)S(1)}, bf16[2,3,2,624]{3,2,1,0:T(2,128)(2,1)S(1)}, u32[]{:S(2)}, u32[]{:S(2)}) %collective-permute-start.4) | collective-permute-done | bytes 15008 | tf_op jit(solution)/shard_map/ppermute | solution.py:148
  48.3 0.6 %copy.21 = bf16[2,3,2,624]{3,2,1,0:T(2,128)(2,1)} copy(bf16[2,3,2,624]{3,2,1,0:T(2,128)(2,1)S(1)} %collective-permute-done.4) | data formatting | bytes 29952
  (17 shorter events, 0.9 us)
Async XLA Ops:
  1.9 1.7 %collective-permute-start = (bf16[2,3,12,1664]{3,2,1,0:T(8,128)(2,1)S(1)}, bf16[2,3,12,1664]{3,2,1,0:T(8,128)(2,1)S(1)}, u32[]{:S(2)}, u32[]{:S(2)}) collective-permute-start(bf16[2,3,12,1664]{3,2,1,0:T(8,128)(2,1)S(1)} %pad_dynamic-slice_fusion), channel_id=1, source_target_pairs={{0,1},{1,0},{2,3},{3,2},{4,5},{5,4},{6,7},{7,6},{8,9},{9,8},{10,11... | collective-permute-start | bytes 718856 | tf_op jit(solution)/shard_map/ppermute | solution.py:33
  3.8 6.2 %collective-permute-start.1 = (bf16[2,3,8,1664]{3,2,1,0:T(8,128)(2,1)S(1)}, bf16[2,3,8,1664]{3,2,1,0:T(8,128)(2,1)S(1)}, u32[]{:S(2)}, u32[]{:S(2)}) collective-permute-start(bf16[2,3,8,1664]{3,2,1,0:T(8,128)(2,1)S(1)} %constant_dynamic-slice_fusion.2), channel_id=1, source_target_pairs={{0,2},{1,3},{2,0},{3,1},{4,6},{5,7},{6,4},{7,5},{8,10},{9,11},{10,... | collective-permute-start | bytes 479240 | tf_op jit(solution)/shard_map/ppermute | solution.py:33
  10.2 5.4 %collective-permute-start.2 = (bf16[2,3,6,1664]{3,2,1,0:T(8,128)(2,1)S(1)}, bf16[2,3,6,1664]{3,2,1,0:T(8,128)(2,1)S(1)}, u32[]{:S(2)}, u32[]{:S(2)}) collective-permute-start(bf16[2,3,6,1664]{3,2,1,0:T(8,128)(2,1)S(1)} %constant_dynamic-slice_fusion.1), channel_id=1, source_target_pairs={{0,4},{1,5},{2,6},{3,7},{4,0},{5,1},{6,2},{7,3},{8,12},{9,13},{10,... | collective-permute-start | bytes 359432 | tf_op jit(solution)/shard_map/ppermute | solution.py:33
  15.7 8.4 %collective-permute-start.3 = (bf16[2,3,5,1664]{3,2,1,0:T(8,128)(2,1)S(1)}, bf16[2,3,5,1664]{3,2,1,0:T(8,128)(2,1)S(1)}, u32[]{:S(2)}, u32[]{:S(2)}) collective-permute-start(bf16[2,3,5,1664]{3,2,1,0:T(8,128)(2,1)S(1)} %constant_dynamic-slice_fusion), channel_id=1, source_target_pairs={{0,8},{1,9},{2,10},{3,11},{4,12},{5,13},{6,14},{7,15},{8,0},{9,1},... | collective-permute-start | bytes 299528 | tf_op jit(solution)/shard_map/ppermute | solution.py:33
  40.6 7.7 %collective-permute-start.4 = (bf16[2,3,2,624]{3,2,1,0:T(2,128)(2,1)S(1)}, bf16[2,3,2,624]{3,2,1,0:T(2,128)(2,1)S(1)}, u32[]{:S(2)}, u32[]{:S(2)}) collective-permute-start(bf16[2,3,2,624]{3,2,1,0:T(2,128)(2,1)S(1)} %reshape.21), channel_id=1, source_target_pairs={{0,0},{1,8},{2,4},{3,12},{4,2},{5,10},{6,6},{7,14},{8,1},{9,9},{10... | collective-permute-start | bytes 44936 | tf_op jit(solution)/shard_map/ppermute | solution.py:148

commit v15 on v14

--- a/solution.py
+++ b/solution.py
@@ -56,15 +56,17 @@
     column = lax.broadcasted_iota(jnp.int32, (span, 1), 0) % LANE
     valid = column < columns
     w_in = w_in_ref[...]
+    columns_all = []
     for j in range(rows_in):
         pieces = []
         for a in range(3):
             for b in range(3):
                 for e in range(3):
                     pieces.append(xt_ref[j + b, e, :, a * LANE : a * LANE + span])
-        patches = jnp.concatenate(pieces, axis=0)
-        first_t = jnp.dot(w_in, patches, preferred_element_type=jnp.float32)
-        first = jnp.where(valid, first_t.T, 0.0)
+        columns_all.append(jnp.concatenate(pieces, axis=0))
+    first_all = jnp.dot(w_in, jnp.concatenate(columns_all, axis=1), preferred_element_type=jnp.float32)
+    for j in range(rows_in):
+        first = jnp.where(valid, first_all[:, j * span : (j + 1) * span].T, 0.0)
         if 1 <= j <= rows_out:
             center_ref[j - 1] = first
         scaled = first * lax.rsqrt(jnp.mean(first * first, axis=-1, keepdims=True) + epsilon)

time: 49.2 us -> 49.3 us (level)
  no operation moved by 1% of the time
where the time goes in v15:
time: 49.3 us; the launch traced here: 49 us
  waiting for transfers between devices  22.9 us (46%)
  Pallas kernels  13.4 us (27%)
  local copies, waits for them, and re-layouts  5.72 us (12%)
  starting transfers between devices  4.46 us (9%)
  other arithmetic  2.29 us (5%)
    ppermute x4, waiting for transfers between devices, gather_rows(): x = own + lax.ppermute(send, 'dev', pairs)  17.1 us
    pallas_call x1, Pallas kernels, decode(): pl.pallas_call(functools.partial(decode_kernel, columns), out_shape=jax.S...  13.4 us
    ppermute x1, waiting for transfers between devices, local(): lax.ppermute(pixels, 'dev', [(i, reverse_bits(i, bits)) for i in range(n)])  5.82 us
    unnamed x4, local copies, waits for them, and re-layouts  2.96 us
    ppermute x4, starting transfers between devices, gather_rows(): x = own + lax.ppermute(send, 'dev', pairs)  2.54 us
    ppermute x1, starting transfers between devices, local(): lax.ppermute(pixels, 'dev', [(i, reverse_bits(i, bits)) for i in range(n)])  1.92 us
    select_n x1, other arithmetic, local(): jnp.where(keep[:, None, None, None], latents[0], jnp.zeros_like(latents[0]))  1.07 us
  transfers between devices with their start and end apart: 5, of which 5 were waited for; matrix products, arithmetic and copies ran while one was open for 4% of the time, Pallas kernels for 0%

profile of v15, /device:TPU:24, one launch (start us, length us, event | category | flops | bytes accessed | tf_op | source)
XLA Modules:
  0.0 49.0 jit_solution(2853361912436594751)
XLA Ops:
  0.0 0.7 %broadcast_compare_fusion = pred[2]{0:T(512)(128)(4,1)S(1)} fusion(s32[2]{0:T(128)} %param.6, s32[]{:T(128)S(6)} %axis_index.12), kind=kLoop, calls=%fused_computation.15 | loop fusion | flops 2 | bytes 14 | tf_op jit(solution)/shard_map/eq | solution.py:133
  0.7 1.1 %bitcast_select_fusion = bf16[2,3,16,1664]{3,2,1,0:T(8,128)(2,1)S(1)} fusion(bf16[1,2,3,16,1664]{4,3,2,1,0:T(8,128)(2,1)} %param.5, pred[2]{0:T(512)(128)(4,1)S(1)} %broadcast_compare_fusion), kind=kLoop, calls=%fused_computation.4 | loop fusion | flops 159744 | bytes 638978 | tf_op jit(solution)/shard_map/jit(_where)/select_n | solution.py:134
  1.7 0.1 pad_dynamic-slice_fusion
  2.0 1.6 %collective-permute-done = bf16[2,3,12,1664]{3,2,1,0:T(8,128)(2,1)S(1)} collective-permute-done((bf16[2,3,12,1664]{3,2,1,0:T(8,128)(2,1)S(1)}, bf16[2,3,12,1664]{3,2,1,0:T(8,128)(2,1)S(1)}, u32[]{:S(2)}, u32[]{:S(2)}) %collective-permute-start) | collective-permute-done | bytes 239648 | tf_op jit(solution)/shard_map/ppermute | solution.py:33
  3.6 0.2 fusion
  3.8 1.6 %collective-permute-start.1 = (bf16[2,3,8,1664]{3,2,1,0:T(8,128)(2,1)S(1)}, bf16[2,3,8,1664]{3,2,1,0:T(8,128)(2,1)S(1)}, u32[]{:S(2)}, u32[]{:S(2)}) collective-permute-start(bf16[2,3,8,1664]{3,2,1,0:T(8,128)(2,1)S(1)} %constant_dynamic-slice_fusion.2), channel_id=1, source_target_pairs={{0,2},{1,3},{2,0},{3,1},{4,6},{5,7},{6,4},{7,5},{8,10},{9,11},{10,... | collective-permute-start | bytes 479240 | tf_op jit(solution)/shard_map/ppermute | solution.py:33
  5.4 4.7 %collective-permute-done.1 = bf16[2,3,8,1664]{3,2,1,0:T(8,128)(2,1)S(1)} collective-permute-done((bf16[2,3,8,1664]{3,2,1,0:T(8,128)(2,1)S(1)}, bf16[2,3,8,1664]{3,2,1,0:T(8,128)(2,1)S(1)}, u32[]{:S(2)}, u32[]{:S(2)}) %collective-permute-start.1) | collective-permute-done | bytes 159776 | tf_op jit(solution)/shard_map/ppermute | solution.py:33
  10.2 0.5 %collective-permute-start.2 = (bf16[2,3,6,1664]{3,2,1,0:T(8,128)(2,1)S(1)}, bf16[2,3,6,1664]{3,2,1,0:T(8,128)(2,1)S(1)}, u32[]{:S(2)}, u32[]{:S(2)}) collective-permute-start(bf16[2,3,6,1664]{3,2,1,0:T(8,128)(2,1)S(1)} %constant_dynamic-slice_fusion.1), channel_id=1, source_target_pairs={{0,4},{1,5},{2,6},{3,7},{4,0},{5,1},{6,2},{7,3},{8,12},{9,13},{10,... | collective-permute-start | bytes 359432 | tf_op jit(solution)/shard_map/ppermute | solution.py:33
  10.7 1.1 %copy.15 = bf16[432,384]{0,1:T(8,128)(2,1)S(1)} copy(bf16[432,384]{1,0:T(8,128)(2,1)} %param.7) | data formatting | bytes 663552 | tf_op args[2]
  11.8 0.8 %copy.16 = bf16[384,12]{1,0:T(8,128)(2,1)S(1)} copy(bf16[384,12]{0,1:T(8,128)(2,1)} %param.9) | data formatting | bytes 18432 | tf_op args[4]
  12.7 2.8 %collective-permute-done.2 = bf16[2,3,6,1664]{3,2,1,0:T(8,128)(2,1)S(1)} collective-permute-done((bf16[2,3,6,1664]{3,2,1,0:T(8,128)(2,1)S(1)}, bf16[2,3,6,1664]{3,2,1,0:T(8,128)(2,1)S(1)}, u32[]{:S(2)}, u32[]{:S(2)}) %collective-permute-start.2) | collective-permute-done | bytes 119840 | tf_op jit(solution)/shard_map/ppermute | solution.py:33
  15.7 0.4 collective-permute-start.3
  16.1 8.0 %collective-permute-done.3 = bf16[2,3,5,1664]{3,2,1,0:T(8,128)(2,1)S(1)} collective-permute-done((bf16[2,3,5,1664]{3,2,1,0:T(8,128)(2,1)S(1)}, bf16[2,3,5,1664]{3,2,1,0:T(8,128)(2,1)S(1)}, u32[]{:S(2)}, u32[]{:S(2)}) %collective-permute-start.3) | collective-permute-done | bytes 99872 | tf_op jit(solution)/shard_map/ppermute | solution.py:33
  24.2 0.6 %reshape.17 = bf16[6,5,104,16]{3,2,0,1:T(8,128)(2,1)S(1)} reshape(bf16[2,3,5,1664]{3,1,0,2:T(4,128)(2,1)S(1)} %copy.11) | data formatting | bytes 199680 | tf_op jit(solution)/shard_map/reshape | solution.py:139
  24.8 0.4 copy.19
  25.3 0.1 fusion.2
  25.6 0.1 maximum_bitcast_fusion
  25.8 13.4 %shard_map.55 = bf16[1,768,128]{2,1,0:T(8,128)(2,1)S(1)} custom-call(f32[3]{0:T(128)S(1)} %and_convert_fusion.row_ok_ref, bf16[5,3,16,1024]{3,2,1,0:T(8,128)(2,1)S(1)} %pad_maximum_fusion.xt_ref, bf16[384,432]{1,0:T(8,128)(2,1)S(1)} %bitcast.24, bf16[9,1152,384]{2,1,0:T(8,128)(2,1)} %bitcast.26, bf16[384,128]{1,0:T(8,128)(2,1)S(1)} %pad.14.w_pix_ref), custom_call_target="tpu_custom_call" | custom-call | tf_op jit(solution)/shard_map/pallas_call | solution.py:99
  39.3 0.1 copy.17
  39.4 0.5 %copy.18 = bf16[2,3,1,2,104,2,3]{6,5,4,3,1,0,2:T(2,128)(2,1)S(1)} copy(bf16[2,3,1,2,104,2,3]{4,1,0,6,5,3,2:T(4,128)(2,1)S(1)} %slice_bitcast_fusion) | data formatting | bytes 29952 | tf_op jit(solution)/shard_map/transpose | solution.py:148
  40.0 0.7 %reshape.21 = bf16[2,3,2,624]{3,2,1,0:T(2,128)(2,1)S(1)} reshape(bf16[2,3,1,2,104,2,3]{6,5,4,3,1,0,2:T(2,128)(2,1)S(1)} %copy.18) | data formatting | bytes 29952 | tf_op jit(solution)/shard_map/reshape | solution.py:149
  40.7 1.9 %collective-permute-start.4 = (bf16[2,3,2,624]{3,2,1,0:T(2,128)(2,1)S(1)}, bf16[2,3,2,624]{3,2,1,0:T(2,128)(2,1)S(1)}, u32[]{:S(2)}, u32[]{:S(2)}) collective-permute-start(bf16[2,3,2,624]{3,2,1,0:T(2,128)(2,1)S(1)} %reshape.21), channel_id=1, source_target_pairs={{0,0},{1,8},{2,4},{3,12},{4,2},{5,10},{6,6},{7,14},{8,1},{9,9},{10... | collective-permute-start | bytes 44936 | tf_op jit(solution)/shard_map/ppermute | solution.py:150
  42.6 5.8 %collective-permute-done.4 = bf16[2,3,2,624]{3,2,1,0:T(2,128)(2,1)S(1)} collective-permute-done((bf16[2,3,2,624]{3,2,1,0:T(2,128)(2,1)S(1)}, bf16[2,3,2,624]{3,2,1,0:T(2,128)(2,1)S(1)}, u32[]{:S(2)}, u32[]{:S(2)}) %collective-permute-start.4) | collective-permute-done | bytes 15008 | tf_op jit(solution)/shard_map/ppermute | solution.py:150
  48.4 0.6 %copy.21 = bf16[2,3,2,624]{3,2,1,0:T(2,128)(2,1)} copy(bf16[2,3,2,624]{3,2,1,0:T(2,128)(2,1)S(1)} %collective-permute-done.4) | data formatting | bytes 29952
  (17 shorter events, 0.9 us)
Async XLA Ops:
  1.9 1.7 %collective-permute-start = (bf16[2,3,12,1664]{3,2,1,0:T(8,128)(2,1)S(1)}, bf16[2,3,12,1664]{3,2,1,0:T(8,128)(2,1)S(1)}, u32[]{:S(2)}, u32[]{:S(2)}) collective-permute-start(bf16[2,3,12,1664]{3,2,1,0:T(8,128)(2,1)S(1)} %pad_dynamic-slice_fusion), channel_id=1, source_target_pairs={{0,1},{1,0},{2,3},{3,2},{4,5},{5,4},{6,7},{7,6},{8,9},{9,8},{10,11... | collective-permute-start | bytes 718856 | tf_op jit(solution)/shard_map/ppermute | solution.py:33
  3.8 6.2 %collective-permute-start.1 = (bf16[2,3,8,1664]{3,2,1,0:T(8,128)(2,1)S(1)}, bf16[2,3,8,1664]{3,2,1,0:T(8,128)(2,1)S(1)}, u32[]{:S(2)}, u32[]{:S(2)}) collective-permute-start(bf16[2,3,8,1664]{3,2,1,0:T(8,128)(2,1)S(1)} %constant_dynamic-slice_fusion.2), channel_id=1, source_target_pairs={{0,2},{1,3},{2,0},{3,1},{4,6},{5,7},{6,4},{7,5},{8,10},{9,11},{10,... | collective-permute-start | bytes 479240 | tf_op jit(solution)/shard_map/ppermute | solution.py:33
  10.2 5.4 %collective-permute-start.2 = (bf16[2,3,6,1664]{3,2,1,0:T(8,128)(2,1)S(1)}, bf16[2,3,6,1664]{3,2,1,0:T(8,128)(2,1)S(1)}, u32[]{:S(2)}, u32[]{:S(2)}) collective-permute-start(bf16[2,3,6,1664]{3,2,1,0:T(8,128)(2,1)S(1)} %constant_dynamic-slice_fusion.1), channel_id=1, source_target_pairs={{0,4},{1,5},{2,6},{3,7},{4,0},{5,1},{6,2},{7,3},{8,12},{9,13},{10,... | collective-permute-start | bytes 359432 | tf_op jit(solution)/shard_map/ppermute | solution.py:33
  15.7 8.4 %collective-permute-start.3 = (bf16[2,3,5,1664]{3,2,1,0:T(8,128)(2,1)S(1)}, bf16[2,3,5,1664]{3,2,1,0:T(8,128)(2,1)S(1)}, u32[]{:S(2)}, u32[]{:S(2)}) collective-permute-start(bf16[2,3,5,1664]{3,2,1,0:T(8,128)(2,1)S(1)} %constant_dynamic-slice_fusion), channel_id=1, source_target_pairs={{0,8},{1,9},{2,10},{3,11},{4,12},{5,13},{6,14},{7,15},{8,0},{9,1},... | collective-permute-start | bytes 299528 | tf_op jit(solution)/shard_map/ppermute | solution.py:33
  40.7 7.7 %collective-permute-start.4 = (bf16[2,3,2,624]{3,2,1,0:T(2,128)(2,1)S(1)}, bf16[2,3,2,624]{3,2,1,0:T(2,128)(2,1)S(1)}, u32[]{:S(2)}, u32[]{:S(2)}) collective-permute-start(bf16[2,3,2,624]{3,2,1,0:T(2,128)(2,1)S(1)} %reshape.21), channel_id=1, source_target_pairs={{0,0},{1,8},{2,4},{3,12},{4,2},{5,10},{6,6},{7,14},{8,1},{9,9},{10... | collective-permute-start | bytes 44936 | tf_op jit(solution)/shard_map/ppermute | solution.py:150

commit v16 on v15

--- a/solution.py
+++ b/solution.py
@@ -130,8 +130,8 @@
     steps = groups * frames
     assert columns < LANE
 
-    keep = owners == position
-    x = jnp.where(keep[:, None, None, None], latents[0], jnp.zeros_like(latents[0]))
+    zero = jnp.zeros_like(latents[0, 0])
+    x = jnp.stack([jnp.where(owners[g] == position, latents[0, g], zero) for g in range(groups)])
     x = jnp.pad(x, ((0, 0), (0, 0), (HALO, HALO), (0, 0)))
     x = gather_rows(x, n, rows_dev, slot, axis=2)
 

time: 49.3 us -> 51.3 us (1.041)
  local copies, waits for them, and re-layouts: 5.72 us -> 7.05 us
  between operations: 0.2 us -> 1.49 us
  other arithmetic: 2.29 us -> 1.7 us
    slice x0 -> x1, local copies, waits for them, and re-layouts: none -> 1.36 us  [local(): owners[g] == position]
    eq x1 -> x0, other arithmetic: 0.66 us -> none  [local(): keep = owners == position]
where the time goes in v16:
time: 51.3 us; the launch traced here: 51 us
  waiting for transfers between devices  22.9 us (45%)
  Pallas kernels  13.4 us (26%)
  local copies, waits for them, and re-layouts  7.05 us (14%)
  starting transfers between devices  4.46 us (9%)
  other arithmetic  1.7 us (3%)
  between operations  1.49 us (3%)
    ppermute x4, waiting for transfers between devices, gather_rows(): x = own + lax.ppermute(send, 'dev', pairs)  17.1 us
    pallas_call x1, Pallas kernels, decode(): pl.pallas_call(functools.partial(decode_kernel, columns), out_shape=jax.S...  13.4 us
    ppermute x1, waiting for transfers between devices, local(): lax.ppermute(pixels, 'dev', [(i, reverse_bits(i, bits)) for i in range(n)])  5.82 us
    unnamed x4, local copies, waits for them, and re-layouts  2.96 us
    ppermute x4, starting transfers between devices, gather_rows(): x = own + lax.ppermute(send, 'dev', pairs)  2.54 us
    ppermute x1, starting transfers between devices, local(): lax.ppermute(pixels, 'dev', [(i, reverse_bits(i, bits)) for i in range(n)])  1.92 us
    slice x1, local copies, waits for them, and re-layouts, local(): owners[g] == position  1.36 us
  transfers between devices with their start and end apart: 5, of which 5 were waited for; matrix products, arithmetic and copies ran while one was open for 4% of the time, Pallas kernels for 0%

profile of v16, /device:TPU:24, one launch (start us, length us, event | category | flops | bytes accessed | tf_op | source)
XLA Modules:
  0.0 51.0 jit_solution(12058596364889701388)
XLA Ops:
  0.0 1.4 %fusion.6 = (s32[1]{0:T(128)}, s32[1]{0:T(128)}) fusion(s32[2]{0:T(128)} %param.6), kind=kLoop, calls=%fused_computation.23 | loop fusion | bytes 16 | tf_op jit(solution)/shard_map/slice | solution.py:134
  2.6 1.0 %select_bitcast_fusion.1 = (bf16[1,3,16,1664]{3,2,1,0:T(8,128)(2,1)S(1)}, bf16[1,3,16,1664]{3,2,1,0:T(8,128)(2,1)S(1)}) fusion(bf16[1,2,3,16,1664]{4,3,2,1,0:T(8,128)(2,1)} %param.5, pred[]{:T(512)S(6)} %eq.6, pred[]{:T(512)S(6)} %eq.7), kind=kLoop, calls=%fused_computation.14 | loop fusion | flops 159744 | bytes 638978 | tf_op jit(solution)/shard_map/jit(_where)/select_n | solution.py:134
  3.7 0.1 fusion.3
  4.0 1.6 %collective-permute-done = bf16[2,3,12,1664]{3,2,1,0:T(8,128)(2,1)S(1)} collective-permute-done((bf16[2,3,12,1664]{3,2,1,0:T(8,128)(2,1)S(1)}, bf16[2,3,12,1664]{3,2,1,0:T(8,128)(2,1)S(1)}, u32[]{:S(2)}, u32[]{:S(2)}) %collective-permute-start) | collective-permute-done | bytes 239648 | tf_op jit(solution)/shard_map/ppermute | solution.py:33
  5.6 0.1 dynamic-slice_add_fusion
  5.8 1.6 %collective-permute-start.1 = (bf16[2,3,8,1664]{3,2,1,0:T(8,128)(2,1)S(1)}, bf16[2,3,8,1664]{3,2,1,0:T(8,128)(2,1)S(1)}, u32[]{:S(2)}, u32[]{:S(2)}) collective-permute-start(bf16[2,3,8,1664]{3,2,1,0:T(8,128)(2,1)S(1)} %constant_dynamic-slice_fusion.2), channel_id=1, source_target_pairs={{0,2},{1,3},{2,0},{3,1},{4,6},{5,7},{6,4},{7,5},{8,10},{9,11},{10,... | collective-permute-start | bytes 479240 | tf_op jit(solution)/shard_map/ppermute | solution.py:33
  7.4 4.7 %collective-permute-done.1 = bf16[2,3,8,1664]{3,2,1,0:T(8,128)(2,1)S(1)} collective-permute-done((bf16[2,3,8,1664]{3,2,1,0:T(8,128)(2,1)S(1)}, bf16[2,3,8,1664]{3,2,1,0:T(8,128)(2,1)S(1)}, u32[]{:S(2)}, u32[]{:S(2)}) %collective-permute-start.1) | collective-permute-done | bytes 159776 | tf_op jit(solution)/shard_map/ppermute | solution.py:33
  12.2 0.5 %collective-permute-start.2 = (bf16[2,3,6,1664]{3,2,1,0:T(8,128)(2,1)S(1)}, bf16[2,3,6,1664]{3,2,1,0:T(8,128)(2,1)S(1)}, u32[]{:S(2)}, u32[]{:S(2)}) collective-permute-start(bf16[2,3,6,1664]{3,2,1,0:T(8,128)(2,1)S(1)} %constant_dynamic-slice_fusion.1), channel_id=1, source_target_pairs={{0,4},{1,5},{2,6},{3,7},{4,0},{5,1},{6,2},{7,3},{8,12},{9,13},{10,... | collective-permute-start | bytes 359432 | tf_op jit(solution)/shard_map/ppermute | solution.py:33
  12.7 1.1 %copy.15 = bf16[432,384]{0,1:T(8,128)(2,1)S(1)} copy(bf16[432,384]{1,0:T(8,128)(2,1)} %param.7) | data formatting | bytes 663552 | tf_op args[2]
  13.8 0.8 %copy.16 = bf16[384,12]{1,0:T(8,128)(2,1)S(1)} copy(bf16[384,12]{0,1:T(8,128)(2,1)} %param.9) | data formatting | bytes 18432 | tf_op args[4]
  14.7 2.8 %collective-permute-done.2 = bf16[2,3,6,1664]{3,2,1,0:T(8,128)(2,1)S(1)} collective-permute-done((bf16[2,3,6,1664]{3,2,1,0:T(8,128)(2,1)S(1)}, bf16[2,3,6,1664]{3,2,1,0:T(8,128)(2,1)S(1)}, u32[]{:S(2)}, u32[]{:S(2)}) %collective-permute-start.2) | collective-permute-done | bytes 119840 | tf_op jit(solution)/shard_map/ppermute | solution.py:33
  17.7 0.4 collective-permute-start.3
  18.1 8.0 %collective-permute-done.3 = bf16[2,3,5,1664]{3,2,1,0:T(8,128)(2,1)S(1)} collective-permute-done((bf16[2,3,5,1664]{3,2,1,0:T(8,128)(2,1)S(1)}, bf16[2,3,5,1664]{3,2,1,0:T(8,128)(2,1)S(1)}, u32[]{:S(2)}, u32[]{:S(2)}) %collective-permute-start.3) | collective-permute-done | bytes 99872 | tf_op jit(solution)/shard_map/ppermute | solution.py:33
  26.2 0.6 %reshape.42 = bf16[6,5,104,16]{3,2,0,1:T(8,128)(2,1)S(1)} reshape(bf16[2,3,5,1664]{3,1,0,2:T(4,128)(2,1)S(1)} %copy.11) | data formatting | bytes 199680 | tf_op jit(solution)/shard_map/reshape | solution.py:139
  26.8 0.4 copy.19
  27.4 0.1 fusion.5
  27.6 0.1 maximum_bitcast_fusion
  27.8 13.4 %shard_map.55 = bf16[1,768,128]{2,1,0:T(8,128)(2,1)S(1)} custom-call(f32[3]{0:T(128)S(1)} %and_convert_fusion.row_ok_ref, bf16[5,3,16,1024]{3,2,1,0:T(8,128)(2,1)S(1)} %pad_maximum_fusion.xt_ref, bf16[384,432]{1,0:T(8,128)(2,1)S(1)} %bitcast.28, bf16[9,1152,384]{2,1,0:T(8,128)(2,1)} %bitcast.30, bf16[384,128]{1,0:T(8,128)(2,1)S(1)} %pad.14.w_pix_ref), custom_call_target="tpu_custom_call" | custom-call | tf_op jit(solution)/shard_map/pallas_call | solution.py:99
  41.3 0.1 copy.17
  41.4 0.5 %copy.18 = bf16[2,3,1,2,104,2,3]{6,5,4,3,1,0,2:T(2,128)(2,1)S(1)} copy(bf16[2,3,1,2,104,2,3]{4,1,0,6,5,3,2:T(4,128)(2,1)S(1)} %slice_bitcast_fusion) | data formatting | bytes 29952 | tf_op jit(solution)/shard_map/transpose | solution.py:148
  42.0 0.7 %reshape.46 = bf16[2,3,2,624]{3,2,1,0:T(2,128)(2,1)S(1)} reshape(bf16[2,3,1,2,104,2,3]{6,5,4,3,1,0,2:T(2,128)(2,1)S(1)} %copy.18) | data formatting | bytes 29952 | tf_op jit(solution)/shard_map/reshape | solution.py:149
  42.7 1.9 %collective-permute-start.4 = (bf16[2,3,2,624]{3,2,1,0:T(2,128)(2,1)S(1)}, bf16[2,3,2,624]{3,2,1,0:T(2,128)(2,1)S(1)}, u32[]{:S(2)}, u32[]{:S(2)}) collective-permute-start(bf16[2,3,2,624]{3,2,1,0:T(2,128)(2,1)S(1)} %reshape.46), channel_id=1, source_target_pairs={{0,0},{1,8},{2,4},{3,12},{4,2},{5,10},{6,6},{7,14},{8,1},{9,9},{10... | collective-permute-start | bytes 44936 | tf_op jit(solution)/shard_map/ppermute | solution.py:150
  44.6 5.8 %collective-permute-done.4 = bf16[2,3,2,624]{3,2,1,0:T(2,128)(2,1)S(1)} collective-permute-done((bf16[2,3,2,624]{3,2,1,0:T(2,128)(2,1)S(1)}, bf16[2,3,2,624]{3,2,1,0:T(2,128)(2,1)S(1)}, u32[]{:S(2)}, u32[]{:S(2)}) %collective-permute-start.4) | collective-permute-done | bytes 15008 | tf_op jit(solution)/shard_map/ppermute | solution.py:150
  50.4 0.6 %copy.21 = bf16[2,3,2,624]{3,2,1,0:T(2,128)(2,1)} copy(bf16[2,3,2,624]{3,2,1,0:T(2,128)(2,1)S(1)} %collective-permute-done.4) | data formatting | bytes 29952
  (18 shorter events, 1.0 us)
Async XLA Ops:
  3.9 1.7 %collective-permute-start = (bf16[2,3,12,1664]{3,2,1,0:T(8,128)(2,1)S(1)}, bf16[2,3,12,1664]{3,2,1,0:T(8,128)(2,1)S(1)}, u32[]{:S(2)}, u32[]{:S(2)}) collective-permute-start(bf16[2,3,12,1664]{3,2,1,0:T(8,128)(2,1)S(1)} %constant_dynamic-slice_fusion.3), channel_id=1, source_target_pairs={{0,1},{1,0},{2,3},{3,2},{4,5},{5,4},{6,7},{7,6},{8,9},{9,8},{10,11... | collective-permute-start | bytes 718856 | tf_op jit(solution)/shard_map/ppermute | solution.py:33
  5.8 6.2 %collective-permute-start.1 = (bf16[2,3,8,1664]{3,2,1,0:T(8,128)(2,1)S(1)}, bf16[2,3,8,1664]{3,2,1,0:T(8,128)(2,1)S(1)}, u32[]{:S(2)}, u32[]{:S(2)}) collective-permute-start(bf16[2,3,8,1664]{3,2,1,0:T(8,128)(2,1)S(1)} %constant_dynamic-slice_fusion.2), channel_id=1, source_target_pairs={{0,2},{1,3},{2,0},{3,1},{4,6},{5,7},{6,4},{7,5},{8,10},{9,11},{10,... | collective-permute-start | bytes 479240 | tf_op jit(solution)/shard_map/ppermute | solution.py:33
  12.2 5.4 %collective-permute-start.2 = (bf16[2,3,6,1664]{3,2,1,0:T(8,128)(2,1)S(1)}, bf16[2,3,6,1664]{3,2,1,0:T(8,128)(2,1)S(1)}, u32[]{:S(2)}, u32[]{:S(2)}) collective-permute-start(bf16[2,3,6,1664]{3,2,1,0:T(8,128)(2,1)S(1)} %constant_dynamic-slice_fusion.1), channel_id=1, source_target_pairs={{0,4},{1,5},{2,6},{3,7},{4,0},{5,1},{6,2},{7,3},{8,12},{9,13},{10,... | collective-permute-start | bytes 359432 | tf_op jit(solution)/shard_map/ppermute | solution.py:33
  17.7 8.4 %collective-permute-start.3 = (bf16[2,3,5,1664]{3,2,1,0:T(8,128)(2,1)S(1)}, bf16[2,3,5,1664]{3,2,1,0:T(8,128)(2,1)S(1)}, u32[]{:S(2)}, u32[]{:S(2)}) collective-permute-start(bf16[2,3,5,1664]{3,2,1,0:T(8,128)(2,1)S(1)} %constant_dynamic-slice_fusion), channel_id=1, source_target_pairs={{0,8},{1,9},{2,10},{3,11},{4,12},{5,13},{6,14},{7,15},{8,0},{9,1},... | collective-permute-start | bytes 299528 | tf_op jit(solution)/shard_map/ppermute | solution.py:33
  42.7 7.7 %collective-permute-start.4 = (bf16[2,3,2,624]{3,2,1,0:T(2,128)(2,1)S(1)}, bf16[2,3,2,624]{3,2,1,0:T(2,128)(2,1)S(1)}, u32[]{:S(2)}, u32[]{:S(2)}) collective-permute-start(bf16[2,3,2,624]{3,2,1,0:T(2,128)(2,1)S(1)} %reshape.46), channel_id=1, source_target_pairs={{0,0},{1,8},{2,4},{3,12},{4,2},{5,10},{6,6},{7,14},{8,1},{9,9},{10... | collective-permute-start | bytes 44936 | tf_op jit(solution)/shard_map/ppermute | solution.py:150

commit v17 on v14

--- a/solution.py
+++ b/solution.py
@@ -63,7 +63,7 @@
                 for e in range(3):
                     pieces.append(xt_ref[j + b, e, :, a * LANE : a * LANE + span])
         patches = jnp.concatenate(pieces, axis=0)
-        first_t = jnp.dot(w_in, patches, preferred_element_type=jnp.float32)
+        first_t = lax.dot_general(w_in, patches, (((0,), (0,)), ((), ())), preferred_element_type=jnp.float32)
         first = jnp.where(valid, first_t.T, 0.0)
         if 1 <= j <= rows_out:
             center_ref[j - 1] = first
@@ -90,7 +90,6 @@
     span = xt.shape[3] - 2 * LANE
     channels = conv_mid.shape[1]
     w_mid = conv_mid.reshape(9, 3 * channels, channels)
-    w_in_t = conv_in.T
     n_pix = to_pixels.shape[1]
     w_pix = jnp.pad(to_pixels, ((0, 0), (0, LANE - n_pix)))
     vmem = pltpu.MemorySpace.VMEM
@@ -112,7 +111,7 @@
             pltpu.SemaphoreType.DMA((3,)),
         ],
         compiler_params=pltpu.CompilerParams(vmem_limit_bytes=48 * 1024 * 1024),
-    )(row_ok, xt, w_in_t, w_mid, w_pix)
+    )(row_ok, xt, conv_in, w_mid, w_pix)
     return out[:, :, :n_pix]
 
 

time: 49.2 us -> 49.4 us (level)
  waiting for transfers between devices: 22.9 us -> 24.1 us
  local copies, waits for them, and re-layouts: 5.72 us -> 4.58 us
    ppermute x4, waiting for transfers between devices: 17.1 us -> 18.2 us  [gather_rows(): x = own + lax.ppermute(send, 'dev', pairs)]
    unnamed x4 -> x5, local copies, waits for them, and re-layouts: 2.96 us -> 1.82 us
  transfers between devices with their start and end apart: 5 -> 5, of which waited for: 5 -> 5; matrix products, arithmetic and copies ran while one was open for 4% -> 2% of each run, Pallas kernels for 0% -> 0%
where the time goes in v17:
time: 49.4 us; the launch traced here: 49.2 us
  waiting for transfers between devices  24.1 us (49%)
  Pallas kernels  13.6 us (28%)
  local copies, waits for them, and re-layouts  4.58 us (9%)
  starting transfers between devices  4.46 us (9%)
  other arithmetic  2.34 us (5%)
    ppermute x4, waiting for transfers between devices, gather_rows(): x = own + lax.ppermute(send, 'dev', pairs)  18.2 us
    pallas_call x1, Pallas kernels, decode(): pl.pallas_call(functools.partial(decode_kernel, columns), out_shape=jax.S...  13.6 us
    ppermute x1, waiting for transfers between devices, local(): lax.ppermute(pixels, 'dev', [(i, reverse_bits(i, bits)) for i in range(n)])  5.82 us
    ppermute x4, starting transfers between devices, gather_rows(): x = own + lax.ppermute(send, 'dev', pairs)  2.54 us
    ppermute x1, starting transfers between devices, local(): lax.ppermute(pixels, 'dev', [(i, reverse_bits(i, bits)) for i in range(n)])  1.92 us
    unnamed x5, local copies, waits for them, and re-layouts  1.82 us
    select_n x1, other arithmetic, local(): jnp.where(keep[:, None, None, None], latents[0], jnp.zeros_like(latents[0]))  1.07 us
  transfers between devices with their start and end apart: 5, of which 5 were waited for; matrix products, arithmetic and copies ran while one was open for 2% of the time, Pallas kernels for 0%

profile of v17, /device:TPU:24, one launch (start us, length us, event | category | flops | bytes accessed | tf_op | source)
XLA Modules:
  0.0 49.2 jit_solution(8366970525177270824)
XLA Ops:
  0.0 0.7 %broadcast_compare_fusion = pred[2]{0:T(512)(128)(4,1)S(1)} fusion(s32[2]{0:T(128)} %param.6, s32[]{:T(128)S(6)} %axis_index.12), kind=kLoop, calls=%fused_computation.15 | loop fusion | flops 2 | bytes 14 | tf_op jit(solution)/shard_map/eq | solution.py:130
  0.7 1.1 %bitcast_select_fusion = bf16[2,3,16,1664]{3,2,1,0:T(8,128)(2,1)S(1)} fusion(bf16[1,2,3,16,1664]{4,3,2,1,0:T(8,128)(2,1)} %param.5, pred[2]{0:T(512)(128)(4,1)S(1)} %broadcast_compare_fusion), kind=kLoop, calls=%fused_computation.4 | loop fusion | flops 159744 | bytes 638978 | tf_op jit(solution)/shard_map/jit(_where)/select_n | solution.py:131
  1.8 0.1 pad_dynamic-slice_fusion
  2.0 1.6 %collective-permute-done = bf16[2,3,12,1664]{3,2,1,0:T(8,128)(2,1)S(1)} collective-permute-done((bf16[2,3,12,1664]{3,2,1,0:T(8,128)(2,1)S(1)}, bf16[2,3,12,1664]{3,2,1,0:T(8,128)(2,1)S(1)}, u32[]{:S(2)}, u32[]{:S(2)}) %collective-permute-start) | collective-permute-done | bytes 239648 | tf_op jit(solution)/shard_map/ppermute | solution.py:33
  3.6 0.2 fusion
  3.9 1.6 %collective-permute-start.1 = (bf16[2,3,8,1664]{3,2,1,0:T(8,128)(2,1)S(1)}, bf16[2,3,8,1664]{3,2,1,0:T(8,128)(2,1)S(1)}, u32[]{:S(2)}, u32[]{:S(2)}) collective-permute-start(bf16[2,3,8,1664]{3,2,1,0:T(8,128)(2,1)S(1)} %constant_dynamic-slice_fusion.2), channel_id=1, source_target_pairs={{0,2},{1,3},{2,0},{3,1},{4,6},{5,7},{6,4},{7,5},{8,10},{9,11},{10,... | collective-permute-start | bytes 479240 | tf_op jit(solution)/shard_map/ppermute | solution.py:33
  5.4 4.7 %collective-permute-done.1 = bf16[2,3,8,1664]{3,2,1,0:T(8,128)(2,1)S(1)} collective-permute-done((bf16[2,3,8,1664]{3,2,1,0:T(8,128)(2,1)S(1)}, bf16[2,3,8,1664]{3,2,1,0:T(8,128)(2,1)S(1)}, u32[]{:S(2)}, u32[]{:S(2)}) %collective-permute-start.1) | collective-permute-done | bytes 159776 | tf_op jit(solution)/shard_map/ppermute | solution.py:33
  10.1 0.1 dynamic-slice_add_fusion.2
  10.2 0.5 %collective-permute-start.2 = (bf16[2,3,6,1664]{3,2,1,0:T(8,128)(2,1)S(1)}, bf16[2,3,6,1664]{3,2,1,0:T(8,128)(2,1)S(1)}, u32[]{:S(2)}, u32[]{:S(2)}) collective-permute-start(bf16[2,3,6,1664]{3,2,1,0:T(8,128)(2,1)S(1)} %constant_dynamic-slice_fusion.1), channel_id=1, source_target_pairs={{0,4},{1,5},{2,6},{3,7},{4,0},{5,1},{6,2},{7,3},{8,12},{9,13},{10,... | collective-permute-start | bytes 359432 | tf_op jit(solution)/shard_map/ppermute | solution.py:33
  10.7 0.8 %copy.14 = bf16[384,12]{1,0:T(8,128)(2,1)S(1)} copy(bf16[384,12]{0,1:T(8,128)(2,1)} %param.9) | data formatting | bytes 18432 | tf_op args[4]
  11.6 4.0 %collective-permute-done.2 = bf16[2,3,6,1664]{3,2,1,0:T(8,128)(2,1)S(1)} collective-permute-done((bf16[2,3,6,1664]{3,2,1,0:T(8,128)(2,1)S(1)}, bf16[2,3,6,1664]{3,2,1,0:T(8,128)(2,1)S(1)}, u32[]{:S(2)}, u32[]{:S(2)}) %collective-permute-start.2) | collective-permute-done | bytes 119840 | tf_op jit(solution)/shard_map/ppermute | solution.py:33
  15.7 0.4 collective-permute-start.3
  16.1 8.0 %collective-permute-done.3 = bf16[2,3,5,1664]{3,2,1,0:T(8,128)(2,1)S(1)} collective-permute-done((bf16[2,3,5,1664]{3,2,1,0:T(8,128)(2,1)S(1)}, bf16[2,3,5,1664]{3,2,1,0:T(8,128)(2,1)S(1)}, u32[]{:S(2)}, u32[]{:S(2)}) %collective-permute-start.3) | collective-permute-done | bytes 99872 | tf_op jit(solution)/shard_map/ppermute | solution.py:33
  24.2 0.6 %reshape.17 = bf16[6,5,104,16]{3,2,0,1:T(8,128)(2,1)S(1)} reshape(bf16[2,3,5,1664]{3,1,0,2:T(4,128)(2,1)S(1)} %copy.10) | data formatting | bytes 199680 | tf_op jit(solution)/shard_map/reshape | solution.py:136
  24.9 0.4 copy.17
  25.4 0.1 fusion.2
  25.7 0.1 maximum_bitcast_fusion
  25.9 13.6 %shard_map.55 = bf16[1,768,128]{2,1,0:T(8,128)(2,1)S(1)} custom-call(f32[3]{0:T(128)S(1)} %and_convert_fusion.row_ok_ref, bf16[5,3,16,1024]{3,2,1,0:T(8,128)(2,1)S(1)} %pad_maximum_fusion.xt_ref, bf16[432,384]{1,0:T(8,128)(2,1)S(1)} %copy-done, bf16[9,1152,384]{2,1,0:T(8,128)(2,1)} %bitcast.24, bf16[384,128]{1,0:T(8,128)(2,1)S(1)} %pad.14.w_pix_ref), custom_call_target="tpu_custom_call" | custom-call | tf_op jit(solution)/shard_map/pallas_call | solution.py:96
  39.5 0.1 copy.15
  39.6 0.5 %copy.16 = bf16[2,3,1,2,104,2,3]{6,5,4,3,1,0,2:T(2,128)(2,1)S(1)} copy(bf16[2,3,1,2,104,2,3]{4,1,0,6,5,3,2:T(4,128)(2,1)S(1)} %slice_bitcast_fusion) | data formatting | bytes 29952 | tf_op jit(solution)/shard_map/transpose | solution.py:145
  40.2 0.7 %reshape.21 = bf16[2,3,2,624]{3,2,1,0:T(2,128)(2,1)S(1)} reshape(bf16[2,3,1,2,104,2,3]{6,5,4,3,1,0,2:T(2,128)(2,1)S(1)} %copy.16) | data formatting | bytes 29952 | tf_op jit(solution)/shard_map/reshape | solution.py:146
  40.9 1.9 %collective-permute-start.4 = (bf16[2,3,2,624]{3,2,1,0:T(2,128)(2,1)S(1)}, bf16[2,3,2,624]{3,2,1,0:T(2,128)(2,1)S(1)}, u32[]{:S(2)}, u32[]{:S(2)}) collective-permute-start(bf16[2,3,2,624]{3,2,1,0:T(2,128)(2,1)S(1)} %reshape.21), channel_id=1, source_target_pairs={{0,0},{1,8},{2,4},{3,12},{4,2},{5,10},{6,6},{7,14},{8,1},{9,9},{10... | collective-permute-start | bytes 44936 | tf_op jit(solution)/shard_map/ppermute | solution.py:147
  42.8 5.8 %collective-permute-done.4 = bf16[2,3,2,624]{3,2,1,0:T(2,128)(2,1)S(1)} collective-permute-done((bf16[2,3,2,624]{3,2,1,0:T(2,128)(2,1)S(1)}, bf16[2,3,2,624]{3,2,1,0:T(2,128)(2,1)S(1)}, u32[]{:S(2)}, u32[]{:S(2)}) %collective-permute-start.4) | collective-permute-done | bytes 15008 | tf_op jit(solution)/shard_map/ppermute | solution.py:147
  48.6 0.6 %copy.19 = bf16[2,3,2,624]{3,2,1,0:T(2,128)(2,1)} copy(bf16[2,3,2,624]{3,2,1,0:T(2,128)(2,1)S(1)} %collective-permute-done.4) | data formatting | bytes 29952
  (18 shorter events, 0.8 us)
Async XLA Ops:
  0.0 25.9 %copy-start = (bf16[432,384]{1,0:T(8,128)(2,1)S(1)}, bf16[432,384]{1,0:T(8,128)(2,1)}, u32[]{:S(2)}) copy-start(bf16[432,384]{1,0:T(8,128)(2,1)} %w_in_ref.1) | copy-start | bytes 995332
  1.9 1.7 %collective-permute-start = (bf16[2,3,12,1664]{3,2,1,0:T(8,128)(2,1)S(1)}, bf16[2,3,12,1664]{3,2,1,0:T(8,128)(2,1)S(1)}, u32[]{:S(2)}, u32[]{:S(2)}) collective-permute-start(bf16[2,3,12,1664]{3,2,1,0:T(8,128)(2,1)S(1)} %pad_dynamic-slice_fusion), channel_id=1, source_target_pairs={{0,1},{1,0},{2,3},{3,2},{4,5},{5,4},{6,7},{7,6},{8,9},{9,8},{10,11... | collective-permute-start | bytes 718856 | tf_op jit(solution)/shard_map/ppermute | solution.py:33
  3.9 6.2 %collective-permute-start.1 = (bf16[2,3,8,1664]{3,2,1,0:T(8,128)(2,1)S(1)}, bf16[2,3,8,1664]{3,2,1,0:T(8,128)(2,1)S(1)}, u32[]{:S(2)}, u32[]{:S(2)}) collective-permute-start(bf16[2,3,8,1664]{3,2,1,0:T(8,128)(2,1)S(1)} %constant_dynamic-slice_fusion.2), channel_id=1, source_target_pairs={{0,2},{1,3},{2,0},{3,1},{4,6},{5,7},{6,4},{7,5},{8,10},{9,11},{10,... | collective-permute-start | bytes 479240 | tf_op jit(solution)/shard_map/ppermute | solution.py:33
  10.2 5.4 %collective-permute-start.2 = (bf16[2,3,6,1664]{3,2,1,0:T(8,128)(2,1)S(1)}, bf16[2,3,6,1664]{3,2,1,0:T(8,128)(2,1)S(1)}, u32[]{:S(2)}, u32[]{:S(2)}) collective-permute-start(bf16[2,3,6,1664]{3,2,1,0:T(8,128)(2,1)S(1)} %constant_dynamic-slice_fusion.1), channel_id=1, source_target_pairs={{0,4},{1,5},{2,6},{3,7},{4,0},{5,1},{6,2},{7,3},{8,12},{9,13},{10,... | collective-permute-start | bytes 359432 | tf_op jit(solution)/shard_map/ppermute | solution.py:33
  15.7 8.4 %collective-permute-start.3 = (bf16[2,3,5,1664]{3,2,1,0:T(8,128)(2,1)S(1)}, bf16[2,3,5,1664]{3,2,1,0:T(8,128)(2,1)S(1)}, u32[]{:S(2)}, u32[]{:S(2)}) collective-permute-start(bf16[2,3,5,1664]{3,2,1,0:T(8,128)(2,1)S(1)} %constant_dynamic-slice_fusion), channel_id=1, source_target_pairs={{0,8},{1,9},{2,10},{3,11},{4,12},{5,13},{6,14},{7,15},{8,0},{9,1},... | collective-permute-start | bytes 299528 | tf_op jit(solution)/shard_map/ppermute | solution.py:33
  40.9 7.7 %collective-permute-start.4 = (bf16[2,3,2,624]{3,2,1,0:T(2,128)(2,1)S(1)}, bf16[2,3,2,624]{3,2,1,0:T(2,128)(2,1)S(1)}, u32[]{:S(2)}, u32[]{:S(2)}) collective-permute-start(bf16[2,3,2,624]{3,2,1,0:T(2,128)(2,1)S(1)} %reshape.21), channel_id=1, source_target_pairs={{0,0},{1,8},{2,4},{3,12},{4,2},{5,10},{6,6},{7,14},{8,1},{9,9},{10... | collective-permute-start | bytes 44936 | tf_op jit(solution)/shard_map/ppermute | solution.py:147

commit v18 on v14

--- a/solution.py
+++ b/solution.py
@@ -44,10 +44,7 @@
     span = act_ref.shape[1] - lead
     channels = w_vmem.shape[2]
     taps = w_vmem.shape[0] // 3
-    copies = [
-        pltpu.make_async_copy(w_hbm.at[pl.ds(a * taps, taps)], w_vmem.at[pl.ds(a * taps, taps)], sem.at[a])
-        for a in range(3)
-    ]
+    copies = [pltpu.make_async_copy(w_hbm.at[t], w_vmem.at[t], sem.at[t]) for t in range(w_vmem.shape[0])]
     for copy in copies:
         copy.start()
     zeros = jnp.zeros((lead, 3 * channels), act_ref.dtype)
@@ -75,9 +72,9 @@
     for jo in range(rows_out):
         acc = center_ref[jo]
         for a in range(3):
-            if jo == 0:
-                copies[a].wait()
             for b in range(3):
+                if jo == 0:
+                    copies[a * taps + b].wait()
                 piece = act_ref[jo + b, a * LANE : a * LANE + span, :]
                 acc = acc + jnp.dot(piece, w_vmem[a * taps + b], preferred_element_type=jnp.float32)
         scale = lax.rsqrt(jnp.mean(acc * acc, axis=-1, keepdims=True) + epsilon)
@@ -109,7 +106,7 @@
             pltpu.VMEM((9, 3 * channels, channels), jnp.bfloat16),
             pltpu.VMEM((rows_in, span + 2 * LANE, 3 * channels), jnp.bfloat16),
             pltpu.VMEM((rows_in - 2, span, channels), jnp.float32),
-            pltpu.SemaphoreType.DMA((3,)),
+            pltpu.SemaphoreType.DMA((9,)),
         ],
         compiler_params=pltpu.CompilerParams(vmem_limit_bytes=48 * 1024 * 1024),
     )(row_ok, xt, w_in_t, w_mid, w_pix)

time: 49.2 us -> 50.4 us (1.024)
  Pallas kernels: 13.4 us -> 14.6 us
    pallas_call x1, Pallas kernels: 13.4 us -> 14.6 us  [decode(): pl.pallas_call(functools.partial(decode_kernel, columns), out_shape=jax.S...]
where the time goes in v18:
time: 50.4 us; the launch traced here: 50.2 us
  waiting for transfers between devices  22.9 us (45%)
  Pallas kernels  14.6 us (29%)
  local copies, waits for them, and re-layouts  5.72 us (11%)
  starting transfers between devices  4.46 us (9%)
  other arithmetic  2.29 us (5%)
    ppermute x4, waiting for transfers between devices, gather_rows(): x = own + lax.ppermute(send, 'dev', pairs)  17.1 us
    pallas_call x1, Pallas kernels, decode(): pl.pallas_call(functools.partial(decode_kernel, columns), out_shape=jax.S...  14.6 us
    ppermute x1, waiting for transfers between devices, local(): lax.ppermute(pixels, 'dev', [(i, reverse_bits(i, bits)) for i in range(n)])  5.82 us
    unnamed x4, local copies, waits for them, and re-layouts  2.96 us
    ppermute x4, starting transfers between devices, gather_rows(): x = own + lax.ppermute(send, 'dev', pairs)  2.54 us
    ppermute x1, starting transfers between devices, local(): lax.ppermute(pixels, 'dev', [(i, reverse_bits(i, bits)) for i in range(n)])  1.92 us
    select_n x1, other arithmetic, local(): jnp.where(keep[:, None, None, None], latents[0], jnp.zeros_like(latents[0]))  1.07 us
  transfers between devices with their start and end apart: 5, of which 5 were waited for; matrix products, arithmetic and copies ran while one was open for 4% of the time, Pallas kernels for 0%

profile of v18, /device:TPU:24, one launch (start us, length us, event | category | flops | bytes accessed | tf_op | source)
XLA Modules:
  0.0 50.2 jit_solution(14978214519127315482)
XLA Ops:
  0.0 0.7 %broadcast_compare_fusion = pred[2]{0:T(512)(128)(4,1)S(1)} fusion(s32[2]{0:T(128)} %param.6, s32[]{:T(128)S(6)} %axis_index.12), kind=kLoop, calls=%fused_computation.15 | loop fusion | flops 2 | bytes 14 | tf_op jit(solution)/shard_map/eq | solution.py:128
  0.7 1.1 %bitcast_select_fusion = bf16[2,3,16,1664]{3,2,1,0:T(8,128)(2,1)S(1)} fusion(bf16[1,2,3,16,1664]{4,3,2,1,0:T(8,128)(2,1)} %param.5, pred[2]{0:T(512)(128)(4,1)S(1)} %broadcast_compare_fusion), kind=kLoop, calls=%fused_computation.4 | loop fusion | flops 159744 | bytes 638978 | tf_op jit(solution)/shard_map/jit(_where)/select_n | solution.py:129
  1.7 0.1 pad_dynamic-slice_fusion
  2.0 1.6 %collective-permute-done = bf16[2,3,12,1664]{3,2,1,0:T(8,128)(2,1)S(1)} collective-permute-done((bf16[2,3,12,1664]{3,2,1,0:T(8,128)(2,1)S(1)}, bf16[2,3,12,1664]{3,2,1,0:T(8,128)(2,1)S(1)}, u32[]{:S(2)}, u32[]{:S(2)}) %collective-permute-start) | collective-permute-done | bytes 239648 | tf_op jit(solution)/shard_map/ppermute | solution.py:33
  3.6 0.2 fusion
  3.8 1.6 %collective-permute-start.1 = (bf16[2,3,8,1664]{3,2,1,0:T(8,128)(2,1)S(1)}, bf16[2,3,8,1664]{3,2,1,0:T(8,128)(2,1)S(1)}, u32[]{:S(2)}, u32[]{:S(2)}) collective-permute-start(bf16[2,3,8,1664]{3,2,1,0:T(8,128)(2,1)S(1)} %constant_dynamic-slice_fusion.2), channel_id=1, source_target_pairs={{0,2},{1,3},{2,0},{3,1},{4,6},{5,7},{6,4},{7,5},{8,10},{9,11},{10,... | collective-permute-start | bytes 479240 | tf_op jit(solution)/shard_map/ppermute | solution.py:33
  5.4 4.7 %collective-permute-done.1 = bf16[2,3,8,1664]{3,2,1,0:T(8,128)(2,1)S(1)} collective-permute-done((bf16[2,3,8,1664]{3,2,1,0:T(8,128)(2,1)S(1)}, bf16[2,3,8,1664]{3,2,1,0:T(8,128)(2,1)S(1)}, u32[]{:S(2)}, u32[]{:S(2)}) %collective-permute-start.1) | collective-permute-done | bytes 159776 | tf_op jit(solution)/shard_map/ppermute | solution.py:33
  10.2 0.5 %collective-permute-start.2 = (bf16[2,3,6,1664]{3,2,1,0:T(8,128)(2,1)S(1)}, bf16[2,3,6,1664]{3,2,1,0:T(8,128)(2,1)S(1)}, u32[]{:S(2)}, u32[]{:S(2)}) collective-permute-start(bf16[2,3,6,1664]{3,2,1,0:T(8,128)(2,1)S(1)} %constant_dynamic-slice_fusion.1), channel_id=1, source_target_pairs={{0,4},{1,5},{2,6},{3,7},{4,0},{5,1},{6,2},{7,3},{8,12},{9,13},{10,... | collective-permute-start | bytes 359432 | tf_op jit(solution)/shard_map/ppermute | solution.py:33
  10.7 1.1 %copy.15 = bf16[432,384]{0,1:T(8,128)(2,1)S(1)} copy(bf16[432,384]{1,0:T(8,128)(2,1)} %param.7) | data formatting | bytes 663552 | tf_op args[2]
  11.8 0.8 %copy.16 = bf16[384,12]{1,0:T(8,128)(2,1)S(1)} copy(bf16[384,12]{0,1:T(8,128)(2,1)} %param.9) | data formatting | bytes 18432 | tf_op args[4]
  12.7 2.8 %collective-permute-done.2 = bf16[2,3,6,1664]{3,2,1,0:T(8,128)(2,1)S(1)} collective-permute-done((bf16[2,3,6,1664]{3,2,1,0:T(8,128)(2,1)S(1)}, bf16[2,3,6,1664]{3,2,1,0:T(8,128)(2,1)S(1)}, u32[]{:S(2)}, u32[]{:S(2)}) %collective-permute-start.2) | collective-permute-done | bytes 119840 | tf_op jit(solution)/shard_map/ppermute | solution.py:33
  15.7 0.4 collective-permute-start.3
  16.1 8.0 %collective-permute-done.3 = bf16[2,3,5,1664]{3,2,1,0:T(8,128)(2,1)S(1)} collective-permute-done((bf16[2,3,5,1664]{3,2,1,0:T(8,128)(2,1)S(1)}, bf16[2,3,5,1664]{3,2,1,0:T(8,128)(2,1)S(1)}, u32[]{:S(2)}, u32[]{:S(2)}) %collective-permute-start.3) | collective-permute-done | bytes 99872 | tf_op jit(solution)/shard_map/ppermute | solution.py:33
  24.2 0.6 %reshape.17 = bf16[6,5,104,16]{3,2,0,1:T(8,128)(2,1)S(1)} reshape(bf16[2,3,5,1664]{3,1,0,2:T(4,128)(2,1)S(1)} %copy.11) | data formatting | bytes 199680 | tf_op jit(solution)/shard_map/reshape | solution.py:134
  24.8 0.4 copy.19
  25.3 0.1 fusion.2
  25.6 0.1 maximum_bitcast_fusion
  25.8 14.6 %shard_map.55 = bf16[1,768,128]{2,1,0:T(8,128)(2,1)S(1)} custom-call(f32[3]{0:T(128)S(1)} %and_convert_fusion.row_ok_ref, bf16[5,3,16,1024]{3,2,1,0:T(8,128)(2,1)S(1)} %pad_maximum_fusion.xt_ref, bf16[384,432]{1,0:T(8,128)(2,1)S(1)} %bitcast.24, bf16[9,1152,384]{2,1,0:T(8,128)(2,1)} %bitcast.26, bf16[384,128]{1,0:T(8,128)(2,1)S(1)} %pad.14.w_pix_ref), custom_call_target="tpu_custom_call" | custom-call | tf_op jit(solution)/shard_map/pallas_call | solution.py:94
  40.4 0.1 copy.17
  40.6 0.5 %copy.18 = bf16[2,3,1,2,104,2,3]{6,5,4,3,1,0,2:T(2,128)(2,1)S(1)} copy(bf16[2,3,1,2,104,2,3]{4,1,0,6,5,3,2:T(4,128)(2,1)S(1)} %slice_bitcast_fusion) | data formatting | bytes 29952 | tf_op jit(solution)/shard_map/transpose | solution.py:143
  41.2 0.7 %reshape.21 = bf16[2,3,2,624]{3,2,1,0:T(2,128)(2,1)S(1)} reshape(bf16[2,3,1,2,104,2,3]{6,5,4,3,1,0,2:T(2,128)(2,1)S(1)} %copy.18) | data formatting | bytes 29952 | tf_op jit(solution)/shard_map/reshape | solution.py:144
  41.8 1.9 %collective-permute-start.4 = (bf16[2,3,2,624]{3,2,1,0:T(2,128)(2,1)S(1)}, bf16[2,3,2,624]{3,2,1,0:T(2,128)(2,1)S(1)}, u32[]{:S(2)}, u32[]{:S(2)}) collective-permute-start(bf16[2,3,2,624]{3,2,1,0:T(2,128)(2,1)S(1)} %reshape.21), channel_id=1, source_target_pairs={{0,0},{1,8},{2,4},{3,12},{4,2},{5,10},{6,6},{7,14},{8,1},{9,9},{10... | collective-permute-start | bytes 44936 | tf_op jit(solution)/shard_map/ppermute | solution.py:145
  43.8 5.8 %collective-permute-done.4 = bf16[2,3,2,624]{3,2,1,0:T(2,128)(2,1)S(1)} collective-permute-done((bf16[2,3,2,624]{3,2,1,0:T(2,128)(2,1)S(1)}, bf16[2,3,2,624]{3,2,1,0:T(2,128)(2,1)S(1)}, u32[]{:S(2)}, u32[]{:S(2)}) %collective-permute-start.4) | collective-permute-done | bytes 15008 | tf_op jit(solution)/shard_map/ppermute | solution.py:145
  49.6 0.6 %copy.21 = bf16[2,3,2,624]{3,2,1,0:T(2,128)(2,1)} copy(bf16[2,3,2,624]{3,2,1,0:T(2,128)(2,1)S(1)} %collective-permute-done.4) | data formatting | bytes 29952
  (17 shorter events, 0.9 us)
Async XLA Ops:
  1.9 1.7 %collective-permute-start = (bf16[2,3,12,1664]{3,2,1,0:T(8,128)(2,1)S(1)}, bf16[2,3,12,1664]{3,2,1,0:T(8,128)(2,1)S(1)}, u32[]{:S(2)}, u32[]{:S(2)}) collective-permute-start(bf16[2,3,12,1664]{3,2,1,0:T(8,128)(2,1)S(1)} %pad_dynamic-slice_fusion), channel_id=1, source_target_pairs={{0,1},{1,0},{2,3},{3,2},{4,5},{5,4},{6,7},{7,6},{8,9},{9,8},{10,11... | collective-permute-start | bytes 718856 | tf_op jit(solution)/shard_map/ppermute | solution.py:33
  3.8 6.2 %collective-permute-start.1 = (bf16[2,3,8,1664]{3,2,1,0:T(8,128)(2,1)S(1)}, bf16[2,3,8,1664]{3,2,1,0:T(8,128)(2,1)S(1)}, u32[]{:S(2)}, u32[]{:S(2)}) collective-permute-start(bf16[2,3,8,1664]{3,2,1,0:T(8,128)(2,1)S(1)} %constant_dynamic-slice_fusion.2), channel_id=1, source_target_pairs={{0,2},{1,3},{2,0},{3,1},{4,6},{5,7},{6,4},{7,5},{8,10},{9,11},{10,... | collective-permute-start | bytes 479240 | tf_op jit(solution)/shard_map/ppermute | solution.py:33
  10.2 5.4 %collective-permute-start.2 = (bf16[2,3,6,1664]{3,2,1,0:T(8,128)(2,1)S(1)}, bf16[2,3,6,1664]{3,2,1,0:T(8,128)(2,1)S(1)}, u32[]{:S(2)}, u32[]{:S(2)}) collective-permute-start(bf16[2,3,6,1664]{3,2,1,0:T(8,128)(2,1)S(1)} %constant_dynamic-slice_fusion.1), channel_id=1, source_target_pairs={{0,4},{1,5},{2,6},{3,7},{4,0},{5,1},{6,2},{7,3},{8,12},{9,13},{10,... | collective-permute-start | bytes 359432 | tf_op jit(solution)/shard_map/ppermute | solution.py:33
  15.7 8.4 %collective-permute-start.3 = (bf16[2,3,5,1664]{3,2,1,0:T(8,128)(2,1)S(1)}, bf16[2,3,5,1664]{3,2,1,0:T(8,128)(2,1)S(1)}, u32[]{:S(2)}, u32[]{:S(2)}) collective-permute-start(bf16[2,3,5,1664]{3,2,1,0:T(8,128)(2,1)S(1)} %constant_dynamic-slice_fusion), channel_id=1, source_target_pairs={{0,8},{1,9},{2,10},{3,11},{4,12},{5,13},{6,14},{7,15},{8,0},{9,1},... | collective-permute-start | bytes 299528 | tf_op jit(solution)/shard_map/ppermute | solution.py:33
  41.8 7.7 %collective-permute-start.4 = (bf16[2,3,2,624]{3,2,1,0:T(2,128)(2,1)S(1)}, bf16[2,3,2,624]{3,2,1,0:T(2,128)(2,1)S(1)}, u32[]{:S(2)}, u32[]{:S(2)}) collective-permute-start(bf16[2,3,2,624]{3,2,1,0:T(2,128)(2,1)S(1)} %reshape.21), channel_id=1, source_target_pairs={{0,0},{1,8},{2,4},{3,12},{4,2},{5,10},{6,6},{7,14},{8,1},{9,9},{10... | collective-permute-start | bytes 44936 | tf_op jit(solution)/shard_map/ppermute | solution.py:145
